TPU v7x, 1024 devices: a whole 8x8x8 slice. The times are simulated.
1024 devices in a mesh: dp: 32 (over z_hi, y), mp: 16 (over x, core), seq: 2 (over z_lo).
Axes of the slice: x: 8, y: 8, z: 8 (z_hi: 4, z_lo: 2; z = z_hi * 2 + z_lo), core: 2. Of those that a mesh axis runs over, the one named last changes fastest.
Arguments:
- queries: bfloat16 [64, 256, 6144], P(('dp', 'seq'), None, 'mp'), may hold values from -20 to 20
- key_rows: bfloat16 [64, 256, 6144], P(('dp', 'seq'), None, 'mp'), may hold values from -12 to 12
- value_rows: bfloat16 [64, 256, 6144], P(('dp', 'seq'), None, 'mp'), may hold values from -6 to 6
- projection: bfloat16 [6144, 4096], P('mp', ('dp', 'seq')), may hold values from -0.21875 to 0.21875
- upstream: bfloat16 [256, 64, 4096], P('mp', ('dp', 'seq')), may hold values from -6 to 6
Outputs:
- projected: bfloat16 [256, 64, 4096], P('mp', ('dp', 'seq'))
- grad_queries: float32 [64, 256, 6144], P(('dp', 'seq'), None, 'mp')
- grad_keys: float32 [64, 256, 6144], P(('dp', 'seq'), None, 'mp')
- grad_values: float32 [64, 256, 6144], P(('dp', 'seq'), None, 'mp')
All inputs are finite; a program needn't handle non-finite values.
Results may differ from a plain program's by a relative error of at most 0.023.
Values may be sent and summed in bfloat16 or wider, within the bound.
No kernel may reach another device: no remote copies, remote signals or barrier semaphores. Data moves between devices by JAX's collectives and lax.ppermute only.
A program may use at most 32 MiB of HBM per device.

v0:
```python
import math

import jax
import jax.numpy as jnp
from jax import lax
from jax.sharding import PartitionSpec as P

HEADS = 48


def split_heads(block, head_count):
    frame_count, row_count, feature_count = block.shape
    return block.reshape(frame_count, row_count, head_count, feature_count // head_count)


def soft_weights(queries, key_rows, head_count):
    split_q = split_heads(queries, head_count)
    factor = 1.0 / math.sqrt(split_q.shape[3])
    scores = (
        jnp.einsum(
            "fqhd,fkhd->fhqk",
            split_q,
            split_heads(key_rows, head_count),
            preferred_element_type=jnp.float32,
        )
        * factor
    )
    return jax.nn.softmax(scores, axis=-1)


def attend_values(soft, value_rows, head_count):
    mixed = jnp.einsum(
        "fhqk,fkhd->fqhd",
        soft.astype(jnp.bfloat16),
        split_heads(value_rows, head_count),
        preferred_element_type=jnp.float32,
    )
    frame_count, row_count = (mixed.shape[0], mixed.shape[1])
    return mixed.astype(jnp.bfloat16).reshape(frame_count, row_count, -1)


def backward_heads(soft, queries, key_rows, value_rows, grad_attended, head_count):
    split_q = split_heads(queries, head_count)
    split_k = split_heads(key_rows, head_count)
    split_v = split_heads(value_rows, head_count)
    split_g = split_heads(grad_attended, head_count)
    factor = 1.0 / math.sqrt(split_q.shape[3])
    grad_soft = jnp.einsum("fqhd,fkhd->fhqk", split_g, split_v, preferred_element_type=jnp.float32)
    inner_sum = jnp.sum(grad_soft * soft, axis=-1, keepdims=True)
    grad_scores = (soft * (grad_soft - inner_sum)).astype(jnp.bfloat16)
    grad_q = (
        jnp.einsum("fhqk,fkhd->fqhd", grad_scores, split_k, preferred_element_type=jnp.float32)
        * factor
    )
    grad_k = (
        jnp.einsum("fhqk,fqhd->fkhd", grad_scores, split_q, preferred_element_type=jnp.float32)
        * factor
    )
    grad_v = jnp.einsum(
        "fhqk,fqhd->fkhd", soft.astype(jnp.bfloat16), split_g, preferred_element_type=jnp.float32
    )
    return (
        grad_q.reshape(queries.shape),
        grad_k.reshape(key_rows.shape),
        grad_v.reshape(value_rows.shape),
    )


def on_device(queries, key_rows, value_rows, projection, upstream):
    head_count = HEADS // lax.axis_size("mp")
    soft = soft_weights(queries, key_rows, head_count)
    attended = attend_values(soft, value_rows, head_count)
    ordered = attended.transpose(1, 0, 2)
    grad_full = lax.all_gather(upstream, "mp", axis=0, tiled=True)
    columns = lax.all_gather(projection, ("dp", "seq"), axis=1, tiled=True)
    grad_attended = jnp.einsum(
        "qfd,cd->fqc", grad_full, columns, preferred_element_type=jnp.float32
    )
    projected = lax.psum_scatter(
        jnp.einsum("qfc,cd->qfd", ordered, columns, preferred_element_type=jnp.float32).astype(
            jnp.bfloat16
        ),
        "mp",
        scatter_dimension=0,
        tiled=True,
    )
    grad_rounded = grad_attended.astype(jnp.bfloat16)
    grad_q, grad_k, grad_v = backward_heads(
        soft, queries, key_rows, value_rows, grad_rounded, head_count
    )
    return (projected, grad_q, grad_k, grad_v)


def solution(mesh):
    return jax.shard_map(
        on_device,
        mesh=mesh,
        in_specs=(
            P(("dp", "seq"), None, "mp"),
            P(("dp", "seq"), None, "mp"),
            P(("dp", "seq"), None, "mp"),
            P("mp", ("dp", "seq")),
            P("mp", ("dp", "seq"), None),
        ),
        out_specs=(
            P("mp", ("dp", "seq"), None),
            P(("dp", "seq"), None, "mp"),
            P(("dp", "seq"), None, "mp"),
            P(("dp", "seq"), None, "mp"),
        ),
        check_vma=False,
    )
```

profile of v0, /device:TPU:1, one launch (start us, length us, event | category | flops | bytes accessed | tf_op | source)
XLA Modules:
  0.0 423.1 jit_solution(11488672296838426748)
XLA Ops:
  7.2 0.0 all-gather.3.cloned.1.call-start
  7.2 0.7 all-gather.3.cloned.1.call-update
  7.9 0.0 all-gather.5.cloned.1.call-start
  7.9 0.7 all-gather.5.cloned.1.call-update
  8.6 0.0 reduce-scatter.2.cloned.1.call-start
  8.7 1.1 copy.23
  9.8 1.1 copy.24
  10.8 1.1 copy.27
  11.9 0.0 copy-start.2
  11.9 1.3 fusion.14
  13.2 1.3 convolution_convert_fusion.1
  14.5 248.9 %all-gather.3.cloned.1.call-done = bf16[384,4096]{0,1:T(8,128)(2,1)} async-done(((bf16[384,64]{0,1:T(8,128)(2,1)}), bf16[384,4096]{0,1:T(8,128)(2,1)}) %all-gather.3.cloned.1.call-update) | async-done | bytes 3145744 | tf_op jit(solution)/shard_map/all_gather | solution.py:75
  263.4 0.0 copy-done.2
  263.4 0.0 copy-start
  263.4 4.8 %fusion.1 = bf16[256,1,4096]{2,0,1:T(8,128)(2,1)} fusion(bf16[256,384]{0,1:T(8,128)(2,1)} %bitcast.71, bf16[384,4096]{0,1:T(8,128)(2,1)} %all-gather.3.cloned.1.call-done), kind=kOutput, calls=%fused_computation.2 | convolution fusion | flops 806354944 | bytes 5439488 | tf_op jit(solution)/shard_map/qfc,cd->qfd/dot_general | solution.py:80
  268.2 0.0 reduce-scatter.2.cloned.1.call-update
  268.2 81.2 %all-gather.5.cloned.1.call-done = bf16[256,1,4096]{2,0,1:T(8,128)(2,1)} async-done(((bf16[16,1,4096]{2,0,1:T(8,128)(2,1)}), bf16[256,1,4096]{2,0,1:T(8,128)(2,1)}) %all-gather.5.cloned.1.call-update) | async-done | bytes 2097168 | tf_op jit(solution)/shard_map/all_gather | solution.py:74
  349.4 0.0 copy-done
  349.4 0.0 copy-start.1
  349.4 0.0 copy-start.3
  349.4 2.8 fusion.6
  352.2 0.0 copy-start.4
  352.2 0.0 copy-done.1
  352.2 0.0 copy-done.3
  352.2 0.3 multiply_reduce_fusion
  352.5 0.2 multiply_convert_fusion
  352.7 0.2 copy-done.4
  352.9 0.3 convolution_multiply_fusion.2
  353.1 0.9 copy.35
  354.1 0.2 convolution_multiply_fusion.1
  354.3 0.9 copy.34
  355.2 1.6 fusion.9
  356.8 0.9 copy.36
  357.7 58.9 %reduce-scatter.2.cloned.1.call-done = bf16[16,1,4096]{2,0,1:T(8,128)(2,1)} async-done(((bf16[256,1,4096]{2,0,1:T(8,128)(2,1)}), bf16[16,1,4096]{2,0,1:T(8,128)(2,1)}) %reduce-scatter.2.cloned.1.call-update) | async-done | bytes 131088 | tf_op jit(solution)/shard_map/reduce_scatter | solution.py:79
Async XLA Ops:
  7.2 256.2 %all-gather.3.cloned.1.call-start = ((), (), s32[]{:S(2)}) async-start(), calls=%async_computation.1 | async-start | bytes 3194880 | tf_op jit(solution)/shard_map/all_gather | solution.py:75
  7.9 341.5 %all-gather.5.cloned.1.call-start = ((), (), s32[]{:S(2)}) async-start(), calls=%async_computation.3 | async-start | bytes 2228224 | tf_op jit(solution)/shard_map/all_gather | solution.py:74
  8.6 407.9 %reduce-scatter.2.cloned.1.call-start = ((), (), s32[]{:S(2)}) async-start(), calls=%async_computation.2 | async-start | bytes 2228224 | tf_op jit(solution)/shard_map/reduce_scatter | solution.py:79
  11.9 251.5 %copy-start.2 = (bf16[1,256,384]{1,2,0:T(8,128)(2,1)}, bf16[1,256,384]{1,2,0:T(8,128)(2,1)S(1)}, u32[]{:S(2)}) copy-start(bf16[1,256,384]{1,2,0:T(8,128)(2,1)S(1)} %copy.27) | copy-start | bytes 589828
  263.4 86.0 %copy-start = (bf16[384,4096]{0,1:T(8,128)(2,1)S(1)}, bf16[384,4096]{0,1:T(8,128)(2,1)}, u32[]{:S(2)}) copy-start(bf16[384,4096]{0,1:T(8,128)(2,1)} %all-gather.3.cloned.1.call-done) | copy-start | bytes 9437188
  349.4 2.8 copy-start.1
  349.4 2.8 copy-start.3
  352.2 0.7 copy-start.4
Sparse Core Ops, SparseCore 0:
  10.7 252.6 all-gather.2
  266.1 83.2 all-gather.4
  353.4 63.1 reduce-scatter.1
where the time goes:
time: 423 us
  waiting for transfers between devices  390 us (92%)
  between operations  13.8 us (3%)
  matrix products  12.5 us (3%)
  local copies, waits for them, and re-layouts  6.12 us (1%)
    all_gather x1, waiting for transfers between devices, on_device(): columns = lax.all_gather(projection, ('dp', 'seq'), axis=1, tiled=True)  249 us
    all_gather x1, waiting for transfers between devices, on_device(): grad_full = lax.all_gather(upstream, 'mp', axis=0, tiled=True)  81.2 us
    reduce_scatter x1, waiting for transfers between devices, on_device(): lax.psum_scatter(jnp.einsum('qfc,cd->qfd', ordered, columns, preferred_el...  58.9 us
  transfers between devices with their start and end apart: 3, of which 3 were waited for; matrix products, arithmetic and copies ran while one was open for 4% of the time, Pallas kernels for 0%

commit v1 on v0

--- a/solution.py
+++ b/solution.py
@@ -3,7 +3,7 @@
 import jax
 import jax.numpy as jnp
 from jax import lax
-from jax.sharding import PartitionSpec as P
+from jax.sharding import Mesh, PartitionSpec as P
 
 HEADS = 48
 
@@ -66,24 +66,30 @@
     )
 
 
+def gather_columns(projection):
+    along_z = lax.all_gather(projection, ("zh", "zl"), axis=1, tiled=True)
+    along_yz = lax.all_gather(along_z, "y", axis=1, tiled=True)
+    rows, width = projection.shape
+    ys, zhs, zls = (lax.axis_size(a) for a in ("y", "zh", "zl"))
+    blocks = along_yz.reshape(rows, ys, zhs, zls, width)
+    return blocks.transpose(0, 2, 1, 3, 4).reshape(rows, -1)
+
+
 def on_device(queries, key_rows, value_rows, projection, upstream):
-    head_count = HEADS // lax.axis_size("mp")
+    head_count = HEADS // (lax.axis_size("x") * lax.axis_size("c"))
     soft = soft_weights(queries, key_rows, head_count)
     attended = attend_values(soft, value_rows, head_count)
     ordered = attended.transpose(1, 0, 2)
-    grad_full = lax.all_gather(upstream, "mp", axis=0, tiled=True)
-    columns = lax.all_gather(projection, ("dp", "seq"), axis=1, tiled=True)
+    grad_full = lax.all_gather(upstream, ("x", "c"), axis=0, tiled=True)
+    columns = gather_columns(projection)
     grad_attended = jnp.einsum(
         "qfd,cd->fqc", grad_full, columns, preferred_element_type=jnp.float32
     )
-    projected = lax.psum_scatter(
-        jnp.einsum("qfc,cd->qfd", ordered, columns, preferred_element_type=jnp.float32).astype(
-            jnp.bfloat16
-        ),
-        "mp",
-        scatter_dimension=0,
-        tiled=True,
-    )
+    partial = jnp.einsum(
+        "qfc,cd->qfd", ordered, columns, preferred_element_type=jnp.float32
+    ).astype(jnp.bfloat16)
+    projected = lax.psum_scatter(partial, "x", scatter_dimension=0, tiled=True)
+    projected = lax.psum_scatter(projected, "c", scatter_dimension=0, tiled=True)
     grad_rounded = grad_attended.astype(jnp.bfloat16)
     grad_q, grad_k, grad_v = backward_heads(
         soft, queries, key_rows, value_rows, grad_rounded, head_count
@@ -91,22 +97,33 @@
     return (projected, grad_q, grad_k, grad_v)
 
 
+def fine_mesh(mesh):
+    devices = mesh.devices
+    dp, mp, seq = devices.shape
+    ys = len({d.coords[1] for d in devices[:, 0, 0]}) if hasattr(devices[0, 0, 0], "coords") else dp
+    shape = (dp // ys, ys, mp // 2, 2, seq)
+    return Mesh(devices.reshape(shape), ("zh", "y", "x", "c", "zl"))
+
+
 def solution(mesh):
+    fine = fine_mesh(mesh)
+    frames = ("zh", "y", "zl")
+    heads = ("x", "c")
     return jax.shard_map(
         on_device,
-        mesh=mesh,
+        mesh=fine,
         in_specs=(
-            P(("dp", "seq"), None, "mp"),
-            P(("dp", "seq"), None, "mp"),
-            P(("dp", "seq"), None, "mp"),
-            P("mp", ("dp", "seq")),
-            P("mp", ("dp", "seq"), None),
+            P(frames, None, heads),
+            P(frames, None, heads),
+            P(frames, None, heads),
+            P(heads, frames),
+            P(heads, frames, None),
         ),
         out_specs=(
-            P("mp", ("dp", "seq"), None),
-            P(("dp", "seq"), None, "mp"),
-            P(("dp", "seq"), None, "mp"),
-            P(("dp", "seq"), None, "mp"),
+            P(heads, frames, None),
+            P(frames, None, heads),
+            P(frames, None, heads),
+            P(frames, None, heads),
         ),
         check_vma=False,
     )

time: 423 us -> 226 us (0.53)
  waiting for transfers between devices: 390 us -> 159 us
  blocking collectives: 0 us -> 34.5 us
    all_gather x2, waiting for transfers between devices: 330 us -> 90.6 us  [the longest x1 48.2 us: gather_columns(): along_yz = lax.all_gather(along_z, 'y', axis=1, tiled=True)]
    all_gather x0 -> x1, blocking collectives: none -> 34.5 us  [gather_columns(): along_z = lax.all_gather(projection, ('zh', 'zl'), axis=1, tiled=True)]
    reduce_scatter x1 -> x2, waiting for transfers between devices: 58.9 us -> 67.4 us  [the longest x1 42.4 us: on_device(): projected = lax.psum_scatter(partial, 'x', scatter_dimension=0, tiled=True)]
  transfers between devices with their start and end apart: 3 -> 4, of which waited for: 3 -> 4; matrix products, arithmetic and copies ran while one was open for 4% -> 8% of each run, Pallas kernels for 0% -> 0%
where the time goes in v1:
time: 226 us; the launch traced here: 225 us
  waiting for transfers between devices  159 us (70%)
  blocking collectives  34.5 us (15%)
  between operations  13.9 us (6%)
  matrix products  9.51 us (4%)
  local copies, waits for them, and re-layouts  8.55 us (4%)
    all_gather x1, waiting for transfers between devices, gather_columns(): along_yz = lax.all_gather(along_z, 'y', axis=1, tiled=True)  48.2 us
    all_gather x1, waiting for transfers between devices, on_device(): grad_full = lax.all_gather(upstream, ('x', 'c'), axis=0, tiled=True)  42.5 us
    reduce_scatter x1, waiting for transfers between devices, on_device(): projected = lax.psum_scatter(partial, 'x', scatter_dimension=0, tiled=True)  42.4 us
    all_gather x1, blocking collectives, gather_columns(): along_z = lax.all_gather(projection, ('zh', 'zl'), axis=1, tiled=True)  34.5 us
    reduce_scatter x1, waiting for transfers between devices, on_device(): lax.psum_scatter(projected, 'c', scatter_dimension=0, tiled=True)  25 us
    unnamed x18, local copies, waits for them, and re-layouts  6.29 us
  transfers between devices with their start and end apart: 4, of which 4 were waited for; matrix products, arithmetic and copies ran while one was open for 8% of the time, Pallas kernels for 0%

profile of v1, /device:TPU:1, one launch (start us, length us, event | category | flops | bytes accessed | tf_op | source)
XLA Modules:
  0.0 225.5 jit_solution(14595003363222210659)
XLA Ops:
  7.2 0.0 all-gather.3.cloned.1.call-start
  7.2 34.5 %all_gather.9 = bf16[384,512]{0,1:T(8,128)(2,1)} all-gather(bf16[384,64]{0,1:T(8,128)(2,1)} %param.8), channel_id=1, replica_groups=mesh['zh'=4,'y'=8,'x'=8,'c'=2,'zl'=2] {'zh','zl'}, dimensions={1}, use_global_device_ids=true | all-gather | bytes 442368 | tf_op jit(solution)/shard_map/all_gather | solution.py:70
  41.7 0.0 all-gather.3.cloned.1.call-update
  41.7 0.0 all-gather.5.cloned.1.call-start
  41.8 0.7 all-gather.5.cloned.1.call-update
  42.5 0.0 reduce-scatter.3.cloned.1.call-start
  42.5 1.1 copy.37
  43.6 1.1 copy.38
  44.7 1.1 copy.41
  45.7 0.0 copy-start.1
  45.7 1.3 fusion.14
  47.1 1.3 convolution_convert_fusion.1
  48.4 48.2 %all-gather.3.cloned.1.call-done = bf16[384,4096]{0,1:T(8,128)(2,1)} async-done(((bf16[384,512]{0,1:T(8,128)(2,1)}), bf16[384,4096]{0,1:T(8,128)(2,1)}) %all-gather.3.cloned.1.call-update) | async-done | bytes 3145744 | tf_op jit(solution)/shard_map/all_gather | solution.py:71
  96.5 0.0 copy-done.1
  96.5 0.0 copy-start.3
  96.5 2.3 %copy.43 = bf16[384,4,8,2,64]{0,4,3,2,1:T(8,128)(2,1)S(1)} copy(bf16[384,4,8,2,64]{0,4,3,1,2:T(8,128)(2,1)} %bitcast.64) | data formatting | bytes 6291456 | tf_op jit(solution)/shard_map/transpose | solution.py:75
  98.8 0.0 copy-done.3
  98.8 2.7 %fusion.1 = bf16[256,1,4096]{2,0,1:T(8,128)(2,1)} fusion(bf16[256,384]{0,1:T(8,128)(2,1)S(1)} %bitcast.78, bf16[384,4096]{0,1:T(8,128)(2,1)S(1)} %bitcast.62), kind=kOutput, calls=%fused_computation.2 | convolution fusion | flops 806354944 | bytes 5439488 | tf_op jit(solution)/shard_map/qfc,cd->qfd/dot_general | solution.py:88
  101.5 0.0 reduce-scatter.3.cloned.1.call-update
  101.5 0.0 reduce-scatter.5.cloned.1.call-start
  101.5 42.5 %all-gather.5.cloned.1.call-done = bf16[256,1,4096]{2,0,1:T(8,128)(2,1)} async-done(((bf16[16,1,4096]{2,0,1:T(8,128)(2,1)}), bf16[256,1,4096]{2,0,1:T(8,128)(2,1)}) %all-gather.5.cloned.1.call-update) | async-done | bytes 2097168 | tf_op jit(solution)/shard_map/all_gather | solution.py:83
  144.0 0.0 copy-start
  144.0 0.0 copy-start.2
  144.0 2.8 %fusion.6 = bf16[384,256]{1,0:T(8,128)(2,1)S(1)} fusion(bf16[384,4096]{0,1:T(8,128)(2,1)S(1)} %bitcast.63, bf16[256,1,4096]{2,0,1:T(8,128)(2,1)} %all-gather.5.cloned.1.call-done), kind=kOutput, calls=%fused_computation.10 | convolution fusion | flops 805404672 | bytes 5439488 | tf_op jit(solution)/shard_map/qfd,cd->fqc/dot_general | solution.py:85
  146.8 0.0 copy-start.4
  146.8 0.0 copy-done
  146.8 0.0 copy-done.2
  146.8 0.3 multiply_reduce_fusion
  147.1 0.3 copy-done.4
  147.5 0.0 copy-start.5
  147.5 0.2 multiply_convert_fusion
  147.6 42.4 %reduce-scatter.3.cloned.1.call-done = bf16[32,1,4096]{2,0,1:T(8,128)(2,1)} async-done(((bf16[256,1,4096]{2,0,1:T(8,128)(2,1)}), bf16[32,1,4096]{2,0,1:T(8,128)(2,1)}) %reduce-scatter.3.cloned.1.call-update) | async-done | bytes 262160 | tf_op jit(solution)/shard_map/reduce_scatter | solution.py:91
  190.0 0.0 reduce-scatter.5.cloned.1.call-update
  190.0 0.3 convolution_multiply_fusion.2
  190.3 0.9 copy.50
  191.2 0.2 convolution_multiply_fusion.1
  191.5 0.9 copy.49
  192.4 0.0 copy-done.5
  192.4 0.6 fusion.9
  193.0 0.9 copy.51
  193.9 25.0 %reduce-scatter.5.cloned.1.call-done = bf16[16,1,4096]{2,0,1:T(8,128)(2,1)} async-done(((bf16[32,1,4096]{2,0,1:T(8,128)(2,1)}), bf16[16,1,4096]{2,0,1:T(8,128)(2,1)}) %reduce-scatter.5.cloned.1.call-update) | async-done | bytes 131088 | tf_op jit(solution)/shard_map/reduce_scatter | solution.py:92
Async XLA Ops:
  7.2 89.4 %all-gather.3.cloned.1.call-start = ((), (), s32[]{:S(2)}) async-start(), calls=%async_computation.2 | async-start | bytes 3538944 | tf_op jit(solution)/shard_map/all_gather | solution.py:71
  41.7 102.3 %all-gather.5.cloned.1.call-start = ((), (), s32[]{:S(2)}) async-start(), calls=%async_computation.5 | async-start | bytes 2228224 | tf_op jit(solution)/shard_map/all_gather | solution.py:83
  42.5 147.5 %reduce-scatter.3.cloned.1.call-start = ((), (), s32[]{:S(2)}) async-start(), calls=%async_computation.3 | async-start | bytes 2359296 | tf_op jit(solution)/shard_map/reduce_scatter | solution.py:91
  45.7 50.8 %copy-start.1 = (bf16[1,256,384]{1,2,0:T(8,128)(2,1)}, bf16[1,256,384]{1,2,0:T(8,128)(2,1)S(1)}, u32[]{:S(2)}) copy-start(bf16[1,256,384]{1,2,0:T(8,128)(2,1)S(1)} %copy.41) | copy-start | bytes 589828
  96.5 2.3 %copy-start.3 = (bf16[3,256,128]{1,2,0:T(8,128)(2,1)S(1)}, bf16[3,256,128]{1,2,0:T(8,128)(2,1)}, u32[]{:S(2)}) copy-start(bf16[3,256,128]{1,2,0:T(8,128)(2,1)} %convolution_convert_fusion.1) | copy-start | bytes 589828
  101.5 117.4 %reduce-scatter.5.cloned.1.call-start = ((), (), s32[]{:S(2)}) async-start(), calls=%async_computation.4 | async-start | bytes 393216 | tf_op jit(solution)/shard_map/reduce_scatter | solution.py:92
  144.0 2.8 %copy-start = (f32[3,256,256]{1,2,0:T(8,128)S(1)}, f32[3,256,256]{1,2,0:T(8,128)}, u32[]{:S(2)}) copy-start(f32[3,256,256]{1,2,0:T(8,128)} %get-tuple-element.17) | copy-start | bytes 2359300
  144.0 2.8 %copy-start.2 = (bf16[1,256,384]{1,2,0:T(8,128)(2,1)S(1)}, bf16[1,256,384]{1,2,0:T(8,128)(2,1)}, u32[]{:S(2)}) copy-start(bf16[1,256,384]{1,2,0:T(8,128)(2,1)} %copy-done.1) | copy-start | bytes 589828
  146.8 0.7 copy-start.4
  147.5 44.9 %copy-start.5 = (bf16[384,256]{1,0:T(8,128)(2,1)S(1)}, bf16[384,256]{1,0:T(8,128)(2,1)}, u32[]{:S(2)}) copy-start(bf16[384,256]{1,0:T(8,128)(2,1)} %copy-done.4) | copy-start | bytes 589828
Sparse Core Ops, SparseCore 0:
  41.8 54.6 all-gather.2
  99.2 44.7 all-gather.4
  147.4 42.5 reduce-scatter.2
  193.8 25.1 reduce-scatter.4

commit v2 on v1

--- a/solution.py
+++ b/solution.py
@@ -75,6 +75,13 @@
     return blocks.transpose(0, 2, 1, 3, 4).reshape(rows, -1)
 
 
+def sum_patch_blocks(partial):
+    groups = lax.axis_size("x") * lax.axis_size("c")
+    blocks = partial.reshape(groups, partial.shape[0] // groups, *partial.shape[1:])
+    received = lax.all_to_all(blocks, ("x", "c"), 0, 0, tiled=False)
+    return received.astype(jnp.float32).sum(axis=0).astype(jnp.bfloat16)
+
+
 def on_device(queries, key_rows, value_rows, projection, upstream):
     head_count = HEADS // (lax.axis_size("x") * lax.axis_size("c"))
     soft = soft_weights(queries, key_rows, head_count)
@@ -88,8 +95,7 @@
     partial = jnp.einsum(
         "qfc,cd->qfd", ordered, columns, preferred_element_type=jnp.float32
     ).astype(jnp.bfloat16)
-    projected = lax.psum_scatter(partial, "x", scatter_dimension=0, tiled=True)
-    projected = lax.psum_scatter(projected, "c", scatter_dimension=0, tiled=True)
+    projected = sum_patch_blocks(partial)
     grad_rounded = grad_attended.astype(jnp.bfloat16)
     grad_q, grad_k, grad_v = backward_heads(
         soft, queries, key_rows, value_rows, grad_rounded, head_count

time: 226 us -> 187 us (0.83)
  the two profiles are of different devices: /device:TPU:1 before, /device:TPU:7 now
where the time goes in v2:
time: 187 us
  waiting for transfers between devices  110 us (59%)
  blocking collectives  33.7 us (18%)
  between operations  14.1 us (8%)
  matrix products  10.5 us (6%)
  local copies, waits for them, and re-layouts  8.39 us (4%)
  starting transfers between devices  8.08 us (4%)
  other arithmetic  2.74 us (1%)
    all_gather x1, waiting for transfers between devices, on_device(): grad_full = lax.all_gather(upstream, ('x', 'c'), axis=0, tiled=True)  60.7 us
    all_gather x1, waiting for transfers between devices, gather_columns(): along_yz = lax.all_gather(along_z, 'y', axis=1, tiled=True)  48.1 us
    all_gather x1, blocking collectives, gather_columns(): along_z = lax.all_gather(projection, ('zh', 'zl'), axis=1, tiled=True)  33.7 us
    all_to_all x1, starting transfers between devices, sum_patch_blocks(): received = lax.all_to_all(blocks, ('x', 'c'), 0, 0, tiled=False)  8 us
    unnamed x16, local copies, waits for them, and re-layouts  6.12 us
  transfers between devices with their start and end apart: 3, of which 2 were waited for; matrix products, arithmetic and copies ran while one was open for 10% of the time, Pallas kernels for 0%

profile of v2, /device:TPU:7, one launch (start us, length us, event | category | flops | bytes accessed | tf_op | source)
XLA Modules:
  0.0 187.0 jit_solution(8895587657414358563)
XLA Ops:
  7.2 0.0 all-gather.3.cloned.1.call-start
  7.2 33.7 %all_gather.9 = bf16[384,512]{0,1:T(8,128)(2,1)} all-gather(bf16[384,64]{0,1:T(8,128)(2,1)} %param.8), channel_id=1, replica_groups=mesh['zh'=4,'y'=8,'x'=8,'c'=2,'zl'=2] {'zh','zl'}, dimensions={1}, use_global_device_ids=true | all-gather | bytes 442368 | tf_op jit(solution)/shard_map/all_gather | solution.py:70
  40.9 0.0 all-gather.3.cloned.1.call-update
  40.9 0.0 all-gather.5.cloned.1.call-start
  40.9 0.7 all-gather.5.cloned.1.call-update
  41.6 1.1 copy.52
  42.7 1.1 copy.53
  43.8 1.1 copy.56
  44.8 0.0 copy-start.1
  44.9 1.3 fusion.13
  46.2 1.3 convolution_convert_fusion.1
  47.5 48.1 %all-gather.3.cloned.1.call-done = bf16[384,4096]{0,1:T(8,128)(2,1)} async-done(((bf16[384,512]{0,1:T(8,128)(2,1)}), bf16[384,4096]{0,1:T(8,128)(2,1)}) %all-gather.3.cloned.1.call-update) | async-done | bytes 3145744 | tf_op jit(solution)/shard_map/all_gather | solution.py:71
  95.6 0.0 copy-done.1
  95.6 0.0 copy-start.3
  95.6 2.3 %copy.58 = bf16[384,4,8,2,64]{0,4,3,2,1:T(8,128)(2,1)S(1)} copy(bf16[384,4,8,2,64]{0,4,3,1,2:T(8,128)(2,1)} %bitcast.67) | data formatting | bytes 6291456 | tf_op jit(solution)/shard_map/transpose | solution.py:75
  97.9 0.0 copy-done.3
  97.9 2.7 %convolution_convert_fusion = bf16[256,4096]{1,0:T(8,128)(2,1)} fusion(bf16[256,384]{0,1:T(8,128)(2,1)S(1)} %bitcast.81, bf16[384,4096]{0,1:T(8,128)(2,1)S(1)} %bitcast.64), kind=kOutput, calls=%fused_computation.1 | convolution fusion | flops 806354944 | bytes 5439488 | tf_op jit(solution)/shard_map/qfc,cd->qfd/dot_general | solution.py:95
  100.6 8.0 %all-to-all-start = ((bf16[16,16,1,4096]{3,1,2,0:T(8,128)(2,1)}), bf16[16,16,1,4096]{3,1,2,0:T(8,128)(2,1)}, u32[]{:S(2)}, u32[]{:S(2)}) async-start(bf16[16,16,1,4096]{3,1,2,0:T(8,128)(2,1)} %bitcast.66), calls=%async_computation | async-start | bytes 4194304 | tf_op jit(solution)/shard_map/all_to_all | solution.py:81
  108.6 60.7 %all-gather.5.cloned.1.call-done = bf16[256,1,4096]{2,0,1:T(8,128)(2,1)} async-done(((bf16[16,1,4096]{2,0,1:T(8,128)(2,1)}), bf16[256,1,4096]{2,0,1:T(8,128)(2,1)}) %all-gather.5.cloned.1.call-update) | async-done | bytes 2097168 | tf_op jit(solution)/shard_map/all_gather | solution.py:90
  169.3 0.0 copy-start
  169.3 0.0 copy-start.2
  169.3 2.8 %fusion.5 = bf16[384,256]{1,0:T(8,128)(2,1)S(1)} fusion(bf16[384,4096]{0,1:T(8,128)(2,1)S(1)} %bitcast.65, bf16[256,1,4096]{2,0,1:T(8,128)(2,1)} %all-gather.5.cloned.1.call-done), kind=kOutput, calls=%fused_computation.9 | convolution fusion | flops 805404672 | bytes 5439488 | tf_op jit(solution)/shard_map/qfd,cd->fqc/dot_general | solution.py:92
  172.1 0.0 copy-start.4
  172.1 0.0 copy-done
  172.1 0.0 copy-done.2
  172.1 0.3 multiply_reduce_fusion
  172.5 0.2 multiply_convert_fusion
  172.6 0.2 copy-done.4
  172.8 0.3 convolution_multiply_fusion.2
  173.1 0.9 copy.66
  174.0 0.2 convolution_multiply_fusion.1
  174.2 0.9 copy.65
  175.1 1.6 fusion.8
  176.7 0.9 copy.67
  177.6 0.0 all-to-all-done
  177.6 2.6 %reduce_sum.33 = bf16[16,4096]{1,0:T(8,128)(2,1)} reduce(bf16[16,16,1,4096]{3,1,2,0:T(8,128)(2,1)} %all-to-all-done, bf16[]{:T(256)} %constant.3.clone.1), dimensions={0,2}, to_apply=%region_2.0 | reduce | flops 983040 | bytes 2228226 | tf_op jit(solution)/shard_map/reduce_sum | solution.py:82
Async XLA Ops:
  7.2 88.5 %all-gather.3.cloned.1.call-start = ((), (), s32[]{:S(2)}) async-start(), calls=%async_computation.1 | async-start | bytes 3538944 | tf_op jit(solution)/shard_map/all_gather | solution.py:71
  40.9 128.4 %all-gather.5.cloned.1.call-start = ((), (), s32[]{:S(2)}) async-start(), calls=%async_computation.2 | async-start | bytes 2228224 | tf_op jit(solution)/shard_map/all_gather | solution.py:90
  44.8 50.8 %copy-start.1 = (bf16[1,256,384]{1,2,0:T(8,128)(2,1)}, bf16[1,256,384]{1,2,0:T(8,128)(2,1)S(1)}, u32[]{:S(2)}) copy-start(bf16[1,256,384]{1,2,0:T(8,128)(2,1)S(1)} %copy.56) | copy-start | bytes 589828
  95.6 2.3 %copy-start.3 = (bf16[3,256,128]{1,2,0:T(8,128)(2,1)S(1)}, bf16[3,256,128]{1,2,0:T(8,128)(2,1)}, u32[]{:S(2)}) copy-start(bf16[3,256,128]{1,2,0:T(8,128)(2,1)} %convolution_convert_fusion.1) | copy-start | bytes 589828
  100.6 77.0 %all-to-all-start = ((bf16[16,16,1,4096]{3,1,2,0:T(8,128)(2,1)}), bf16[16,16,1,4096]{3,1,2,0:T(8,128)(2,1)}, u32[]{:S(2)}, u32[]{:S(2)}) async-start(bf16[16,16,1,4096]{3,1,2,0:T(8,128)(2,1)} %bitcast.66), calls=%async_computation | async-start | bytes 4194304 | tf_op jit(solution)/shard_map/all_to_all | solution.py:81
  169.3 2.8 %copy-start = (f32[3,256,256]{1,2,0:T(8,128)S(1)}, f32[3,256,256]{1,2,0:T(8,128)}, u32[]{:S(2)}) copy-start(f32[3,256,256]{1,2,0:T(8,128)} %get-tuple-element.21) | copy-start | bytes 2359300
  169.3 2.8 %copy-start.2 = (bf16[1,256,384]{1,2,0:T(8,128)(2,1)S(1)}, bf16[1,256,384]{1,2,0:T(8,128)(2,1)}, u32[]{:S(2)}) copy-start(bf16[1,256,384]{1,2,0:T(8,128)(2,1)} %copy-done.1) | copy-start | bytes 589828
  172.1 0.7 copy-start.4
Sparse Core Ops, SparseCore 0:
  41.0 54.5 all-gather.2
  98.3 70.9 all-gather.4

commit v3 on v2

--- a/solution.py
+++ b/solution.py
@@ -75,6 +75,13 @@
     return blocks.transpose(0, 2, 1, 3, 4).reshape(rows, -1)
 
 
+def gather_patch_blocks(upstream):
+    groups = lax.axis_size("x") * lax.axis_size("c")
+    copies = jnp.broadcast_to(upstream[None], (groups,) + upstream.shape)
+    received = lax.all_to_all(copies, ("x", "c"), 0, 0, tiled=False)
+    return received.reshape(groups * upstream.shape[0], *upstream.shape[1:])
+
+
 def sum_patch_blocks(partial):
     groups = lax.axis_size("x") * lax.axis_size("c")
     blocks = partial.reshape(groups, partial.shape[0] // groups, *partial.shape[1:])
@@ -87,7 +94,7 @@
     soft = soft_weights(queries, key_rows, head_count)
     attended = attend_values(soft, value_rows, head_count)
     ordered = attended.transpose(1, 0, 2)
-    grad_full = lax.all_gather(upstream, ("x", "c"), axis=0, tiled=True)
+    grad_full = gather_patch_blocks(upstream)
     columns = gather_columns(projection)
     grad_attended = jnp.einsum(
         "qfd,cd->fqc", grad_full, columns, preferred_element_type=jnp.float32

time: 187 us -> 170 us (0.909)
  the two profiles are of different devices: /device:TPU:7 before, /device:TPU:1 now
where the time goes in v3:
time: 170 us
  waiting for transfers between devices  81.8 us (48%)
  blocking collectives  34.5 us (20%)
  starting transfers between devices  18.2 us (11%)
  between operations  14.2 us (8%)
  matrix products  10.4 us (6%)
  local copies, waits for them, and re-layouts  8.23 us (5%)
  other arithmetic  2.74 us (2%)
    all_to_all x1, waiting for transfers between devices, sum_patch_blocks(): received = lax.all_to_all(blocks, ('x', 'c'), 0, 0, tiled=False)  40.8 us
    all_gather x1, waiting for transfers between devices, gather_columns(): along_yz = lax.all_gather(along_z, 'y', axis=1, tiled=True)  35.9 us
    all_gather x1, blocking collectives, gather_columns(): along_z = lax.all_gather(projection, ('zh', 'zl'), axis=1, tiled=True)  34.5 us
    all_to_all x1, starting transfers between devices, gather_patch_blocks(): received = lax.all_to_all(copies, ('x', 'c'), 0, 0, tiled=False)  13.2 us
    all_to_all x1, waiting for transfers between devices, gather_patch_blocks(): received = lax.all_to_all(copies, ('x', 'c'), 0, 0, tiled=False)  5.1 us
    all_to_all x1, starting transfers between devices, sum_patch_blocks(): received = lax.all_to_all(blocks, ('x', 'c'), 0, 0, tiled=False)  4.98 us
  transfers between devices with their start and end apart: 3, of which 3 were waited for; matrix products, arithmetic and copies ran while one was open for 11% of the time, Pallas kernels for 0%

profile of v3, /device:TPU:1, one launch (start us, length us, event | category | flops | bytes accessed | tf_op | source)
XLA Modules:
  0.0 170.0 jit_solution(3773984097139178739)
XLA Ops:
  7.2 0.0 all-gather.2.cloned.1.call-start
  7.2 34.5 %all_gather.6 = bf16[384,512]{0,1:T(8,128)(2,1)} all-gather(bf16[384,64]{0,1:T(8,128)(2,1)} %param.8), channel_id=1, replica_groups=mesh['zh'=4,'y'=8,'x'=8,'c'=2,'zl'=2] {'zh','zl'}, dimensions={1}, use_global_device_ids=true | all-gather | bytes 442368 | tf_op jit(solution)/shard_map/all_gather | solution.py:70
  41.7 0.0 all-gather.2.cloned.1.call-update
  41.7 0.0 copy-start.1
  41.7 0.0 copy-start.2
  41.7 0.0 copy-start.3
  41.8 2.6 %broadcast_in_dim.5 = bf16[16,16,1,4096]{3,1,2,0:T(8,128)(2,1)} broadcast(bf16[16,4096]{1,0:T(8,128)(2,1)} %bitcast.80), dimensions={1,3} | broadcast | bytes 2228224 | tf_op jit(solution)/shard_map/broadcast_in_dim | solution.py:80
  44.3 13.2 %all-to-all-start.1 = ((bf16[16,16,1,4096]{3,1,2,0:T(8,128)(2,1)}), bf16[16,16,1,4096]{3,1,2,0:T(8,128)(2,1)}, u32[]{:S(2)}, u32[]{:S(2)}) async-start(bf16[16,16,1,4096]{3,1,2,0:T(8,128)(2,1)} %broadcast_in_dim.5), calls=%async_computation.1 | async-start | bytes 4194304 | tf_op jit(solution)/shard_map/all_to_all | solution.py:81
  57.5 0.0 copy-done.1
  57.5 0.1 copy.52
  57.7 0.0 copy-done.2
  57.7 0.1 copy.53
  57.8 0.0 copy-done.3
  57.9 0.1 copy.56
  58.0 0.0 copy-start.4
  58.0 1.3 fusion.8
  59.3 1.3 convolution_convert_fusion.1
  60.6 35.9 %all-gather.2.cloned.1.call-done = bf16[384,4096]{0,1:T(8,128)(2,1)} async-done(((bf16[384,512]{0,1:T(8,128)(2,1)}), bf16[384,4096]{0,1:T(8,128)(2,1)}) %all-gather.2.cloned.1.call-update) | async-done | bytes 3145744 | tf_op jit(solution)/shard_map/all_gather | solution.py:71
  96.5 0.0 copy-done.4
  96.5 0.0 copy-start.6
  96.5 2.3 %copy.58 = bf16[384,4,8,2,64]{0,4,3,2,1:T(8,128)(2,1)S(1)} copy(bf16[384,4,8,2,64]{0,4,3,1,2:T(8,128)(2,1)} %bitcast.65) | data formatting | bytes 6291456 | tf_op jit(solution)/shard_map/transpose | solution.py:75
  98.8 0.0 copy-done.6
  98.8 2.7 %convolution_convert_fusion = bf16[256,4096]{1,0:T(8,128)(2,1)} fusion(bf16[256,384]{0,1:T(8,128)(2,1)S(1)} %bitcast.79, bf16[384,4096]{0,1:T(8,128)(2,1)S(1)} %bitcast.62), kind=kOutput, calls=%fused_computation.1 | convolution fusion | flops 806354944 | bytes 5439488 | tf_op jit(solution)/shard_map/qfc,cd->qfd/dot_general | solution.py:102
  101.5 5.1 %all-to-all-done.1 = bf16[16,16,1,4096]{3,1,2,0:T(8,128)(2,1)} async-done(((bf16[16,16,1,4096]{3,1,2,0:T(8,128)(2,1)}), bf16[16,16,1,4096]{3,1,2,0:T(8,128)(2,1)}, u32[]{:S(2)}, u32[]{:S(2)}) %all-to-all-start.1) | async-done | bytes 2097184 | tf_op jit(solution)/shard_map/all_to_all | solution.py:81
  106.6 5.0 %all-to-all-start = ((bf16[16,16,1,4096]{3,1,2,0:T(8,128)(2,1)}), bf16[16,16,1,4096]{3,1,2,0:T(8,128)(2,1)}, u32[]{:S(2)}, u32[]{:S(2)}) async-start(bf16[16,16,1,4096]{3,1,2,0:T(8,128)(2,1)} %bitcast.64), calls=%async_computation | async-start | bytes 4194304 | tf_op jit(solution)/shard_map/all_to_all | solution.py:88
  111.6 0.0 copy-start
  111.6 0.0 copy-start.5
  111.6 2.8 %convolution_convert_fusion.2 = bf16[384,256]{1,0:T(8,128)(2,1)S(1)} fusion(bf16[384,4096]{0,1:T(8,128)(2,1)S(1)} %bitcast.63, bf16[256,4096]{1,0:T(8,128)(2,1)} %bitcast.14), kind=kOutput, calls=%fused_computation.8 | convolution fusion | flops 805404672 | bytes 5439488 | tf_op jit(solution)/shard_map/qfd,cd->fqc/dot_general | solution.py:99
  114.3 0.0 copy-start.7
  114.3 0.0 copy-done
  114.4 0.0 copy-done.5
  114.4 0.3 multiply_reduce_fusion
  114.7 0.2 multiply_convert_fusion
  114.9 0.2 copy-done.7
  115.0 0.3 convolution_multiply_fusion.2
  115.3 0.9 copy.66
  116.2 0.2 convolution_multiply_fusion.1
  116.4 0.9 copy.65
  117.4 1.6 fusion.3
  118.9 0.9 copy.67
  119.8 40.8 %all-to-all-done = bf16[16,16,1,4096]{3,1,2,0:T(8,128)(2,1)} async-done(((bf16[16,16,1,4096]{3,1,2,0:T(8,128)(2,1)}), bf16[16,16,1,4096]{3,1,2,0:T(8,128)(2,1)}, u32[]{:S(2)}, u32[]{:S(2)}) %all-to-all-start) | async-done | bytes 2097184 | tf_op jit(solution)/shard_map/all_to_all | solution.py:88
  160.6 2.6 %reduce_sum.33 = bf16[16,4096]{1,0:T(8,128)(2,1)} reduce(bf16[16,16,1,4096]{3,1,2,0:T(8,128)(2,1)} %all-to-all-done, bf16[]{:T(256)} %constant.3.clone.1), dimensions={0,2}, to_apply=%region_2.0 | reduce | flops 983040 | bytes 2228226 | tf_op jit(solution)/shard_map/reduce_sum | solution.py:89
Async XLA Ops:
  7.2 89.4 %all-gather.2.cloned.1.call-start = ((), (), s32[]{:S(2)}) async-start(), calls=%async_computation.2 | async-start | bytes 3538944 | tf_op jit(solution)/shard_map/all_gather | solution.py:71
  41.7 15.8 %copy-start.1 = (bf16[1,256,384]{2,1,0:T(8,128)(2,1)S(1)}, bf16[1,256,384]{2,1,0:T(8,128)(2,1)}, u32[]{:S(2)}) copy-start(bf16[1,256,384]{2,1,0:T(8,128)(2,1)} %param.5) | copy-start | bytes 589828
  41.7 15.9 %copy-start.2 = (bf16[1,256,384]{2,1,0:T(8,128)(2,1)S(1)}, bf16[1,256,384]{2,1,0:T(8,128)(2,1)}, u32[]{:S(2)}) copy-start(bf16[1,256,384]{2,1,0:T(8,128)(2,1)} %param.6) | copy-start | bytes 589828
  41.7 16.1 %copy-start.3 = (bf16[1,256,384]{2,1,0:T(8,128)(2,1)S(1)}, bf16[1,256,384]{2,1,0:T(8,128)(2,1)}, u32[]{:S(2)}) copy-start(bf16[1,256,384]{2,1,0:T(8,128)(2,1)} %param.7) | copy-start | bytes 589828
  44.3 62.3 %all-to-all-start.1 = ((bf16[16,16,1,4096]{3,1,2,0:T(8,128)(2,1)}), bf16[16,16,1,4096]{3,1,2,0:T(8,128)(2,1)}, u32[]{:S(2)}, u32[]{:S(2)}) async-start(bf16[16,16,1,4096]{3,1,2,0:T(8,128)(2,1)} %broadcast_in_dim.5), calls=%async_computation.1 | async-start | bytes 4194304 | tf_op jit(solution)/shard_map/all_to_all | solution.py:81
  58.0 38.5 %copy-start.4 = (bf16[1,256,384]{1,2,0:T(8,128)(2,1)}, bf16[1,256,384]{1,2,0:T(8,128)(2,1)S(1)}, u32[]{:S(2)}) copy-start(bf16[1,256,384]{1,2,0:T(8,128)(2,1)S(1)} %copy.56) | copy-start | bytes 589828
  96.5 2.3 %copy-start.6 = (bf16[3,256,128]{1,2,0:T(8,128)(2,1)S(1)}, bf16[3,256,128]{1,2,0:T(8,128)(2,1)}, u32[]{:S(2)}) copy-start(bf16[3,256,128]{1,2,0:T(8,128)(2,1)} %convolution_convert_fusion.1) | copy-start | bytes 589828
  106.6 54.0 %all-to-all-start = ((bf16[16,16,1,4096]{3,1,2,0:T(8,128)(2,1)}), bf16[16,16,1,4096]{3,1,2,0:T(8,128)(2,1)}, u32[]{:S(2)}, u32[]{:S(2)}) async-start(bf16[16,16,1,4096]{3,1,2,0:T(8,128)(2,1)} %bitcast.64), calls=%async_computation | async-start | bytes 4194304 | tf_op jit(solution)/shard_map/all_to_all | solution.py:88
  111.6 2.8 %copy-start = (f32[3,256,256]{1,2,0:T(8,128)S(1)}, f32[3,256,256]{1,2,0:T(8,128)}, u32[]{:S(2)}) copy-start(f32[3,256,256]{1,2,0:T(8,128)} %get-tuple-element.21) | copy-start | bytes 2359300
  111.6 2.8 %copy-start.5 = (bf16[1,256,384]{1,2,0:T(8,128)(2,1)S(1)}, bf16[1,256,384]{1,2,0:T(8,128)(2,1)}, u32[]{:S(2)}) copy-start(bf16[1,256,384]{1,2,0:T(8,128)(2,1)} %copy-done.4) | copy-start | bytes 589828
  114.3 0.7 copy-start.7
Sparse Core Ops, SparseCore 0:
  41.8 54.6 all-gather.1

commit v4 on v2

--- a/solution.py
+++ b/solution.py
@@ -75,10 +75,28 @@
     return blocks.transpose(0, 2, 1, 3, 4).reshape(rows, -1)
 
 
+def swap_cores(block):
+    return lax.ppermute(block, "c", [(0, 1), (1, 0)])
+
+
+def gather_patch_blocks(upstream):
+    chips = lax.axis_size("x")
+    copies = jnp.broadcast_to(upstream[None], (chips,) + upstream.shape)
+    mine = lax.all_to_all(copies, "x", 0, 0, tiled=False)
+    other = swap_cores(mine)
+    first = lax.axis_index("c") == 0
+    both = jnp.stack([jnp.where(first, mine, other), jnp.where(first, other, mine)], axis=1)
+    return both.reshape(chips * 2 * upstream.shape[0], *upstream.shape[1:])
+
+
 def sum_patch_blocks(partial):
-    groups = lax.axis_size("x") * lax.axis_size("c")
-    blocks = partial.reshape(groups, partial.shape[0] // groups, *partial.shape[1:])
-    received = lax.all_to_all(blocks, ("x", "c"), 0, 0, tiled=False)
+    chips = lax.axis_size("x")
+    blocks = partial.reshape(chips, 2, partial.shape[0] // (2 * chips), *partial.shape[1:])
+    core = lax.axis_index("c")
+    keep = lax.dynamic_index_in_dim(blocks, core, axis=1, keepdims=False)
+    send = lax.dynamic_index_in_dim(blocks, 1 - core, axis=1, keepdims=False)
+    pair = (keep.astype(jnp.float32) + swap_cores(send).astype(jnp.float32)).astype(jnp.bfloat16)
+    received = lax.all_to_all(pair, "x", 0, 0, tiled=False)
     return received.astype(jnp.float32).sum(axis=0).astype(jnp.bfloat16)
 
 
@@ -87,7 +105,7 @@
     soft = soft_weights(queries, key_rows, head_count)
     attended = attend_values(soft, value_rows, head_count)
     ordered = attended.transpose(1, 0, 2)
-    grad_full = lax.all_gather(upstream, ("x", "c"), axis=0, tiled=True)
+    grad_full = gather_patch_blocks(upstream)
     columns = gather_columns(projection)
     grad_attended = jnp.einsum(
         "qfd,cd->fqc", grad_full, columns, preferred_element_type=jnp.float32

time: 187 us -> 157 us (0.84)
  the two profiles are of different devices: /device:TPU:7 before, /device:TPU:1 now
where the time goes in v4:
time: 157 us; the launch traced here: 156 us
  waiting for transfers between devices  54.5 us (35%)
  blocking collectives  34.6 us (22%)
  starting transfers between devices  23.3 us (15%)
  between operations  14.2 us (9%)
  local copies, waits for them, and re-layouts  11.3 us (7%)
  other arithmetic  9.53 us (6%)
  matrix products  8.61 us (5%)
    all_gather x1, blocking collectives, gather_columns(): along_z = lax.all_gather(projection, ('zh', 'zl'), axis=1, tiled=True)  34.6 us
    all_to_all x1, waiting for transfers between devices, gather_patch_blocks(): mine = lax.all_to_all(copies, 'x', 0, 0, tiled=False)  22.5 us
    all_to_all x1, waiting for transfers between devices, sum_patch_blocks(): received = lax.all_to_all(pair, 'x', 0, 0, tiled=False)  18.7 us
    all_gather x1, waiting for transfers between devices, gather_columns(): along_yz = lax.all_gather(along_z, 'y', axis=1, tiled=True)  13.2 us
    ppermute x2, starting transfers between devices, swap_cores(): return lax.ppermute(block, 'c', [(0, 1), (1, 0)])  10.4 us
    all_to_all x1, starting transfers between devices, gather_patch_blocks(): mine = lax.all_to_all(copies, 'x', 0, 0, tiled=False)  6.48 us
    all_to_all x1, starting transfers between devices, sum_patch_blocks(): received = lax.all_to_all(pair, 'x', 0, 0, tiled=False)  6.39 us
    another operation x2, other arithmetic, gather_patch_blocks(): jnp.stack([jnp.where(first, mine, other), jnp.where(first, other, mine)],...  4.91 us
  transfers between devices with their start and end apart: 5, of which 3 were waited for; matrix products, arithmetic and copies ran while one was open for 15% of the time, Pallas kernels for 0%

profile of v4, /device:TPU:1, one launch (start us, length us, event | category | flops | bytes accessed | tf_op | source)
XLA Modules:
  0.0 156.1 jit_solution(10951910996104827004)
XLA Ops:
  7.2 0.0 copy-start.3
  7.2 0.0 all-gather.2.cloned.1.call-start
  7.2 34.6 %all_gather.6 = bf16[384,512]{0,1:T(8,128)(2,1)} all-gather(bf16[384,64]{0,1:T(8,128)(2,1)} %param.8), channel_id=1, replica_groups=mesh['zh'=4,'y'=8,'x'=8,'c'=2,'zl'=2] {'zh','zl'}, dimensions={1}, use_global_device_ids=true | all-gather | bytes 442368 | tf_op jit(solution)/shard_map/all_gather | solution.py:70
  41.8 0.0 all-gather.2.cloned.1.call-update
  41.9 0.0 copy-start.5
  41.9 2.0 %broadcast_in_dim.5 = bf16[8,16,1,4096]{3,1,2,0:T(8,128)(2,1)} broadcast(bf16[16,4096]{1,0:T(8,128)(2,1)} %bitcast.100), dimensions={1,3} | broadcast | bytes 1179648 | tf_op jit(solution)/shard_map/broadcast_in_dim | solution.py:84
  43.9 6.5 %all-to-all-start.1 = ((bf16[8,16,1,4096]{3,1,2,0:T(8,128)(2,1)}), bf16[8,16,1,4096]{3,1,2,0:T(8,128)(2,1)}, u32[]{:S(2)}, u32[]{:S(2)}) async-start(bf16[8,16,1,4096]{3,1,2,0:T(8,128)(2,1)} %broadcast_in_dim.5), calls=%async_computation.1 | async-start | bytes 2097152 | tf_op jit(solution)/shard_map/all_to_all | solution.py:85
  50.4 0.0 copy-done.3
  50.4 0.1 copy.60
  50.6 0.0 copy-done.4
  50.6 0.1 copy.61
  50.7 0.0 copy-done.5
  50.7 0.1 copy.64
  50.9 0.0 copy-start.6
  50.9 1.4 fusion.10
  52.2 22.5 %all-to-all-done.1 = bf16[8,16,1,4096]{3,1,2,0:T(8,128)(2,1)} async-done(((bf16[8,16,1,4096]{3,1,2,0:T(8,128)(2,1)}), bf16[8,16,1,4096]{3,1,2,0:T(8,128)(2,1)}, u32[]{:S(2)}, u32[]{:S(2)}) %all-to-all-start.1) | async-done | bytes 1048608 | tf_op jit(solution)/shard_map/all_to_all | solution.py:85
  74.7 7.4 %collective-permute-start.1 = (bf16[8,16,1,4096]{3,1,0,2:T(8,128)(2,1)}, bf16[8,16,1,4096]{3,1,0,2:T(8,128)(2,1)}, u32[]{:S(2)}, u32[]{:S(2)}) collective-permute-start(bf16[8,16,1,4096]{3,1,0,2:T(8,128)(2,1)} %bitcast.15), channel_id=1, source_target_pairs={{0,2},{2,0},{1,3},{3,1},{4,6},{6,4},{5,7},{7,5},{8,10},{10,8},{9,1... | collective-permute-start | bytes 3145736 | tf_op jit(solution)/shard_map/ppermute | solution.py:79
  82.1 1.3 convolution_convert_fusion.1
  83.4 0.0 copy-done.6
  83.4 13.2 %all-gather.2.cloned.1.call-done = bf16[384,4096]{0,1:T(8,128)(2,1)} async-done(((bf16[384,512]{0,1:T(8,128)(2,1)}), bf16[384,4096]{0,1:T(8,128)(2,1)}) %all-gather.2.cloned.1.call-update) | async-done | bytes 3145744 | tf_op jit(solution)/shard_map/all_gather | solution.py:71
  96.7 2.3 %copy.66 = bf16[384,4,8,2,64]{0,4,3,2,1:T(8,128)(2,1)S(1)} copy(bf16[384,4,8,2,64]{0,4,3,1,2:T(8,128)(2,1)} %bitcast.82) | data formatting | bytes 6291456 | tf_op jit(solution)/shard_map/transpose | solution.py:75
  99.0 0.0 copy-done.7
  99.0 1.3 convolution_convert_fusion
  100.3 0.0 copy-start
  100.3 1.3 copy-done
  101.6 1.1 dynamic-slice_bitcast_fusion
  102.7 3.0 %collective-permute-start = (bf16[8,16,1,4096]{3,1,2,0:T(8,128)(2,1)}, bf16[8,16,1,4096]{3,1,2,0:T(8,128)(2,1)}, u32[]{:S(2)}, u32[]{:S(2)}) collective-permute-start(bf16[8,16,1,4096]{3,1,2,0:T(8,128)(2,1)} %dynamic-slice_bitcast_fusion), channel_id=1, source_target_pairs={{0,2},{2,0},{1,3},{3,1},{4,6},{6,4},{5,7},{7,5},{8,10},{10,8},{9,1... | collective-permute-start | bytes 3145736 | tf_op jit(solution)/shard_map/ppermute | solution.py:79
  105.7 0.0 copy-start.1
  105.7 0.0 collective-permute-done.1
  105.8 3.2 %select_bitcast_fusion.1 = (bf16[8,1,16,1,4096]{4,2,0,3,1:T(8,128)(2,1)}, bf16[8,1,16,1,4096]{4,2,0,3,1:T(8,128)(2,1)}) fusion(bf16[8,16,1,4096]{3,1,0,2:T(8,128)(2,1)} %collective-permute-done.1, pred[]{:T(512)S(6)} %eq.3, bf16[8,16,1,4096]{3,1,2,0:T(8,128)(2,1)} %all-to-all-done.1), kind=kLoop, calls=%fused_computation.14 | loop fusion | flops 1048576 | bytes 4194305 | tf_op jit(solution)/shard_map/stack | solution.py:88
  108.9 0.0 collective-permute-done
  108.9 0.0 copy-done.1
  108.9 2.4 %fusion.1 = bf16[8,16,1,4096]{3,1,2,0:T(8,128)(2,1)} fusion(bf16[8,16,1,4096]{3,1,2,0:T(8,128)(2,1)} %collective-permute-done, bf16[8,2,16,1,4096]{4,2,1,0,3:T(8,128)(2,1)S(1)} %bitcast.81, s32[]{:T(128)S(6)} %select_n.19), kind=kLoop, calls=%fused_computation.4 | loop fusion | flops 2097152 | bytes 3145732 | tf_op jit(solution)/shard_map/convert_element_type | solution.py:98
  111.4 6.4 %all-to-all-start = ((bf16[8,16,1,4096]{3,1,2,0:T(8,128)(2,1)}), bf16[8,16,1,4096]{3,1,2,0:T(8,128)(2,1)}, u32[]{:S(2)}, u32[]{:S(2)}) async-start(bf16[8,16,1,4096]{3,1,2,0:T(8,128)(2,1)} %fusion.1), calls=%async_computation | async-start | bytes 2097152 | tf_op jit(solution)/shard_map/all_to_all | solution.py:99
  117.8 1.7 %pad_maximum_fusion = bf16[8,2,16,1,4096]{4,2,0,3,1:T(8,128)(2,1)S(1)} fusion(bf16[8,1,16,1,4096]{4,2,0,3,1:T(8,128)(2,1)} %get-tuple-element.21, bf16[8,1,16,1,4096]{4,2,0,3,1:T(8,128)(2,1)} %get-tuple-element.20), kind=kLoop, calls=%fused_computation.2 | loop fusion | flops 1048576 | bytes 4194304 | tf_op jit(solution)/shard_map/stack | solution.py:88
  119.5 0.2 copy.71
  119.7 2.0 %fusion.4 = bf16[1,256,384]{2,1,0:T(8,128)(2,1)} fusion(bf16[256,4096]{1,0:T(8,128)(2,1)S(1)} %bitcast.83, bf16[384,4096]{0,1:T(8,128)(2,1)S(1)} %bitcast.79), kind=kOutput, calls=%fused_computation.12 | convolution fusion | flops 805404672 | bytes 5439488 | tf_op jit(solution)/shard_map/qfd,cd->fqc/dot_general | solution.py:110
  121.7 1.1 copy.72
  122.8 1.6 %multiply_reduce_fusion = (f32[3,256]{1,0:T(4,128)S(1)}, f32[3,256,256]{1,2,0:T(8,128)S(1)}) fusion(f32[3,256,256]{1,2,0:T(8,128)} %get-tuple-element.23, f32[3,256]{1,0:T(4,128)S(1)} %get-tuple-element.22, bf16[256,3,128]{0,2,1:T(8,128)(2,1)S(1)} %bitcast.97, bf16[256,3,128]{0,2,1:T(8,128)(2,1)} %bitcast.96), kind=kOutput, calls=%fused_computation.17 | convolution fusion | flops 50920704 | bytes 1972224 | tf_op jit(solution)/shard_map/fqhd,fkhd->fhqk/dot_general | solution.py:48
  124.4 0.1 multiply_convert_fusion
  124.5 0.3 convolution_multiply_fusion.2
  124.8 0.9 copy.79
  125.8 0.2 convolution_multiply_fusion.1
  126.0 0.9 copy.78
  126.9 0.6 fusion.5
  127.5 0.9 copy.80
  128.4 18.7 %all-to-all-done = bf16[8,16,1,4096]{3,1,2,0:T(8,128)(2,1)} async-done(((bf16[8,16,1,4096]{3,1,2,0:T(8,128)(2,1)}), bf16[8,16,1,4096]{3,1,2,0:T(8,128)(2,1)}, u32[]{:S(2)}, u32[]{:S(2)}) %all-to-all-start) | async-done | bytes 1048608 | tf_op jit(solution)/shard_map/all_to_all | solution.py:99
  147.2 2.1 %reduce_sum.33 = bf16[16,4096]{1,0:T(8,128)(2,1)} reduce(bf16[8,16,1,4096]{3,1,2,0:T(8,128)(2,1)} %all-to-all-done, bf16[]{:T(256)} %constant.26.clone.1), dimensions={0,2}, to_apply=%region_2.3 | reduce | flops 458752 | bytes 1179650 | tf_op jit(solution)/shard_map/reduce_sum | solution.py:100
  (4 shorter events, 0.0 us)
Async XLA Ops:
  7.2 43.2 %copy-start.3 = (bf16[1,256,384]{2,1,0:T(8,128)(2,1)S(1)}, bf16[1,256,384]{2,1,0:T(8,128)(2,1)}, u32[]{:S(2)}) copy-start(bf16[1,256,384]{2,1,0:T(8,128)(2,1)} %param.5) | copy-start | bytes 589828
  7.2 89.5 %all-gather.2.cloned.1.call-start = ((), (), s32[]{:S(2)}) async-start(), calls=%async_computation.2 | async-start | bytes 3538944 | tf_op jit(solution)/shard_map/all_gather | solution.py:71
  41.8 8.7 %copy-start.4 = (bf16[1,256,384]{2,1,0:T(8,128)(2,1)S(1)}, bf16[1,256,384]{2,1,0:T(8,128)(2,1)}, u32[]{:S(2)}) copy-start(bf16[1,256,384]{2,1,0:T(8,128)(2,1)} %param.6) | copy-start | bytes 589828
  41.9 8.9 %copy-start.5 = (bf16[1,256,384]{2,1,0:T(8,128)(2,1)S(1)}, bf16[1,256,384]{2,1,0:T(8,128)(2,1)}, u32[]{:S(2)}) copy-start(bf16[1,256,384]{2,1,0:T(8,128)(2,1)} %param.7) | copy-start | bytes 589828
  43.9 30.8 %all-to-all-start.1 = ((bf16[8,16,1,4096]{3,1,2,0:T(8,128)(2,1)}), bf16[8,16,1,4096]{3,1,2,0:T(8,128)(2,1)}, u32[]{:S(2)}, u32[]{:S(2)}) async-start(bf16[8,16,1,4096]{3,1,2,0:T(8,128)(2,1)} %broadcast_in_dim.5), calls=%async_computation.1 | async-start | bytes 2097152 | tf_op jit(solution)/shard_map/all_to_all | solution.py:85
  50.9 32.6 %copy-start.6 = (bf16[1,256,384]{1,2,0:T(8,128)(2,1)}, bf16[1,256,384]{1,2,0:T(8,128)(2,1)S(1)}, u32[]{:S(2)}) copy-start(bf16[1,256,384]{1,2,0:T(8,128)(2,1)S(1)} %copy.64) | copy-start | bytes 589828
  74.7 31.0 %collective-permute-start.1 = (bf16[8,16,1,4096]{3,1,0,2:T(8,128)(2,1)}, bf16[8,16,1,4096]{3,1,0,2:T(8,128)(2,1)}, u32[]{:S(2)}, u32[]{:S(2)}) collective-permute-start(bf16[8,16,1,4096]{3,1,0,2:T(8,128)(2,1)} %bitcast.15), channel_id=1, source_target_pairs={{0,2},{2,0},{1,3},{3,1},{4,6},{6,4},{5,7},{7,5},{8,10},{10,8},{9,1... | collective-permute-start | bytes 3145736 | tf_op jit(solution)/shard_map/ppermute | solution.py:79
  96.7 2.3 %copy-start.7 = (bf16[3,256,128]{1,2,0:T(8,128)(2,1)S(1)}, bf16[3,256,128]{1,2,0:T(8,128)(2,1)}, u32[]{:S(2)}) copy-start(bf16[3,256,128]{1,2,0:T(8,128)(2,1)} %convolution_convert_fusion.1) | copy-start | bytes 589828
  100.3 1.3 copy-start
  102.7 6.2 %collective-permute-start = (bf16[8,16,1,4096]{3,1,2,0:T(8,128)(2,1)}, bf16[8,16,1,4096]{3,1,2,0:T(8,128)(2,1)}, u32[]{:S(2)}, u32[]{:S(2)}) collective-permute-start(bf16[8,16,1,4096]{3,1,2,0:T(8,128)(2,1)} %dynamic-slice_bitcast_fusion), channel_id=1, source_target_pairs={{0,2},{2,0},{1,3},{3,1},{4,6},{6,4},{5,7},{7,5},{8,10},{10,8},{9,1... | collective-permute-start | bytes 3145736 | tf_op jit(solution)/shard_map/ppermute | solution.py:79
  105.7 3.2 %copy-start.1 = (bf16[256,4096]{1,0:T(8,128)(2,1)S(1)}, bf16[256,4096]{1,0:T(8,128)(2,1)}, u32[]{:S(2)}) copy-start(bf16[256,4096]{1,0:T(8,128)(2,1)} %copy-done) | copy-start | bytes 6291460
  111.4 35.8 %all-to-all-start = ((bf16[8,16,1,4096]{3,1,2,0:T(8,128)(2,1)}), bf16[8,16,1,4096]{3,1,2,0:T(8,128)(2,1)}, u32[]{:S(2)}, u32[]{:S(2)}) async-start(bf16[8,16,1,4096]{3,1,2,0:T(8,128)(2,1)} %fusion.1), calls=%async_computation | async-start | bytes 2097152 | tf_op jit(solution)/shard_map/all_to_all | solution.py:99
  121.7 2.7 %copy-start.2 = (f32[3,256,256]{1,2,0:T(8,128)S(1)}, f32[3,256,256]{1,2,0:T(8,128)}, u32[]{:S(2)}) copy-start(f32[3,256,256]{1,2,0:T(8,128)} %get-tuple-element.23) | copy-start | bytes 2359300
Sparse Core Ops, SparseCore 0:
  42.0 54.6 all-gather.1

commit v5 on v4

--- a/solution.py
+++ b/solution.py
@@ -66,32 +66,26 @@
     )
 
 
-def gather_columns(projection):
-    along_z = lax.all_gather(projection, ("zh", "zl"), axis=1, tiled=True)
-    along_yz = lax.all_gather(along_z, "y", axis=1, tiled=True)
-    rows, width = projection.shape
-    ys, zhs, zls = (lax.axis_size(a) for a in ("y", "zh", "zl"))
-    blocks = along_yz.reshape(rows, ys, zhs, zls, width)
-    return blocks.transpose(0, 2, 1, 3, 4).reshape(rows, -1)
-
-
 def swap_cores(block):
     return lax.ppermute(block, "c", [(0, 1), (1, 0)])
 
 
-def gather_patch_blocks(upstream):
+def gather_by_all_to_all(block, axis):
+    count = lax.axis_size(axis)
+    copies = jnp.broadcast_to(block[None], (count,) + block.shape)
+    return lax.all_to_all(copies, axis, 0, 0, tiled=False)
+
+
+def gather_patch_blocks(pieces):
     chips = lax.axis_size("x")
-    copies = jnp.broadcast_to(upstream[None], (chips,) + upstream.shape)
-    mine = lax.all_to_all(copies, "x", 0, 0, tiled=False)
+    mine = gather_by_all_to_all(pieces, "x")
     other = swap_cores(mine)
     first = lax.axis_index("c") == 0
     both = jnp.stack([jnp.where(first, mine, other), jnp.where(first, other, mine)], axis=1)
-    return both.reshape(chips * 2 * upstream.shape[0], *upstream.shape[1:])
+    return both.reshape(chips * 2 * pieces.shape[0], *pieces.shape[1:])
 
 
-def sum_patch_blocks(partial):
-    chips = lax.axis_size("x")
-    blocks = partial.reshape(chips, 2, partial.shape[0] // (2 * chips), *partial.shape[1:])
+def sum_patch_blocks(blocks):
     core = lax.axis_index("c")
     keep = lax.dynamic_index_in_dim(blocks, core, axis=1, keepdims=False)
     send = lax.dynamic_index_in_dim(blocks, 1 - core, axis=1, keepdims=False)
@@ -101,20 +95,35 @@
 
 
 def on_device(queries, key_rows, value_rows, projection, upstream):
-    head_count = HEADS // (lax.axis_size("x") * lax.axis_size("c"))
+    chips, ys = lax.axis_size("x"), lax.axis_size("y")
+    zhs, zls = lax.axis_size("zh"), lax.axis_size("zl")
+    head_count = HEADS // (chips * 2)
     soft = soft_weights(queries, key_rows, head_count)
     attended = attend_values(soft, value_rows, head_count)
-    ordered = attended.transpose(1, 0, 2)
-    grad_full = gather_patch_blocks(upstream)
-    columns = gather_columns(projection)
-    grad_attended = jnp.einsum(
-        "qfd,cd->fqc", grad_full, columns, preferred_element_type=jnp.float32
+    patches, width = attended.shape[1], attended.shape[2]
+    block = patches // (chips * 2)
+    columns = lax.all_gather(projection, ("zh", "zl"), axis=1, tiled=True)
+    span = columns.shape[1]
+    group = gather_by_all_to_all(attended[0], "y")
+    tokens = group.reshape(ys, chips, 2, block, width)
+    partial = jnp.einsum(
+        "gxcpf,fd->xcgpd", tokens, columns, preferred_element_type=jnp.float32
+    ).astype(jnp.bfloat16)
+    summed = sum_patch_blocks(partial)
+    own = lax.all_to_all(summed, "y", 0, 0, tiled=False)
+    projected = (
+        own.reshape(ys, block, zhs, zls, span // (zhs * zls))
+        .transpose(1, 2, 0, 3, 4)
+        .reshape(block, 1, -1)
     )
-    partial = jnp.einsum(
-        "qfc,cd->qfd", ordered, columns, preferred_element_type=jnp.float32
+    pieces = upstream[:, 0].reshape(block, zhs, ys, zls, -1).transpose(2, 0, 1, 3, 4)
+    pieces = lax.all_to_all(pieces.reshape(ys, block, span), "y", 0, 0, tiled=False)
+    grad_full = gather_patch_blocks(pieces.transpose(1, 0, 2))
+    grad_partial = jnp.einsum(
+        "qgd,cd->gqc", grad_full, columns, preferred_element_type=jnp.float32
     ).astype(jnp.bfloat16)
-    projected = sum_patch_blocks(partial)
-    grad_rounded = grad_attended.astype(jnp.bfloat16)
+    grad_parts = lax.all_to_all(grad_partial, "y", 0, 0, tiled=False)
+    grad_rounded = grad_parts.astype(jnp.float32).sum(axis=0).astype(jnp.bfloat16)[None]
     grad_q, grad_k, grad_v = backward_heads(
         soft, queries, key_rows, value_rows, grad_rounded, head_count
     )

time: 157 us -> 213 us (1.36)
  blocking collectives: 34.6 us -> 65.1 us
  starting transfers between devices: 23.3 us -> 48.8 us
  waiting for transfers between devices: 54.5 us -> 71 us
  between operations: 14.2 us -> 0.92 us
  other arithmetic: 9.53 us -> 4.4 us
    all_to_all x0 -> x1, blocking collectives: none -> 31.8 us  [gather_by_all_to_all(): return lax.all_to_all(copies, axis, 0, 0, tiled=False)]
    all_to_all x1 -> x4, starting transfers between devices: 6.48 us -> 29.8 us  [the longest x1 14.6 us: gather_by_all_to_all(): return lax.all_to_all(copies, axis, 0, 0, tiled=False)]
    all_to_all x1 -> x4, waiting for transfers between devices: 22.5 us -> 45.3 us  [the longest x1 37.3 us: on_device(): grad_parts = lax.all_to_all(grad_partial, 'y', 0, 0, tiled=False)]
    all_gather x1 -> x0, waiting for transfers between devices: 13.2 us -> none  [gather_columns(): along_yz = lax.all_gather(along_z, 'y', axis=1, tiled=True)]
    all_to_all x1, waiting for transfers between devices: 18.7 us -> 25 us  [sum_patch_blocks(): received = lax.all_to_all(pair, 'x', 0, 0, tiled=False)]
    another operation x2, other arithmetic: 4.91 us -> 1.56 us  [gather_patch_blocks(): jnp.stack([jnp.where(first, mine, other), jnp.where(first, other, mine)],...]
    unnamed x22 -> x26, local copies, waits for them, and re-layouts: 4.55 us -> 4.67 us
  transfers between devices with their start and end apart: 5 -> 7, of which waited for: 3 -> 5; matrix products, arithmetic and copies ran while one was open for 15% -> 9% of each run, Pallas kernels for 0% -> 0%
where the time goes in v5:
time: 213 us; the launch traced here: 211 us
  waiting for transfers between devices  71 us (33%)
  blocking collectives  65.1 us (31%)
  starting transfers between devices  48.8 us (23%)
  local copies, waits for them, and re-layouts  12.3 us (6%)
  matrix products  8.47 us (4%)
  other arithmetic  4.4 us (2%)
    all_to_all x1, waiting for transfers between devices, on_device(): grad_parts = lax.all_to_all(grad_partial, 'y', 0, 0, tiled=False)  37.3 us
    all_gather x1, blocking collectives, on_device(): columns = lax.all_gather(projection, ('zh', 'zl'), axis=1, tiled=True)  33.3 us
    all_to_all x1, blocking collectives, gather_by_all_to_all(): return lax.all_to_all(copies, axis, 0, 0, tiled=False)  31.8 us
    all_to_all x1, waiting for transfers between devices, sum_patch_blocks(): received = lax.all_to_all(pair, 'x', 0, 0, tiled=False)  25 us
    all_to_all x1, starting transfers between devices, gather_by_all_to_all(): return lax.all_to_all(copies, axis, 0, 0, tiled=False)  14.6 us
    ppermute x2, starting transfers between devices, swap_cores(): return lax.ppermute(block, 'c', [(0, 1), (1, 0)])  12.3 us
    all_to_all x1, starting transfers between devices, on_device(): lax.all_to_all(pieces.reshape(ys, block, span), 'y', 0, 0, tiled=False)  8.11 us
    all_to_all x1, starting transfers between devices, sum_patch_blocks(): received = lax.all_to_all(pair, 'x', 0, 0, tiled=False)  6.66 us
  transfers between devices with their start and end apart: 7, of which 5 were waited for; matrix products, arithmetic and copies ran while one was open for 9% of the time, Pallas kernels for 0%

profile of v5, /device:TPU:1, one launch (start us, length us, event | category | flops | bytes accessed | tf_op | source)
XLA Modules:
  0.0 211.0 jit_solution(13939815184477941616)
XLA Ops:
  0.7 1.2 reshape_squeeze.3
  1.9 0.2 copy.116
  2.1 0.9 reshape.115
  2.9 8.1 %all-to-all-start.3 = ((bf16[8,16,512]{2,1,0:T(8,128)(2,1)}), bf16[8,16,512]{2,1,0:T(8,128)(2,1)S(1)}, u32[]{:S(2)}, u32[]{:S(2)}) async-start(bf16[8,16,512]{2,1,0:T(8,128)(2,1)} %reshape.115), calls=%async_computation.3 | async-start | bytes 262144 | tf_op jit(solution)/shard_map/all_to_all | solution.py:120
  11.0 1.1 copy.84
  12.1 0.1 copy.85
  12.3 0.1 copy.88
  12.5 1.3 fusion.12
  13.8 0.6 convolution_convert_fusion.2
  14.4 0.2 copy.90
  14.6 4.4 %all-to-all-done.3 = bf16[8,16,512]{2,1,0:T(8,128)(2,1)S(1)} async-done(((bf16[8,16,512]{2,1,0:T(8,128)(2,1)}), bf16[8,16,512]{2,1,0:T(8,128)(2,1)S(1)}, u32[]{:S(2)}, u32[]{:S(2)}) %all-to-all-start.3) | async-done | bytes 131104 | tf_op jit(solution)/shard_map/all_to_all | solution.py:120
  19.0 0.1 broadcast_in_dim.7
  19.1 31.8 %all_to_all.30 = bf16[8,256,384]{2,1,0:T(8,128)(2,1)} all-to-all(bf16[8,256,384]{2,1,0:T(8,128)(2,1)S(1)} %broadcast_in_dim.7), channel_id=1, replica_groups=mesh['zh'=4,'y'=8,'x'=8,'c'=2,'zl'=2] {'y'}, dimensions={0} | all-to-all | bytes 3145728 | tf_op jit(solution)/shard_map/all_to_all | solution.py:76
  50.9 1.1 broadcast_in_dim.8
  52.0 14.6 %all-to-all-start.4 = ((bf16[8,16,8,512]{3,1,2,0:T(8,128)(2,1)}), bf16[8,16,8,512]{3,1,2,0:T(8,128)(2,1)S(1)}, u32[]{:S(2)}, u32[]{:S(2)}) async-start(bf16[8,16,8,512]{3,1,2,0:T(8,128)(2,1)} %broadcast_in_dim.8), calls=%async_computation.4 | async-start | bytes 2097152 | tf_op jit(solution)/shard_map/all_to_all | solution.py:76
  66.6 33.3 %all_gather.3 = bf16[384,512]{0,1:T(8,128)(2,1)S(1)} all-gather(bf16[384,64]{0,1:T(8,128)(2,1)S(1)} %copy-done.9), channel_id=1, replica_groups=mesh['zh'=4,'y'=8,'x'=8,'c'=2,'zl'=2] {'zh','zl'}, dimensions={1}, use_global_device_ids=true | all-gather | bytes 442368 | tf_op jit(solution)/shard_map/all_gather | solution.py:105
  99.9 2.7 %convolution_convert_fusion = bf16[8,8,2,16,512]{4,3,2,1,0:T(8,128)(2,1)S(1)} fusion(bf16[8,8,2,16,384]{4,3,2,1,0:T(8,128)(2,1)} %bitcast.82, bf16[384,512]{0,1:T(8,128)(2,1)S(1)} %all_gather.3), kind=kOutput, calls=%fused_computation.4 | convolution fusion | flops 806354944 | bytes 4063232 | tf_op jit(solution)/shard_map/gxcpf,fd->xcgpd/dot_general | solution.py:109
  102.6 1.1 dynamic-slice_bitcast_fusion
  103.7 10.4 %collective-permute-start = (bf16[8,8,16,512]{3,2,0,1:T(8,128)(2,1)}, bf16[8,8,16,512]{3,2,0,1:T(8,128)(2,1)}, u32[]{:S(2)}, u32[]{:S(2)}) collective-permute-start(bf16[8,8,16,512]{3,2,0,1:T(8,128)(2,1)} %dynamic-slice_bitcast_fusion), channel_id=1, source_target_pairs={{0,2},{2,0},{1,3},{3,1},{4,6},{6,4},{5,7},{7,5},{8,10},{10,8},{9,1... | collective-permute-start | bytes 3145736 | tf_op jit(solution)/shard_map/ppermute | solution.py:70
  114.2 1.9 collective-permute-start.1
  116.1 0.7 collective-permute-done
  116.8 1.6 fusion.1
  118.4 1.1 copy.92
  119.5 6.7 %all-to-all-start.1 = ((bf16[8,8,16,512]{3,2,1,0:T(8,128)(2,1)}), bf16[8,8,16,512]{3,2,1,0:T(8,128)(2,1)S(1)}, u32[]{:S(2)}, u32[]{:S(2)}) async-start(bf16[8,8,16,512]{3,2,1,0:T(8,128)(2,1)} %copy.92), calls=%async_computation.1 | async-start | bytes 2097152 | tf_op jit(solution)/shard_map/all_to_all | solution.py:93
  126.1 1.4 select_bitcast_fusion.1
  127.5 0.2 pad_maximum_fusion
  127.7 0.2 copy.95
  127.9 2.4 %fusion.2 = bf16[8,256,384]{2,1,0:T(8,128)(2,1)} fusion(bf16[256,8,512]{2,0,1:T(8,128)(2,1)S(1)} %bitcast.81, bf16[384,512]{0,1:T(8,128)(2,1)S(1)} %all_gather.3), kind=kOutput, calls=%fused_computation.6 | convolution fusion | flops 806092800 | bytes 4063232 | tf_op jit(solution)/shard_map/qgd,cd->gqc/dot_general | solution.py:122
  130.3 25.0 %all-to-all-done.1 = bf16[8,8,16,512]{3,2,1,0:T(8,128)(2,1)S(1)} async-done(((bf16[8,8,16,512]{3,2,1,0:T(8,128)(2,1)}), bf16[8,8,16,512]{3,2,1,0:T(8,128)(2,1)S(1)}, u32[]{:S(2)}, u32[]{:S(2)}) %all-to-all-start.1) | async-done | bytes 1048608 | tf_op jit(solution)/shard_map/all_to_all | solution.py:93
  155.4 3.6 %all-to-all-start.5 = ((bf16[8,256,384]{2,1,0:T(8,128)(2,1)}), bf16[8,256,384]{2,1,0:T(8,128)(2,1)S(1)}, u32[]{:S(2)}, u32[]{:S(2)}) async-start(bf16[8,256,384]{2,1,0:T(8,128)(2,1)} %fusion.2), calls=%async_computation.5 | async-start | bytes 3145728 | tf_op jit(solution)/shard_map/all_to_all | solution.py:125
  158.9 0.8 reduce_sum.43
  159.8 37.3 %all-to-all-done.5 = bf16[8,256,384]{2,1,0:T(8,128)(2,1)S(1)} async-done(((bf16[8,256,384]{2,1,0:T(8,128)(2,1)}), bf16[8,256,384]{2,1,0:T(8,128)(2,1)S(1)}, u32[]{:S(2)}, u32[]{:S(2)}) %all-to-all-start.5) | async-done | bytes 1572896 | tf_op jit(solution)/shard_map/all_to_all | solution.py:125
  197.1 3.6 %all-to-all-start.2 = ((bf16[8,16,512]{2,1,0:T(8,128)(2,1)}), bf16[8,16,512]{2,1,0:T(8,128)(2,1)S(1)}, u32[]{:S(2)}, u32[]{:S(2)}) async-start(bf16[8,16,512]{2,1,0:T(8,128)(2,1)} %reduce_sum.43), calls=%async_computation.2 | async-start | bytes 262144 | tf_op jit(solution)/shard_map/all_to_all | solution.py:113
  200.7 0.3 reduce_sum.44
  200.9 0.1 copy.96
  201.1 0.3 multiply_reduce_fusion
  201.4 0.1 multiply_convert_fusion
  201.6 0.5 copy-done.2
  202.0 0.3 convolution_multiply_fusion.2
  202.4 0.2 convolution_multiply_fusion.1
  202.6 0.9 copy.103
  203.5 0.9 copy.102
  204.4 0.6 fusion.7
  205.1 3.6 %all-to-all-done.2 = bf16[8,16,512]{2,1,0:T(8,128)(2,1)S(1)} async-done(((bf16[8,16,512]{2,1,0:T(8,128)(2,1)}), bf16[8,16,512]{2,1,0:T(8,128)(2,1)S(1)}, u32[]{:S(2)}, u32[]{:S(2)}) %all-to-all-start.2) | async-done | bytes 131104 | tf_op jit(solution)/shard_map/all_to_all | solution.py:113
  208.7 0.2 reshape.113
  208.9 0.2 copy.93
  209.1 0.9 reshape.114
  210.1 0.9 copy.104
  (21 shorter events, 0.1 us)
Async XLA Ops:
  0.6 11.5 %copy-start.5 = (bf16[1,256,384]{2,1,0:T(8,128)(2,1)S(1)}, bf16[1,256,384]{2,1,0:T(8,128)(2,1)}, u32[]{:S(2)}) copy-start(bf16[1,256,384]{2,1,0:T(8,128)(2,1)} %param.6) | copy-start | bytes 589828
  0.6 11.6 %copy-start.6 = (bf16[1,256,384]{2,1,0:T(8,128)(2,1)S(1)}, bf16[1,256,384]{2,1,0:T(8,128)(2,1)}, u32[]{:S(2)}) copy-start(bf16[1,256,384]{2,1,0:T(8,128)(2,1)} %param.7) | copy-start | bytes 589828
  2.9 16.0 %all-to-all-start.3 = ((bf16[8,16,512]{2,1,0:T(8,128)(2,1)}), bf16[8,16,512]{2,1,0:T(8,128)(2,1)S(1)}, u32[]{:S(2)}, u32[]{:S(2)}) async-start(bf16[8,16,512]{2,1,0:T(8,128)(2,1)} %reshape.115), calls=%async_computation.3 | async-start | bytes 262144 | tf_op jit(solution)/shard_map/all_to_all | solution.py:120
  12.1 2.3 %copy-start.1 = (bf16[1,256,384]{1,2,0:T(8,128)(2,1)}, bf16[1,256,384]{1,2,0:T(8,128)(2,1)S(1)}, u32[]{:S(2)}) copy-start(bf16[1,256,384]{1,2,0:T(8,128)(2,1)S(1)} %copy.84) | copy-start | bytes 589828
  12.3 2.1 %copy-start.3 = (bf16[1,256,384]{1,2,0:T(8,128)(2,1)}, bf16[1,256,384]{1,2,0:T(8,128)(2,1)S(1)}, u32[]{:S(2)}) copy-start(bf16[1,256,384]{1,2,0:T(8,128)(2,1)S(1)} %copy.85) | copy-start | bytes 589828
  12.5 2.0 copy-start.7
  50.9 15.7 %copy-start.9 = (bf16[384,64]{0,1:T(8,128)(2,1)S(1)}, bf16[384,64]{0,1:T(8,128)(2,1)}, u32[]{:S(2)}) copy-start(bf16[384,64]{0,1:T(8,128)(2,1)} %param.8) | copy-start | bytes 147460
  52.0 62.1 %all-to-all-start.4 = ((bf16[8,16,8,512]{3,1,2,0:T(8,128)(2,1)}), bf16[8,16,8,512]{3,1,2,0:T(8,128)(2,1)S(1)}, u32[]{:S(2)}, u32[]{:S(2)}) async-start(bf16[8,16,8,512]{3,1,2,0:T(8,128)(2,1)} %broadcast_in_dim.8), calls=%async_computation.4 | async-start | bytes 2097152 | tf_op jit(solution)/shard_map/all_to_all | solution.py:76
  103.7 13.0 %collective-permute-start = (bf16[8,8,16,512]{3,2,0,1:T(8,128)(2,1)}, bf16[8,8,16,512]{3,2,0,1:T(8,128)(2,1)}, u32[]{:S(2)}, u32[]{:S(2)}) collective-permute-start(bf16[8,8,16,512]{3,2,0,1:T(8,128)(2,1)} %dynamic-slice_bitcast_fusion), channel_id=1, source_target_pairs={{0,2},{2,0},{1,3},{3,1},{4,6},{6,4},{5,7},{7,5},{8,10},{10,8},{9,1... | collective-permute-start | bytes 3145736 | tf_op jit(solution)/shard_map/ppermute | solution.py:70
  114.2 12.0 %collective-permute-start.1 = (bf16[8,16,8,512]{3,1,2,0:T(8,128)(2,1)S(1)}, bf16[8,16,8,512]{3,1,2,0:T(8,128)(2,1)}, u32[]{:S(2)}, u32[]{:S(2)}) collective-permute-start(bf16[8,16,8,512]{3,1,2,0:T(8,128)(2,1)S(1)} %all-to-all-done.4), channel_id=1, source_target_pairs={{0,2},{2,0},{1,3},{3,1},{4,6},{6,4},{5,7},{7,5},{8,10},{10,8},{9,1... | collective-permute-start | bytes 3145736 | tf_op jit(solution)/shard_map/ppermute | solution.py:70
  119.5 35.9 %all-to-all-start.1 = ((bf16[8,8,16,512]{3,2,1,0:T(8,128)(2,1)}), bf16[8,8,16,512]{3,2,1,0:T(8,128)(2,1)S(1)}, u32[]{:S(2)}, u32[]{:S(2)}) async-start(bf16[8,8,16,512]{3,2,1,0:T(8,128)(2,1)} %copy.92), calls=%async_computation.1 | async-start | bytes 2097152 | tf_op jit(solution)/shard_map/all_to_all | solution.py:93
  155.4 41.7 %all-to-all-start.5 = ((bf16[8,256,384]{2,1,0:T(8,128)(2,1)}), bf16[8,256,384]{2,1,0:T(8,128)(2,1)S(1)}, u32[]{:S(2)}, u32[]{:S(2)}) async-start(bf16[8,256,384]{2,1,0:T(8,128)(2,1)} %fusion.2), calls=%async_computation.5 | async-start | bytes 3145728 | tf_op jit(solution)/shard_map/all_to_all | solution.py:125
  158.9 42.1 %copy-start = (f32[3,256,256]{1,2,0:T(8,128)S(1)}, f32[3,256,256]{1,2,0:T(8,128)}, u32[]{:S(2)}) copy-start(f32[3,256,256]{1,2,0:T(8,128)} %get-tuple-element.27) | copy-start | bytes 2359300
  159.8 41.3 %copy-start.8 = (bf16[1,256,384]{1,2,0:T(8,128)(2,1)S(1)}, bf16[1,256,384]{1,2,0:T(8,128)(2,1)}, u32[]{:S(2)}) copy-start(bf16[1,256,384]{1,2,0:T(8,128)(2,1)} %copy-done.7) | copy-start | bytes 589828
  197.1 11.6 %all-to-all-start.2 = ((bf16[8,16,512]{2,1,0:T(8,128)(2,1)}), bf16[8,16,512]{2,1,0:T(8,128)(2,1)S(1)}, u32[]{:S(2)}, u32[]{:S(2)}) async-start(bf16[8,16,512]{2,1,0:T(8,128)(2,1)} %reduce_sum.43), calls=%async_computation.2 | async-start | bytes 262144 | tf_op jit(solution)/shard_map/all_to_all | solution.py:113
  201.1 0.9 copy-start.2
  201.4 1.0 copy-start.4

commit v6 on v5

--- a/solution.py
+++ b/solution.py
@@ -102,28 +102,29 @@
     attended = attend_values(soft, value_rows, head_count)
     patches, width = attended.shape[1], attended.shape[2]
     block = patches // (chips * 2)
-    columns = lax.all_gather(projection, ("zh", "zl"), axis=1, tiled=True)
+    columns = lax.all_gather(projection, "zh", axis=1, tiled=True)
+    columns = lax.all_gather(columns, "y", axis=1, tiled=True)
     span = columns.shape[1]
-    group = gather_by_all_to_all(attended[0], "y")
-    tokens = group.reshape(ys, chips, 2, block, width)
+    group = gather_by_all_to_all(attended[0], "zl")
+    tokens = group.reshape(zls, chips, 2, block, width)
     partial = jnp.einsum(
         "gxcpf,fd->xcgpd", tokens, columns, preferred_element_type=jnp.float32
     ).astype(jnp.bfloat16)
     summed = sum_patch_blocks(partial)
-    own = lax.all_to_all(summed, "y", 0, 0, tiled=False)
+    own = lax.all_to_all(summed, "zl", 0, 0, tiled=False)
     projected = (
-        own.reshape(ys, block, zhs, zls, span // (zhs * zls))
-        .transpose(1, 2, 0, 3, 4)
+        own.reshape(zls, block, ys, zhs, span // (ys * zhs))
+        .transpose(1, 3, 2, 0, 4)
         .reshape(block, 1, -1)
     )
-    pieces = upstream[:, 0].reshape(block, zhs, ys, zls, -1).transpose(2, 0, 1, 3, 4)
-    pieces = lax.all_to_all(pieces.reshape(ys, block, span), "y", 0, 0, tiled=False)
+    pieces = upstream[:, 0].reshape(block, zhs, ys, zls, -1).transpose(3, 0, 2, 1, 4)
+    pieces = lax.all_to_all(pieces.reshape(zls, block, span), "zl", 0, 0, tiled=False)
     grad_full = gather_patch_blocks(pieces.transpose(1, 0, 2))
     grad_partial = jnp.einsum(
         "qgd,cd->gqc", grad_full, columns, preferred_element_type=jnp.float32
-    ).astype(jnp.bfloat16)
-    grad_parts = lax.all_to_all(grad_partial, "y", 0, 0, tiled=False)
-    grad_rounded = grad_parts.astype(jnp.float32).sum(axis=0).astype(jnp.bfloat16)[None]
+    )
+    grad_parts = lax.all_to_all(grad_partial, "zl", 0, 0, tiled=False)
+    grad_rounded = grad_parts.sum(axis=0).astype(jnp.bfloat16)[None]
     grad_q, grad_k, grad_v = backward_heads(
         soft, queries, key_rows, value_rows, grad_rounded, head_count
     )

time: 213 us -> 164 us (0.77)
  blocking collectives: 65.1 us -> 30.4 us
  starting transfers between devices: 48.8 us -> 29.2 us
  between operations: 0.92 us -> 14.4 us
  waiting for transfers between devices: 71 us -> 66.2 us
    all_to_all x3 -> x2, waiting for transfers between devices: 45.3 us -> 9.67 us  [the longest x1 7.93 us: on_device(): grad_parts = lax.all_to_all(grad_partial, 'zl', 0, 0, tiled=False)]
    all_to_all x1 -> x2, waiting for transfers between devices: 0.01 us -> 30.7 us  [gather_by_all_to_all(): return lax.all_to_all(copies, axis, 0, 0, tiled=False)]
    all_to_all x1, blocking collectives: 31.8 us -> 7.11 us  [on_device(): lax.all_to_all(pieces.reshape(zls, block, span), 'zl', 0, 0, tiled=False)]
    all_gather x1, blocking collectives: 33.3 us -> 23.3 us  [on_device(): columns = lax.all_gather(projection, 'zh', axis=1, tiled=True)]
    all_to_all x3 -> x2, starting transfers between devices: 15.2 us -> 6.91 us  [the longest x1 3.53 us: on_device(): grad_parts = lax.all_to_all(grad_partial, 'zl', 0, 0, tiled=False)]
    all_to_all x1 -> x2, starting transfers between devices: 14.6 us -> 10.1 us  [gather_by_all_to_all(): return lax.all_to_all(copies, axis, 0, 0, tiled=False)]
    ppermute x2, starting transfers between devices: 12.3 us -> 8.5 us  [swap_cores(): return lax.ppermute(block, 'c', [(0, 1), (1, 0)])]
    all_to_all x1, starting transfers between devices: 6.66 us -> 3.56 us  [sum_patch_blocks(): received = lax.all_to_all(pair, 'x', 0, 0, tiled=False)]
  transfers between devices with their start and end apart: 7 -> 8, of which waited for: 5 -> 5; matrix products, arithmetic and copies ran while one was open for 9% -> 12% of each run, Pallas kernels for 0% -> 0%
where the time goes in v6:
time: 164 us
  waiting for transfers between devices  66.2 us (40%)
  blocking collectives  30.4 us (19%)
  starting transfers between devices  29.2 us (18%)
  between operations  14.4 us (9%)
  local copies, waits for them, and re-layouts  12.1 us (7%)
  matrix products  8.22 us (5%)
  other arithmetic  3.26 us (2%)
    all_to_all x2, waiting for transfers between devices, gather_by_all_to_all(): return lax.all_to_all(copies, axis, 0, 0, tiled=False)  30.7 us
    all_to_all x1, waiting for transfers between devices, sum_patch_blocks(): received = lax.all_to_all(pair, 'x', 0, 0, tiled=False)  25.8 us
    all_gather x1, blocking collectives, on_device(): columns = lax.all_gather(projection, 'zh', axis=1, tiled=True)  23.3 us
    all_to_all x2, starting transfers between devices, gather_by_all_to_all(): return lax.all_to_all(copies, axis, 0, 0, tiled=False)  10.1 us
    ppermute x2, starting transfers between devices, swap_cores(): return lax.ppermute(block, 'c', [(0, 1), (1, 0)])  8.5 us
    all_to_all x1, waiting for transfers between devices, on_device(): grad_parts = lax.all_to_all(grad_partial, 'zl', 0, 0, tiled=False)  7.93 us
    all_to_all x1, blocking collectives, on_device(): lax.all_to_all(pieces.reshape(zls, block, span), 'zl', 0, 0, tiled=False)  7.11 us
    unnamed x26, local copies, waits for them, and re-layouts  4.7 us
  transfers between devices with their start and end apart: 8, of which 5 were waited for; matrix products, arithmetic and copies ran while one was open for 12% of the time, Pallas kernels for 0%

profile of v6, /device:TPU:1, one launch (start us, length us, event | category | flops | bytes accessed | tf_op | source)
XLA Modules:
  0.0 163.7 jit_solution(14529034399345409803)
XLA Ops:
  7.2 23.3 %all_gather.6 = bf16[384,256]{0,1:T(8,128)(2,1)S(1)} all-gather(bf16[384,64]{0,1:T(8,128)(2,1)} %param.8), channel_id=1, replica_groups=mesh['zh'=4,'y'=8,'x'=8,'c'=2,'zl'=2] {'zh'}, dimensions={1}, use_global_device_ids=true | all-gather | bytes 245760 | tf_op jit(solution)/shard_map/all_gather | solution.py:105
  30.5 0.8 copy.95
  31.4 1.2 reshape_squeeze.3
  32.7 0.3 reshape.116
  33.0 7.1 %all_to_all.30 = bf16[2,16,2048]{2,1,0:T(8,128)(2,1)S(1)} all-to-all(bf16[2,16,2048]{2,1,0:T(8,128)(2,1)S(1)} %reshape.116), channel_id=1, replica_groups=mesh['zh'=4,'y'=8,'x'=8,'c'=2,'zl'=2] {'zl'}, dimensions={0} | all-to-all | bytes 262144 | tf_op jit(solution)/shard_map/all_to_all | solution.py:121
  40.1 1.1 broadcast_in_dim.8
  41.1 6.7 %all-to-all-start.4 = ((bf16[8,16,2,2048]{3,1,2,0:T(8,128)(2,1)}), bf16[8,16,2,2048]{3,1,2,0:T(8,128)(2,1)S(1)}, u32[]{:S(2)}, u32[]{:S(2)}) async-start(bf16[8,16,2,2048]{3,1,2,0:T(8,128)(2,1)} %broadcast_in_dim.8), calls=%async_computation.4 | async-start | bytes 2097152 | tf_op jit(solution)/shard_map/all_to_all | solution.py:76
  47.8 0.1 copy.88
  48.0 0.1 copy.89
  48.2 0.1 copy.92
  48.3 1.3 fusion.15
  49.7 24.0 %all-to-all-done.4 = bf16[8,16,2,2048]{3,1,2,0:T(8,128)(2,1)S(1)} async-done(((bf16[8,16,2,2048]{3,1,2,0:T(8,128)(2,1)}), bf16[8,16,2,2048]{3,1,2,0:T(8,128)(2,1)S(1)}, u32[]{:S(2)}, u32[]{:S(2)}) %all-to-all-start.4) | async-done | bytes 1048608 | tf_op jit(solution)/shard_map/all_to_all | solution.py:76
  73.7 5.8 %collective-permute-start.1 = (bf16[8,16,2,2048]{3,1,2,0:T(8,128)(2,1)S(1)}, bf16[8,16,2,2048]{3,1,2,0:T(8,128)(2,1)S(1)}, u32[]{:S(2)}, u32[]{:S(2)}) collective-permute-start(bf16[8,16,2,2048]{3,1,2,0:T(8,128)(2,1)S(1)} %all-to-all-done.4), channel_id=1, source_target_pairs={{0,2},{2,0},{1,3},{3,1},{4,6},{6,4},{5,7},{7,5},{8,10},{10,8},{9,1... | collective-permute-start | bytes 3145736 | tf_op jit(solution)/shard_map/ppermute | solution.py:70
  79.5 0.6 convolution_convert_fusion.1
  80.1 0.2 copy.94
  80.3 0.8 broadcast_in_dim.7
  81.0 3.5 %all-to-all-start = ((bf16[2,256,384]{2,1,0:T(8,128)(2,1)}), bf16[2,256,384]{2,1,0:T(8,128)(2,1)S(1)}, u32[]{:S(2)}, u32[]{:S(2)}) async-start(bf16[2,256,384]{2,1,0:T(8,128)(2,1)} %broadcast_in_dim.7), calls=%async_computation | async-start | bytes 786432 | tf_op jit(solution)/shard_map/all_to_all | solution.py:76
  84.5 6.7 %all-to-all-done = bf16[2,256,384]{2,1,0:T(8,128)(2,1)S(1)} async-done(((bf16[2,256,384]{2,1,0:T(8,128)(2,1)}), bf16[2,256,384]{2,1,0:T(8,128)(2,1)S(1)}, u32[]{:S(2)}, u32[]{:S(2)}) %all-to-all-start) | async-done | bytes 393248 | tf_op jit(solution)/shard_map/all_to_all | solution.py:76
  91.2 2.7 %convolution_convert_fusion = bf16[2,8,2,16,2048]{4,3,2,1,0:T(8,128)(2,1)S(1)} fusion(bf16[2,8,2,16,384]{4,3,2,1,0:T(8,128)(2,1)S(1)} %bitcast.97, bf16[384,2048]{1,0:T(8,128)(2,1)} %all-gather.2.cloned.1.call-done), kind=kOutput, calls=%fused_computation.1 | convolution fusion | flops 806354944 | bytes 4063232 | tf_op jit(solution)/shard_map/gxcpf,fd->xcgpd/dot_general | solution.py:110
  93.9 0.1 dynamic-slice_bitcast_fusion
  94.0 2.7 %collective-permute-start = (bf16[8,2,16,2048]{3,2,0,1:T(8,128)(2,1)S(1)}, bf16[8,2,16,2048]{3,2,0,1:T(8,128)(2,1)}, u32[]{:S(2)}, u32[]{:S(2)}) collective-permute-start(bf16[8,2,16,2048]{3,2,0,1:T(8,128)(2,1)S(1)} %dynamic-slice_bitcast_fusion), channel_id=1, source_target_pairs={{0,2},{2,0},{1,3},{3,1},{4,6},{6,4},{5,7},{7,5},{8,10},{10,8},{9,1... | collective-permute-start | bytes 3145736 | tf_op jit(solution)/shard_map/ppermute | solution.py:70
  96.8 0.1 select_bitcast_fusion.1
  96.9 0.2 pad_maximum_fusion
  97.1 0.2 copy.100
  97.4 1.2 copy-done.9
  98.5 2.1 %fusion.6 = f32[2,256,384]{2,1,0:T(8,128)} fusion(bf16[256,2,2048]{2,0,1:T(8,128)(2,1)S(1)} %bitcast.83, bf16[384,2048]{1,0:T(8,128)(2,1)S(1)} %copy-done.9), kind=kOutput, calls=%fused_computation.9 | convolution fusion | flops 805306368 | bytes 4456448 | tf_op jit(solution)/shard_map/qgd,cd->gqc/dot_general | solution.py:123
  100.7 3.5 %all-to-all-start.5 = ((f32[2,256,384]{2,1,0:T(8,128)}), f32[2,256,384]{2,1,0:T(8,128)S(1)}, u32[]{:S(2)}, u32[]{:S(2)}) async-start(f32[2,256,384]{2,1,0:T(8,128)} %fusion.6), calls=%async_computation.5 | async-start | bytes 1572864 | tf_op jit(solution)/shard_map/all_to_all | solution.py:126
  104.2 1.9 %fusion.1 = bf16[8,2,16,2048]{3,2,0,1:T(8,128)(2,1)S(1)} fusion(bf16[8,2,16,2048]{3,2,0,1:T(8,128)(2,1)} %collective-permute-done, bf16[2,8,2,16,2048]{4,3,2,1,0:T(8,128)(2,1)} %copy-done, s32[]{:T(128)S(6)} %select_n.19), kind=kLoop, calls=%fused_computation.4 | loop fusion | flops 2097152 | bytes 3145732 | tf_op jit(solution)/shard_map/convert_element_type | solution.py:92
  106.2 1.0 copy.97
  107.2 7.9 %all-to-all-done.5 = f32[2,256,384]{2,1,0:T(8,128)S(1)} async-done(((f32[2,256,384]{2,1,0:T(8,128)}), f32[2,256,384]{2,1,0:T(8,128)S(1)}, u32[]{:S(2)}, u32[]{:S(2)}) %all-to-all-start.5) | async-done | bytes 786464 | tf_op jit(solution)/shard_map/all_to_all | solution.py:126
  115.2 3.6 %all-to-all-start.1 = ((bf16[8,2,16,2048]{3,2,1,0:T(8,128)(2,1)}), bf16[8,2,16,2048]{3,2,1,0:T(8,128)(2,1)S(1)}, u32[]{:S(2)}, u32[]{:S(2)}) async-start(bf16[8,2,16,2048]{3,2,1,0:T(8,128)(2,1)} %copy.97), calls=%async_computation.1 | async-start | bytes 2097152 | tf_op jit(solution)/shard_map/all_to_all | solution.py:93
  118.8 0.1 copy.101
  119.0 0.3 multiply_reduce_fusion
  119.3 0.3 copy-done.7
  119.6 0.1 multiply_convert_fusion
  119.7 0.3 convolution_multiply_fusion.2
  120.0 0.9 copy.108
  120.9 0.2 convolution_multiply_fusion.1
  121.2 0.9 copy.107
  122.1 25.8 %all-to-all-done.1 = bf16[8,2,16,2048]{3,2,1,0:T(8,128)(2,1)S(1)} async-done(((bf16[8,2,16,2048]{3,2,1,0:T(8,128)(2,1)}), bf16[8,2,16,2048]{3,2,1,0:T(8,128)(2,1)S(1)}, u32[]{:S(2)}, u32[]{:S(2)}) %all-to-all-start.1) | async-done | bytes 1048608 | tf_op jit(solution)/shard_map/all_to_all | solution.py:93
  147.9 0.8 reduce_sum.40
  148.7 3.4 %all-to-all-start.2 = ((bf16[2,16,2048]{2,1,0:T(8,128)(2,1)}), bf16[2,16,2048]{2,1,0:T(8,128)(2,1)S(1)}, u32[]{:S(2)}, u32[]{:S(2)}) async-start(bf16[2,16,2048]{2,1,0:T(8,128)(2,1)} %reduce_sum.40), calls=%async_computation.2 | async-start | bytes 262144 | tf_op jit(solution)/shard_map/all_to_all | solution.py:114
  152.1 0.6 fusion.10
  152.7 0.9 copy.109
  153.6 1.7 %all-to-all-done.2 = bf16[2,16,2048]{2,1,0:T(8,128)(2,1)S(1)} async-done(((bf16[2,16,2048]{2,1,0:T(8,128)(2,1)}), bf16[2,16,2048]{2,1,0:T(8,128)(2,1)S(1)}, u32[]{:S(2)}, u32[]{:S(2)}) %all-to-all-start.2) | async-done | bytes 131104 | tf_op jit(solution)/shard_map/all_to_all | solution.py:114
  155.4 0.2 reshape.114
  155.6 0.3 copy.98
  155.9 0.9 reshape.115
  (25 shorter events, 0.3 us)
Async XLA Ops:
  7.2 84.1 %all-gather.2.cloned.1.call-start = ((), (), s32[]{:S(2)}) async-start(), calls=%async_computation.6 | async-start | bytes 1769472 | tf_op jit(solution)/shard_map/all_gather | solution.py:106
  32.7 15.2 %copy-start.2 = (bf16[1,256,384]{2,1,0:T(8,128)(2,1)S(1)}, bf16[1,256,384]{2,1,0:T(8,128)(2,1)}, u32[]{:S(2)}) copy-start(bf16[1,256,384]{2,1,0:T(8,128)(2,1)} %param.5) | copy-start | bytes 589828
  32.7 15.3 %copy-start.3 = (bf16[1,256,384]{2,1,0:T(8,128)(2,1)S(1)}, bf16[1,256,384]{2,1,0:T(8,128)(2,1)}, u32[]{:S(2)}) copy-start(bf16[1,256,384]{2,1,0:T(8,128)(2,1)} %param.6) | copy-start | bytes 589828
  40.1 8.1 %copy-start.4 = (bf16[1,256,384]{2,1,0:T(8,128)(2,1)S(1)}, bf16[1,256,384]{2,1,0:T(8,128)(2,1)}, u32[]{:S(2)}) copy-start(bf16[1,256,384]{2,1,0:T(8,128)(2,1)} %param.7) | copy-start | bytes 589828
  41.1 32.5 %all-to-all-start.4 = ((bf16[8,16,2,2048]{3,1,2,0:T(8,128)(2,1)}), bf16[8,16,2,2048]{3,1,2,0:T(8,128)(2,1)S(1)}, u32[]{:S(2)}, u32[]{:S(2)}) async-start(bf16[8,16,2,2048]{3,1,2,0:T(8,128)(2,1)} %broadcast_in_dim.8), calls=%async_computation.4 | async-start | bytes 2097152 | tf_op jit(solution)/shard_map/all_to_all | solution.py:76
  48.3 31.8 %copy-start.5 = (bf16[1,256,384]{1,2,0:T(8,128)(2,1)}, bf16[1,256,384]{1,2,0:T(8,128)(2,1)S(1)}, u32[]{:S(2)}) copy-start(bf16[1,256,384]{1,2,0:T(8,128)(2,1)S(1)} %copy.92) | copy-start | bytes 589828
  73.7 23.1 %collective-permute-start.1 = (bf16[8,16,2,2048]{3,1,2,0:T(8,128)(2,1)S(1)}, bf16[8,16,2,2048]{3,1,2,0:T(8,128)(2,1)S(1)}, u32[]{:S(2)}, u32[]{:S(2)}) collective-permute-start(bf16[8,16,2,2048]{3,1,2,0:T(8,128)(2,1)S(1)} %all-to-all-done.4), channel_id=1, source_target_pairs={{0,2},{2,0},{1,3},{3,1},{4,6},{6,4},{5,7},{7,5},{8,10},{10,8},{9,1... | collective-permute-start | bytes 3145736 | tf_op jit(solution)/shard_map/ppermute | solution.py:70
  81.0 10.2 %all-to-all-start = ((bf16[2,256,384]{2,1,0:T(8,128)(2,1)}), bf16[2,256,384]{2,1,0:T(8,128)(2,1)S(1)}, u32[]{:S(2)}, u32[]{:S(2)}) async-start(bf16[2,256,384]{2,1,0:T(8,128)(2,1)} %broadcast_in_dim.7), calls=%async_computation | async-start | bytes 786432 | tf_op jit(solution)/shard_map/all_to_all | solution.py:76
  93.9 2.8 %copy-start = (bf16[2,8,2,16,2048]{4,3,2,1,0:T(8,128)(2,1)}, bf16[2,8,2,16,2048]{4,3,2,1,0:T(8,128)(2,1)S(1)}, u32[]{:S(2)}) copy-start(bf16[2,8,2,16,2048]{4,3,2,1,0:T(8,128)(2,1)S(1)} %convolution_convert_fusion) | copy-start | bytes 6291460
  94.0 10.2 %collective-permute-start = (bf16[8,2,16,2048]{3,2,0,1:T(8,128)(2,1)S(1)}, bf16[8,2,16,2048]{3,2,0,1:T(8,128)(2,1)}, u32[]{:S(2)}, u32[]{:S(2)}) collective-permute-start(bf16[8,2,16,2048]{3,2,0,1:T(8,128)(2,1)S(1)} %dynamic-slice_bitcast_fusion), channel_id=1, source_target_pairs={{0,2},{2,0},{1,3},{3,1},{4,6},{6,4},{5,7},{7,5},{8,10},{10,8},{9,1... | collective-permute-start | bytes 3145736 | tf_op jit(solution)/shard_map/ppermute | solution.py:70
  97.1 1.4 copy-start.9
  100.7 14.5 %all-to-all-start.5 = ((f32[2,256,384]{2,1,0:T(8,128)}), f32[2,256,384]{2,1,0:T(8,128)S(1)}, u32[]{:S(2)}, u32[]{:S(2)}) async-start(f32[2,256,384]{2,1,0:T(8,128)} %fusion.6), calls=%async_computation.5 | async-start | bytes 1572864 | tf_op jit(solution)/shard_map/all_to_all | solution.py:126
  107.2 11.7 %copy-start.1 = (f32[3,256,256]{1,2,0:T(8,128)S(1)}, f32[3,256,256]{1,2,0:T(8,128)}, u32[]{:S(2)}) copy-start(f32[3,256,256]{1,2,0:T(8,128)} %get-tuple-element.27) | copy-start | bytes 2359300
  107.2 11.7 %copy-start.6 = (bf16[1,256,384]{1,2,0:T(8,128)(2,1)S(1)}, bf16[1,256,384]{1,2,0:T(8,128)(2,1)}, u32[]{:S(2)}) copy-start(bf16[1,256,384]{1,2,0:T(8,128)(2,1)} %copy-done.5) | copy-start | bytes 589828
  115.2 32.7 %all-to-all-start.1 = ((bf16[8,2,16,2048]{3,2,1,0:T(8,128)(2,1)}), bf16[8,2,16,2048]{3,2,1,0:T(8,128)(2,1)S(1)}, u32[]{:S(2)}, u32[]{:S(2)}) async-start(bf16[8,2,16,2048]{3,2,1,0:T(8,128)(2,1)} %copy.97), calls=%async_computation.1 | async-start | bytes 2097152 | tf_op jit(solution)/shard_map/all_to_all | solution.py:93
  118.9 0.7 copy-start.7
  120.0 32.1 %copy-start.8 = (bf16[256,384]{0,1:T(8,128)(2,1)S(1)}, bf16[256,384]{0,1:T(8,128)(2,1)}, u32[]{:S(2)}) copy-start(bf16[256,384]{0,1:T(8,128)(2,1)} %copy-done.7) | copy-start | bytes 589828
  148.7 6.7 %all-to-all-start.2 = ((bf16[2,16,2048]{2,1,0:T(8,128)(2,1)}), bf16[2,16,2048]{2,1,0:T(8,128)(2,1)S(1)}, u32[]{:S(2)}, u32[]{:S(2)}) async-start(bf16[2,16,2048]{2,1,0:T(8,128)(2,1)} %reduce_sum.40), calls=%async_computation.2 | async-start | bytes 262144 | tf_op jit(solution)/shard_map/all_to_all | solution.py:114
Sparse Core Ops, SparseCore 0:
  31.5 48.4 all-gather.1

commit v7 on v6

--- a/solution.py
+++ b/solution.py
@@ -76,6 +76,22 @@
     return lax.all_to_all(copies, axis, 0, 0, tiled=False)
 
 
+def swap_pair(block):
+    return lax.ppermute(block, "zl", [(0, 1), (1, 0)])
+
+
+def in_pair_order(mine, other, axis=0):
+    first = lax.axis_index("zl") == 0
+    return jnp.stack([jnp.where(first, mine, other), jnp.where(first, other, mine)], axis=axis)
+
+
+def split_pair(blocks):
+    pair = lax.axis_index("zl")
+    keep = lax.dynamic_index_in_dim(blocks, pair, axis=0, keepdims=False)
+    send = lax.dynamic_index_in_dim(blocks, 1 - pair, axis=0, keepdims=False)
+    return keep, send
+
+
 def gather_patch_blocks(pieces):
     chips = lax.axis_size("x")
     mine = gather_by_all_to_all(pieces, "x")
@@ -105,26 +121,28 @@
     columns = lax.all_gather(projection, "zh", axis=1, tiled=True)
     columns = lax.all_gather(columns, "y", axis=1, tiled=True)
     span = columns.shape[1]
-    group = gather_by_all_to_all(attended[0], "zl")
+    group = in_pair_order(attended[0], swap_pair(attended[0]))
     tokens = group.reshape(zls, chips, 2, block, width)
     partial = jnp.einsum(
         "gxcpf,fd->xcgpd", tokens, columns, preferred_element_type=jnp.float32
     ).astype(jnp.bfloat16)
     summed = sum_patch_blocks(partial)
-    own = lax.all_to_all(summed, "zl", 0, 0, tiled=False)
+    keep, send = split_pair(summed)
+    own = in_pair_order(keep, swap_pair(send))
     projected = (
         own.reshape(zls, block, ys, zhs, span // (ys * zhs))
         .transpose(1, 3, 2, 0, 4)
         .reshape(block, 1, -1)
     )
     pieces = upstream[:, 0].reshape(block, zhs, ys, zls, -1).transpose(3, 0, 2, 1, 4)
-    pieces = lax.all_to_all(pieces.reshape(zls, block, span), "zl", 0, 0, tiled=False)
+    keep, send = split_pair(pieces.reshape(zls, block, span))
+    pieces = in_pair_order(keep, swap_pair(send))
     grad_full = gather_patch_blocks(pieces.transpose(1, 0, 2))
     grad_partial = jnp.einsum(
         "qgd,cd->gqc", grad_full, columns, preferred_element_type=jnp.float32
     )
-    grad_parts = lax.all_to_all(grad_partial, "zl", 0, 0, tiled=False)
-    grad_rounded = grad_parts.sum(axis=0).astype(jnp.bfloat16)[None]
+    keep, send = split_pair(grad_partial)
+    grad_rounded = (keep + swap_pair(send)).astype(jnp.bfloat16)[None]
     grad_q, grad_k, grad_v = backward_heads(
         soft, queries, key_rows, value_rows, grad_rounded, head_count
     )

time: 164 us -> 153 us (0.933)
  waiting for transfers between devices: 66.2 us -> 50.5 us
  starting transfers between devices: 29.2 us -> 39.1 us
  blocking collectives: 30.4 us -> 21.8 us
    ppermute x0 -> x4, starting transfers between devices: none -> 15.3 us  [swap_pair(): return lax.ppermute(block, 'zl', [(0, 1), (1, 0)])]
    all_to_all x1, waiting for transfers between devices: 25.8 us -> 12.2 us  [sum_patch_blocks(): received = lax.all_to_all(pair, 'x', 0, 0, tiled=False)]
    all_to_all x2 -> x0, waiting for transfers between devices: 9.67 us -> none  [the longest x1 7.93 us: on_device(): grad_parts = lax.all_to_all(grad_partial, 'zl', 0, 0, tiled=False)]
    ppermute x0 -> x4, waiting for transfers between devices: none -> 9.27 us  [swap_pair(): return lax.ppermute(block, 'zl', [(0, 1), (1, 0)])]
    all_to_all x2 -> x1, waiting for transfers between devices: 30.7 us -> 22.4 us  [gather_by_all_to_all(): return lax.all_to_all(copies, axis, 0, 0, tiled=False)]
    all_to_all x1 -> x0, blocking collectives: 7.11 us -> none  [on_device(): lax.all_to_all(pieces.reshape(zls, block, span), 'zl', 0, 0, tiled=False)]
    all_to_all x2 -> x0, starting transfers between devices: 6.91 us -> none  [the longest x1 3.53 us: on_device(): grad_parts = lax.all_to_all(grad_partial, 'zl', 0, 0, tiled=False)]
    all_gather x1, waiting for transfers between devices: 0.01 us -> 6.63 us  [on_device(): columns = lax.all_gather(columns, 'y', axis=1, tiled=True)]
  transfers between devices with their start and end apart: 8 -> 9, of which waited for: 5 -> 4; matrix products, arithmetic and copies ran while one was open for 12% -> 13% of each run, Pallas kernels for 0% -> 0%
where the time goes in v7:
time: 153 us; the launch traced here: 152 us
  waiting for transfers between devices  50.5 us (33%)
  starting transfers between devices  39.1 us (26%)
  blocking collectives  21.8 us (14%)
  between operations  14.4 us (9%)
  local copies, waits for them, and re-layouts  13.7 us (9%)
  matrix products  8.97 us (6%)
  other arithmetic  3.82 us (2%)
    all_to_all x1, waiting for transfers between devices, gather_by_all_to_all(): return lax.all_to_all(copies, axis, 0, 0, tiled=False)  22.4 us
    all_gather x1, blocking collectives, on_device(): columns = lax.all_gather(projection, 'zh', axis=1, tiled=True)  21.8 us
    ppermute x4, starting transfers between devices, swap_pair(): return lax.ppermute(block, 'zl', [(0, 1), (1, 0)])  15.3 us
    all_to_all x1, waiting for transfers between devices, sum_patch_blocks(): received = lax.all_to_all(pair, 'x', 0, 0, tiled=False)  12.2 us
    ppermute x2, starting transfers between devices, swap_cores(): return lax.ppermute(block, 'c', [(0, 1), (1, 0)])  11.2 us
    ppermute x4, waiting for transfers between devices, swap_pair(): return lax.ppermute(block, 'zl', [(0, 1), (1, 0)])  9.27 us
    all_gather x1, waiting for transfers between devices, on_device(): columns = lax.all_gather(columns, 'y', axis=1, tiled=True)  6.63 us
    all_to_all x1, starting transfers between devices, gather_by_all_to_all(): return lax.all_to_all(copies, axis, 0, 0, tiled=False)  6.48 us
  transfers between devices with their start and end apart: 9, of which 4 were waited for; matrix products, arithmetic and copies ran while one was open for 13% of the time, Pallas kernels for 0%

profile of v7, /device:TPU:1, one launch (start us, length us, event | category | flops | bytes accessed | tf_op | source)
XLA Modules:
  0.0 152.3 jit_solution(9666938711950409108)
XLA Ops:
  7.2 1.2 reshape_squeeze.3
  8.4 0.1 copy.105
  8.5 0.3 reshape.120
  8.8 5.7 %collective-permute-start.3 = (bf16[16,2048]{1,0:T(8,128)(2,1)S(1)}, bf16[16,2048]{1,0:T(8,128)(2,1)S(1)}, u32[]{:S(2)}, u32[]{:S(2)}) collective-permute-start(bf16[16,2048]{1,0:T(8,128)(2,1)S(1)} %dynamic-slice_bitcast_fusion.2), channel_id=1, source_target_pairs={{0,1},{1,0},{2,3},{3,2},{4,5},{5,4},{6,7},{7,6},{8,9},{9,8},{10,11... | collective-permute-start | bytes 196616 | tf_op jit(solution)/shard_map/ppermute | solution.py:80
  14.5 21.8 %all_gather.6 = bf16[384,256]{0,1:T(8,128)(2,1)S(1)} all-gather(bf16[384,64]{0,1:T(8,128)(2,1)} %param.8), channel_id=1, replica_groups=mesh['zh'=4,'y'=8,'x'=8,'c'=2,'zl'=2] {'zh'}, dimensions={1}, use_global_device_ids=true | all-gather | bytes 245760 | tf_op jit(solution)/shard_map/all_gather | solution.py:121
  36.4 0.8 copy.79
  37.3 1.1 broadcast_in_dim.2
  38.4 6.5 %all-to-all-start.1 = ((bf16[8,16,2,2048]{3,1,2,0:T(8,128)(2,1)}), bf16[8,16,2,2048]{3,1,2,0:T(8,128)(2,1)S(1)}, u32[]{:S(2)}, u32[]{:S(2)}) async-start(bf16[8,16,2,2048]{3,1,2,0:T(8,128)(2,1)} %broadcast_in_dim.2), calls=%async_computation.1 | async-start | bytes 2097152 | tf_op jit(solution)/shard_map/all_to_all | solution.py:76
  44.9 0.1 copy.71
  45.0 0.1 copy.72
  45.2 0.1 copy.75
  45.4 1.3 fusion.19
  46.7 0.6 convolution_convert_fusion.1
  47.3 1.9 %collective-permute-start = (bf16[256,384]{0,1:T(8,128)(2,1)S(1)}, bf16[256,384]{0,1:T(8,128)(2,1)S(1)}, u32[]{:S(2)}, u32[]{:S(2)}) collective-permute-start(bf16[256,384]{0,1:T(8,128)(2,1)S(1)} %bitcast.126), channel_id=1, source_target_pairs={{0,1},{1,0},{2,3},{3,2},{4,5},{5,4},{6,7},{7,6},{8,9},{9,8},{10,11... | collective-permute-start | bytes 589832 | tf_op jit(solution)/shard_map/ppermute | solution.py:80
  49.2 22.4 %all-to-all-done.1 = bf16[8,16,2,2048]{3,1,2,0:T(8,128)(2,1)S(1)} async-done(((bf16[8,16,2,2048]{3,1,2,0:T(8,128)(2,1)}), bf16[8,16,2,2048]{3,1,2,0:T(8,128)(2,1)S(1)}, u32[]{:S(2)}, u32[]{:S(2)}) %all-to-all-start.1) | async-done | bytes 1048608 | tf_op jit(solution)/shard_map/all_to_all | solution.py:76
  71.6 4.9 %collective-permute-start.4 = (bf16[8,16,2,2048]{3,1,2,0:T(8,128)(2,1)S(1)}, bf16[8,16,2,2048]{3,1,2,0:T(8,128)(2,1)}, u32[]{:S(2)}, u32[]{:S(2)}) collective-permute-start(bf16[8,16,2,2048]{3,1,2,0:T(8,128)(2,1)S(1)} %all-to-all-done.1), channel_id=1, source_target_pairs={{0,2},{2,0},{1,3},{3,1},{4,6},{6,4},{5,7},{7,5},{8,10},{10,8},{9,1... | collective-permute-start | bytes 3145736 | tf_op jit(solution)/shard_map/ppermute | solution.py:70
  76.6 0.8 copy.77
  77.4 0.8 copy.78
  78.2 6.6 %all-gather.2.cloned.1.call-done = bf16[384,2048]{1,0:T(8,128)(2,1)} async-done(((bf16[384,256]{1,0:T(8,128)(2,1)}), bf16[384,2048]{1,0:T(8,128)(2,1)}) %all-gather.2.cloned.1.call-update) | async-done | bytes 1572880 | tf_op jit(solution)/shard_map/all_gather | solution.py:122
  84.8 2.9 %convolution_convert_fusion = bf16[2,8,2,16,2048]{4,3,2,1,0:T(8,128)(2,1)S(1)} fusion(bf16[384,2048]{1,0:T(8,128)(2,1)} %all-gather.2.cloned.1.call-done, bf16[1,8,2,16,384]{4,3,2,1,0:T(8,128)(2,1)} %bitcast.125, bf16[1,8,2,16,384]{4,3,2,1,0:T(8,128)(2,1)} %bitcast.124), kind=kOutput, calls=%fused_computation.1 | convolution fusion | flops 806551552 | bytes 4063232 | tf_op jit(solution)/shard_map/gxcpf,fd->xcgpd/dot_general | solution.py:126
  87.7 1.1 dynamic-slice_bitcast_fusion
  88.8 6.3 %collective-permute-start.1 = (bf16[8,2,16,2048]{3,2,0,1:T(8,128)(2,1)}, bf16[8,2,16,2048]{3,2,0,1:T(8,128)(2,1)}, u32[]{:S(2)}, u32[]{:S(2)}) collective-permute-start(bf16[8,2,16,2048]{3,2,0,1:T(8,128)(2,1)} %dynamic-slice_bitcast_fusion), channel_id=1, source_target_pairs={{0,2},{2,0},{1,3},{3,1},{4,6},{6,4},{5,7},{7,5},{8,10},{10,8},{9,1... | collective-permute-start | bytes 3145736 | tf_op jit(solution)/shard_map/ppermute | solution.py:70
  95.2 1.4 select_bitcast_fusion.1
  96.5 0.2 pad_maximum_fusion
  96.7 1.5 copy.84
  98.2 1.6 %fusion.1 = bf16[8,2,16,2048]{3,2,0,1:T(8,128)(2,1)S(1)} fusion(bf16[8,2,16,2048]{3,2,0,1:T(8,128)(2,1)} %collective-permute-done.1, bf16[2,8,2,16,2048]{4,3,2,1,0:T(8,128)(2,1)S(1)} %convolution_convert_fusion, s32[]{:T(128)S(6)} %select_n.67), kind=kLoop, calls=%fused_computation.4 | loop fusion | flops 2097152 | bytes 3145732 | tf_op jit(solution)/shard_map/convert_element_type | solution.py:108
  99.8 1.1 copy.81
  100.9 6.1 %all-to-all-start = ((bf16[8,2,16,2048]{3,2,1,0:T(8,128)(2,1)}), bf16[8,2,16,2048]{3,2,1,0:T(8,128)(2,1)S(1)}, u32[]{:S(2)}, u32[]{:S(2)}) async-start(bf16[8,2,16,2048]{3,2,1,0:T(8,128)(2,1)} %copy.81), calls=%async_computation | async-start | bytes 2097152 | tf_op jit(solution)/shard_map/all_to_all | solution.py:109
  107.0 2.7 %fusion.3 = f32[256,2,384]{2,0,1:T(8,128)S(1)} fusion(bf16[256,2,2048]{2,0,1:T(8,128)(2,1)S(1)} %bitcast.107, bf16[384,2048]{1,0:T(8,128)(2,1)} %all-gather.2.cloned.1.call-done), kind=kOutput, calls=%fused_computation.6 | convolution fusion | flops 805306368 | bytes 4456448 | tf_op jit(solution)/shard_map/qgd,cd->gqc/dot_general | solution.py:141
  109.8 3.9 %collective-permute-start.5 = (f32[256,384]{1,0:T(8,128)S(1)}, f32[256,384]{1,0:T(8,128)S(1)}, u32[]{:S(2)}, u32[]{:S(2)}) collective-permute-start(f32[256,384]{1,0:T(8,128)S(1)} %dynamic-slice_bitcast_fusion.1), channel_id=1, source_target_pairs={{0,1},{1,0},{2,3},{3,2},{4,5},{5,4},{6,7},{7,6},{8,9},{9,8},{10,11... | collective-permute-start | bytes 1179656 | tf_op jit(solution)/shard_map/ppermute | solution.py:80
  113.7 9.3 %collective-permute-done.5 = f32[256,384]{1,0:T(8,128)S(1)} collective-permute-done((f32[256,384]{1,0:T(8,128)S(1)}, f32[256,384]{1,0:T(8,128)S(1)}, u32[]{:S(2)}, u32[]{:S(2)}) %collective-permute-start.5) | collective-permute-done | bytes 393248 | tf_op jit(solution)/shard_map/ppermute | solution.py:80
  123.0 0.1 copy.85
  123.2 0.3 multiply_reduce_fusion
  123.5 0.1 multiply_convert_fusion
  123.6 0.3 convolution_multiply_fusion.2
  123.9 0.2 convolution_multiply_fusion.1
  124.1 12.2 %all-to-all-done = bf16[8,2,16,2048]{3,2,1,0:T(8,128)(2,1)S(1)} async-done(((bf16[8,2,16,2048]{3,2,1,0:T(8,128)(2,1)}), bf16[8,2,16,2048]{3,2,1,0:T(8,128)(2,1)S(1)}, u32[]{:S(2)}, u32[]{:S(2)}) %all-to-all-start) | async-done | bytes 1048608 | tf_op jit(solution)/shard_map/all_to_all | solution.py:109
  136.3 0.2 reduce_sum.31
  136.5 3.8 %collective-permute-start.2 = (bf16[16,2048]{1,0:T(8,128)(2,1)S(1)}, bf16[16,2048]{1,0:T(8,128)(2,1)S(1)}, u32[]{:S(2)}, u32[]{:S(2)}) collective-permute-start(bf16[16,2048]{1,0:T(8,128)(2,1)S(1)} %dynamic-slice_bitcast_fusion.3), channel_id=1, source_target_pairs={{0,1},{1,0},{2,3},{3,2},{4,5},{5,4},{6,7},{7,6},{8,9},{9,8},{10,11... | collective-permute-start | bytes 196616 | tf_op jit(solution)/shard_map/ppermute | solution.py:80
  140.3 0.6 fusion.11
  140.9 0.9 copy.93
  141.8 0.9 copy.92
  142.7 0.9 copy.91
  143.7 0.2 stack.39
  143.8 0.2 stack.40
  144.0 0.2 maximum_bitcast_fusion
  144.3 0.3 copy.82
  144.5 0.9 reshape.119
  (29 shorter events, 0.3 us)
Async XLA Ops:
  7.2 77.7 %all-gather.2.cloned.1.call-start = ((), (), s32[]{:S(2)}) async-start(), calls=%async_computation.2 | async-start | bytes 1769472 | tf_op jit(solution)/shard_map/all_gather | solution.py:122
  8.8 28.4 %collective-permute-start.3 = (bf16[16,2048]{1,0:T(8,128)(2,1)S(1)}, bf16[16,2048]{1,0:T(8,128)(2,1)S(1)}, u32[]{:S(2)}, u32[]{:S(2)}) collective-permute-start(bf16[16,2048]{1,0:T(8,128)(2,1)S(1)} %dynamic-slice_bitcast_fusion.2), channel_id=1, source_target_pairs={{0,1},{1,0},{2,3},{3,2},{4,5},{5,4},{6,7},{7,6},{8,9},{9,8},{10,11... | collective-permute-start | bytes 196616 | tf_op jit(solution)/shard_map/ppermute | solution.py:80
  37.2 7.7 %copy-start.2 = (bf16[1,256,384]{2,1,0:T(8,128)(2,1)S(1)}, bf16[1,256,384]{2,1,0:T(8,128)(2,1)}, u32[]{:S(2)}) copy-start(bf16[1,256,384]{2,1,0:T(8,128)(2,1)} %param.5) | copy-start | bytes 589828
  37.2 7.8 %copy-start.3 = (bf16[1,256,384]{2,1,0:T(8,128)(2,1)S(1)}, bf16[1,256,384]{2,1,0:T(8,128)(2,1)}, u32[]{:S(2)}) copy-start(bf16[1,256,384]{2,1,0:T(8,128)(2,1)} %param.6) | copy-start | bytes 589828
  37.3 7.9 %copy-start.4 = (bf16[1,256,384]{2,1,0:T(8,128)(2,1)S(1)}, bf16[1,256,384]{2,1,0:T(8,128)(2,1)}, u32[]{:S(2)}) copy-start(bf16[1,256,384]{2,1,0:T(8,128)(2,1)} %param.7) | copy-start | bytes 589828
  38.4 33.3 %all-to-all-start.1 = ((bf16[8,16,2,2048]{3,1,2,0:T(8,128)(2,1)}), bf16[8,16,2,2048]{3,1,2,0:T(8,128)(2,1)S(1)}, u32[]{:S(2)}, u32[]{:S(2)}) async-start(bf16[8,16,2,2048]{3,1,2,0:T(8,128)(2,1)} %broadcast_in_dim.2), calls=%async_computation.1 | async-start | bytes 2097152 | tf_op jit(solution)/shard_map/all_to_all | solution.py:76
  45.3 1.9 %copy-start.5 = (bf16[1,256,384]{1,2,0:T(8,128)(2,1)}, bf16[1,256,384]{1,2,0:T(8,128)(2,1)S(1)}, u32[]{:S(2)}) copy-start(bf16[1,256,384]{1,2,0:T(8,128)(2,1)S(1)} %copy.75) | copy-start | bytes 589828
  47.3 29.2 %collective-permute-start = (bf16[256,384]{0,1:T(8,128)(2,1)S(1)}, bf16[256,384]{0,1:T(8,128)(2,1)S(1)}, u32[]{:S(2)}, u32[]{:S(2)}) collective-permute-start(bf16[256,384]{0,1:T(8,128)(2,1)S(1)} %bitcast.126), channel_id=1, source_target_pairs={{0,1},{1,0},{2,3},{3,2},{4,5},{5,4},{6,7},{7,6},{8,9},{9,8},{10,11... | collective-permute-start | bytes 589832 | tf_op jit(solution)/shard_map/ppermute | solution.py:80
  71.6 23.5 %collective-permute-start.4 = (bf16[8,16,2,2048]{3,1,2,0:T(8,128)(2,1)S(1)}, bf16[8,16,2,2048]{3,1,2,0:T(8,128)(2,1)}, u32[]{:S(2)}, u32[]{:S(2)}) collective-permute-start(bf16[8,16,2,2048]{3,1,2,0:T(8,128)(2,1)S(1)} %all-to-all-done.1), channel_id=1, source_target_pairs={{0,2},{2,0},{1,3},{3,1},{4,6},{6,4},{5,7},{7,5},{8,10},{10,8},{9,1... | collective-permute-start | bytes 3145736 | tf_op jit(solution)/shard_map/ppermute | solution.py:70
  88.8 9.4 %collective-permute-start.1 = (bf16[8,2,16,2048]{3,2,0,1:T(8,128)(2,1)}, bf16[8,2,16,2048]{3,2,0,1:T(8,128)(2,1)}, u32[]{:S(2)}, u32[]{:S(2)}) collective-permute-start(bf16[8,2,16,2048]{3,2,0,1:T(8,128)(2,1)} %dynamic-slice_bitcast_fusion), channel_id=1, source_target_pairs={{0,2},{2,0},{1,3},{3,1},{4,6},{6,4},{5,7},{7,5},{8,10},{10,8},{9,1... | collective-permute-start | bytes 3145736 | tf_op jit(solution)/shard_map/ppermute | solution.py:70
  99.8 7.2 %copy-start = (bf16[8,2,16,2,2048]{4,2,1,0,3:T(8,128)(2,1)S(1)}, bf16[8,2,16,2,2048]{4,2,1,0,3:T(8,128)(2,1)}, u32[]{:S(2)}) copy-start(bf16[8,2,16,2,2048]{4,2,1,0,3:T(8,128)(2,1)} %copy.84) | copy-start | bytes 6291460
  100.9 35.4 %all-to-all-start = ((bf16[8,2,16,2048]{3,2,1,0:T(8,128)(2,1)}), bf16[8,2,16,2048]{3,2,1,0:T(8,128)(2,1)S(1)}, u32[]{:S(2)}, u32[]{:S(2)}) async-start(bf16[8,2,16,2048]{3,2,1,0:T(8,128)(2,1)} %copy.81), calls=%async_computation | async-start | bytes 2097152 | tf_op jit(solution)/shard_map/all_to_all | solution.py:109
  109.7 13.4 %copy-start.1 = (f32[3,256,256]{1,2,0:T(8,128)S(1)}, f32[3,256,256]{1,2,0:T(8,128)}, u32[]{:S(2)}) copy-start(f32[3,256,256]{1,2,0:T(8,128)} %get-tuple-element.29) | copy-start | bytes 2359300
  109.7 13.4 %copy-start.6 = (bf16[1,256,384]{1,2,0:T(8,128)(2,1)S(1)}, bf16[1,256,384]{1,2,0:T(8,128)(2,1)}, u32[]{:S(2)}) copy-start(bf16[1,256,384]{1,2,0:T(8,128)(2,1)} %copy-done.5) | copy-start | bytes 589828
  109.8 13.2 %collective-permute-start.5 = (f32[256,384]{1,0:T(8,128)S(1)}, f32[256,384]{1,0:T(8,128)S(1)}, u32[]{:S(2)}, u32[]{:S(2)}) collective-permute-start(f32[256,384]{1,0:T(8,128)S(1)} %dynamic-slice_bitcast_fusion.1), channel_id=1, source_target_pairs={{0,1},{1,0},{2,3},{3,2},{4,5},{5,4},{6,7},{7,6},{8,9},{9,8},{10,11... | collective-permute-start | bytes 1179656 | tf_op jit(solution)/shard_map/ppermute | solution.py:80
  136.5 7.2 %collective-permute-start.2 = (bf16[16,2048]{1,0:T(8,128)(2,1)S(1)}, bf16[16,2048]{1,0:T(8,128)(2,1)S(1)}, u32[]{:S(2)}, u32[]{:S(2)}) collective-permute-start(bf16[16,2048]{1,0:T(8,128)(2,1)S(1)} %dynamic-slice_bitcast_fusion.3), channel_id=1, source_target_pairs={{0,1},{1,0},{2,3},{3,2},{4,5},{5,4},{6,7},{7,6},{8,9},{9,8},{10,11... | collective-permute-start | bytes 196616 | tf_op jit(solution)/shard_map/ppermute | solution.py:80
Sparse Core Ops, SparseCore 0:
  37.3 47.4 all-gather.1

commit v8 on v7

--- a/solution.py
+++ b/solution.py
@@ -93,20 +93,25 @@
 
 
 def gather_patch_blocks(pieces):
-    chips = lax.axis_size("x")
-    mine = gather_by_all_to_all(pieces, "x")
+    chips, pairs = lax.axis_size("x"), lax.axis_size("zl")
+    copies = jnp.broadcast_to(pieces[None], (chips,) + pieces.shape)
+    mine = lax.all_to_all(copies.reshape(chips * pairs, *pieces.shape[1:]), ("x", "zl"), 0, 0, tiled=False)
+    mine = mine.reshape(chips, pairs, *pieces.shape[1:])
     other = swap_cores(mine)
     first = lax.axis_index("c") == 0
     both = jnp.stack([jnp.where(first, mine, other), jnp.where(first, other, mine)], axis=1)
-    return both.reshape(chips * 2 * pieces.shape[0], *pieces.shape[1:])
+    return both.transpose(0, 1, 3, 2, 4).reshape(chips * 2 * pieces.shape[1], pairs, pieces.shape[2])
 
 
 def sum_patch_blocks(blocks):
+    chips, pairs = lax.axis_size("x"), lax.axis_size("zl")
     core = lax.axis_index("c")
     keep = lax.dynamic_index_in_dim(blocks, core, axis=1, keepdims=False)
     send = lax.dynamic_index_in_dim(blocks, 1 - core, axis=1, keepdims=False)
     pair = (keep.astype(jnp.float32) + swap_cores(send).astype(jnp.float32)).astype(jnp.bfloat16)
-    received = lax.all_to_all(pair, "x", 0, 0, tiled=False)
+    pair = pair.reshape(chips * pairs, *pair.shape[2:])
+    received = lax.all_to_all(pair, ("x", "zl"), 0, 0, tiled=False)
+    received = received.reshape(chips, pairs, *pair.shape[1:])
     return received.astype(jnp.float32).sum(axis=0).astype(jnp.bfloat16)
 
 
@@ -126,18 +131,14 @@
     partial = jnp.einsum(
         "gxcpf,fd->xcgpd", tokens, columns, preferred_element_type=jnp.float32
     ).astype(jnp.bfloat16)
-    summed = sum_patch_blocks(partial)
-    keep, send = split_pair(summed)
-    own = in_pair_order(keep, swap_pair(send))
+    own = sum_patch_blocks(partial)
     projected = (
         own.reshape(zls, block, ys, zhs, span // (ys * zhs))
         .transpose(1, 3, 2, 0, 4)
         .reshape(block, 1, -1)
     )
     pieces = upstream[:, 0].reshape(block, zhs, ys, zls, -1).transpose(3, 0, 2, 1, 4)
-    keep, send = split_pair(pieces.reshape(zls, block, span))
-    pieces = in_pair_order(keep, swap_pair(send))
-    grad_full = gather_patch_blocks(pieces.transpose(1, 0, 2))
+    grad_full = gather_patch_blocks(pieces.reshape(zls, block, span))
     grad_partial = jnp.einsum(
         "qgd,cd->gqc", grad_full, columns, preferred_element_type=jnp.float32
     )

time: 153 us -> 138 us (0.902)
  starting transfers between devices: 39.1 us -> 28.4 us
  waiting for transfers between devices: 50.5 us -> 47 us
  other arithmetic: 3.82 us -> 2.11 us
    ppermute x4 -> x2, starting transfers between devices: 15.3 us -> 5.16 us  [swap_pair(): return lax.ppermute(block, 'zl', [(0, 1), (1, 0)])]
    ppermute x4 -> x2, waiting for transfers between devices: 9.27 us -> 16.9 us  [swap_pair(): return lax.ppermute(block, 'zl', [(0, 1), (1, 0)])]
    all_gather x1, waiting for transfers between devices: 6.63 us -> 0.02 us  [on_device(): columns = lax.all_gather(columns, 'y', axis=1, tiled=True)]
    all_to_all x2, waiting for transfers between devices: 34.6 us -> 30.1 us  [the longest x1 23.5 us: gather_patch_blocks(): lax.all_to_all(copies.reshape(chips * pairs, *pieces.shape[1:]), ('x', 'z...]
    ppermute x2, starting transfers between devices: 11.2 us -> 8.81 us  [swap_cores(): return lax.ppermute(block, 'c', [(0, 1), (1, 0)])]
    all_to_all x2, starting transfers between devices: 12.6 us -> 14.4 us  [the longest x1 9.22 us: gather_patch_blocks(): lax.all_to_all(copies.reshape(chips * pairs, *pieces.shape[1:]), ('x', 'z...]
    another operation x3 -> x0, local copies, waits for them, and re-layouts: 1.83 us -> none  [the longest x1 1.48 us: gather_patch_blocks(): jnp.stack([jnp.where(first, mine, other), jnp.where(first, other, mine)],...]
  transfers between devices with their start and end apart: 9 -> 7, of which waited for: 4 -> 4; matrix products, arithmetic and copies ran while one was open for 13% -> 13% of each run, Pallas kernels for 0% -> 0%
where the time goes in v8:
time: 138 us; the launch traced here: 136 us
  waiting for transfers between devices  47 us (34%)
  starting transfers between devices  28.4 us (21%)
  blocking collectives  23.3 us (17%)
  between operations  14.3 us (10%)
  local copies, waits for them, and re-layouts  12.5 us (9%)
  matrix products  8.19 us (6%)
  other arithmetic  2.11 us (2%)
    all_to_all x1, waiting for transfers between devices, gather_patch_blocks(): lax.all_to_all(copies.reshape(chips * pairs, *pieces.shape[1:]), ('x', 'z...  23.5 us
    all_gather x1, blocking collectives, on_device(): columns = lax.all_gather(projection, 'zh', axis=1, tiled=True)  23.3 us
    ppermute x2, waiting for transfers between devices, swap_pair(): return lax.ppermute(block, 'zl', [(0, 1), (1, 0)])  16.9 us
    all_to_all x1, starting transfers between devices, gather_patch_blocks(): lax.all_to_all(copies.reshape(chips * pairs, *pieces.shape[1:]), ('x', 'z...  9.22 us
    ppermute x2, starting transfers between devices, swap_cores(): return lax.ppermute(block, 'c', [(0, 1), (1, 0)])  8.81 us
    all_to_all x1, waiting for transfers between devices, sum_patch_blocks(): received = lax.all_to_all(pair, ('x', 'zl'), 0, 0, tiled=False)  6.65 us
    all_to_all x1, starting transfers between devices, sum_patch_blocks(): received = lax.all_to_all(pair, ('x', 'zl'), 0, 0, tiled=False)  5.18 us
    ppermute x2, starting transfers between devices, swap_pair(): return lax.ppermute(block, 'zl', [(0, 1), (1, 0)])  5.16 us
  transfers between devices with their start and end apart: 7, of which 4 were waited for; matrix products, arithmetic and copies ran while one was open for 13% of the time, Pallas kernels for 0%

profile of v8, /device:TPU:1, one launch (start us, length us, event | category | flops | bytes accessed | tf_op | source)
XLA Modules:
  0.0 135.9 jit_solution(17472010248724602592)
XLA Ops:
  7.2 0.0 all-gather.2.cloned.1.call-start
  7.2 23.3 %all_gather.6 = bf16[384,256]{0,1:T(8,128)(2,1)S(1)} all-gather(bf16[384,64]{0,1:T(8,128)(2,1)} %param.8), channel_id=1, replica_groups=mesh['zh'=4,'y'=8,'x'=8,'c'=2,'zl'=2] {'zh'}, dimensions={1}, use_global_device_ids=true | all-gather | bytes 245760 | tf_op jit(solution)/shard_map/all_gather | solution.py:126
  30.5 0.8 copy.81
  31.4 1.2 reshape_squeeze.3
  32.6 0.1 copy.107
  32.7 0.3 broadcast_in_dim.4
  33.0 1.1 broadcast_in_dim.5
  34.0 9.2 %all-to-all-start.1 = ((bf16[16,16,2048]{2,1,0:T(8,128)(2,1)}), bf16[16,16,2048]{2,1,0:T(8,128)(2,1)S(1)}, u32[]{:S(2)}, u32[]{:S(2)}) async-start(bf16[16,16,2048]{2,1,0:T(8,128)(2,1)} %bitcast.22), calls=%async_computation.1 | async-start | bytes 2097152 | tf_op jit(solution)/shard_map/all_to_all | solution.py:98
  43.3 0.1 copy.73
  43.4 0.1 copy.74
  43.6 0.1 copy.77
  43.8 0.5 fusion.17
  44.2 23.5 %all-to-all-done.1 = bf16[16,16,2048]{2,1,0:T(8,128)(2,1)S(1)} async-done(((bf16[16,16,2048]{2,1,0:T(8,128)(2,1)}), bf16[16,16,2048]{2,1,0:T(8,128)(2,1)S(1)}, u32[]{:S(2)}, u32[]{:S(2)}) %all-to-all-start.1) | async-done | bytes 1048608 | tf_op jit(solution)/shard_map/all_to_all | solution.py:98
  67.7 6.1 %collective-permute-start.2 = (bf16[8,2,16,2048]{3,2,1,0:T(8,128)(2,1)S(1)}, bf16[8,2,16,2048]{3,2,1,0:T(8,128)(2,1)S(1)}, u32[]{:S(2)}, u32[]{:S(2)}) collective-permute-start(bf16[8,2,16,2048]{3,2,1,0:T(8,128)(2,1)S(1)} %bitcast.92), channel_id=1, source_target_pairs={{0,2},{2,0},{1,3},{3,1},{4,6},{6,4},{5,7},{7,5},{8,10},{10,8},{9,1... | collective-permute-start | bytes 3145736 | tf_op jit(solution)/shard_map/ppermute | solution.py:70
  73.8 1.3 convolution_convert_fusion.1
  75.1 1.9 %collective-permute-start = (bf16[256,384]{0,1:T(8,128)(2,1)}, bf16[256,384]{0,1:T(8,128)(2,1)}, u32[]{:S(2)}, u32[]{:S(2)}) collective-permute-start(bf16[256,384]{0,1:T(8,128)(2,1)} %bitcast.115), channel_id=1, source_target_pairs={{0,1},{1,0},{2,3},{3,2},{4,5},{5,4},{6,7},{7,6},{8,9},{9,8},{10,11... | collective-permute-start | bytes 589832 | tf_op jit(solution)/shard_map/ppermute | solution.py:80
  77.0 6.8 %collective-permute-done = bf16[256,384]{0,1:T(8,128)(2,1)} collective-permute-done((bf16[256,384]{0,1:T(8,128)(2,1)}, bf16[256,384]{0,1:T(8,128)(2,1)}, u32[]{:S(2)}, u32[]{:S(2)}) %collective-permute-start) | collective-permute-done | bytes 196640 | tf_op jit(solution)/shard_map/ppermute | solution.py:80
  83.8 1.1 broadcast_select_fusion.1
  84.9 0.8 copy.79
  85.7 0.2 copy.80
  85.9 2.8 %convolution_convert_fusion = bf16[2,8,2,16,2048]{4,3,2,1,0:T(8,128)(2,1)S(1)} fusion(bf16[384,2048]{1,0:T(8,128)(2,1)} %all-gather.2.cloned.1.call-done, bf16[1,8,2,16,384]{4,3,2,1,0:T(8,128)(2,1)S(1)} %bitcast.114, bf16[1,8,2,16,384]{4,3,2,1,0:T(8,128)(2,1)} %bitcast.113), kind=kOutput, calls=%fused_computation.1 | convolution fusion | flops 806551552 | bytes 4063232 | tf_op jit(solution)/shard_map/gxcpf,fd->xcgpd/dot_general | solution.py:131
  88.7 0.1 dynamic-slice_bitcast_fusion
  88.8 2.7 %collective-permute-start.1 = (bf16[8,2,16,2048]{3,2,0,1:T(8,128)(2,1)S(1)}, bf16[8,2,16,2048]{3,2,0,1:T(8,128)(2,1)S(1)}, u32[]{:S(2)}, u32[]{:S(2)}) collective-permute-start(bf16[8,2,16,2048]{3,2,0,1:T(8,128)(2,1)S(1)} %dynamic-slice_bitcast_fusion), channel_id=1, source_target_pairs={{0,2},{2,0},{1,3},{3,1},{4,6},{6,4},{5,7},{7,5},{8,10},{10,8},{9,1... | collective-permute-start | bytes 3145736 | tf_op jit(solution)/shard_map/ppermute | solution.py:70
  91.5 0.1 select_bitcast_fusion.1
  91.7 0.2 maximum_bitcast_fusion
  91.9 0.2 copy.86
  92.1 1.2 copy-done.6
  93.3 1.3 fusion.3
  94.5 0.4 fusion.1
  95.0 1.0 copy.83
  96.0 5.2 %all-to-all-start = ((bf16[16,16,2048]{2,1,0:T(8,128)(2,1)}), bf16[16,16,2048]{2,1,0:T(8,128)(2,1)S(1)}, u32[]{:S(2)}, u32[]{:S(2)}) async-start(bf16[16,16,2048]{2,1,0:T(8,128)(2,1)} %bitcast.18), calls=%async_computation | async-start | bytes 2097152 | tf_op jit(solution)/shard_map/all_to_all | solution.py:113
  101.2 0.8 dynamic-slice_bitcast_fusion.1
  102.0 3.3 %collective-permute-start.3 = (f32[256,384]{1,0:T(8,128)}, f32[256,384]{1,0:T(8,128)S(1)}, u32[]{:S(2)}, u32[]{:S(2)}) collective-permute-start(f32[256,384]{1,0:T(8,128)} %dynamic-slice_bitcast_fusion.1), channel_id=1, source_target_pairs={{0,1},{1,0},{2,3},{3,2},{4,5},{5,4},{6,7},{7,6},{8,9},{9,8},{10,11... | collective-permute-start | bytes 1179656 | tf_op jit(solution)/shard_map/ppermute | solution.py:80
  105.2 10.1 %collective-permute-done.3 = f32[256,384]{1,0:T(8,128)S(1)} collective-permute-done((f32[256,384]{1,0:T(8,128)}, f32[256,384]{1,0:T(8,128)S(1)}, u32[]{:S(2)}, u32[]{:S(2)}) %collective-permute-start.3) | collective-permute-done | bytes 393248 | tf_op jit(solution)/shard_map/ppermute | solution.py:80
  115.4 0.1 copy.87
  115.5 1.3 multiply_reduce_fusion
  116.8 0.1 multiply_convert_fusion
  116.9 0.3 convolution_multiply_fusion.2
  117.2 0.9 copy.94
  118.1 0.2 convolution_multiply_fusion.1
  118.4 0.9 copy.93
  119.3 0.6 fusion.11
  119.9 0.9 copy.95
  120.8 6.7 %all-to-all-done = bf16[16,16,2048]{2,1,0:T(8,128)(2,1)S(1)} async-done(((bf16[16,16,2048]{2,1,0:T(8,128)(2,1)}), bf16[16,16,2048]{2,1,0:T(8,128)(2,1)S(1)}, u32[]{:S(2)}, u32[]{:S(2)}) %all-to-all-start) | async-done | bytes 1048608 | tf_op jit(solution)/shard_map/all_to_all | solution.py:113
  127.5 0.2 reduce_sum.31
  127.6 0.2 reshape.128
  127.9 0.3 copy.84
  128.2 0.9 reshape.129
  (18 shorter events, 0.1 us)
Async XLA Ops:
  7.2 78.7 %all-gather.2.cloned.1.call-start = ((), (), s32[]{:S(2)}) async-start(), calls=%async_computation.2 | async-start | bytes 1769472 | tf_op jit(solution)/shard_map/all_gather | solution.py:127
  32.5 10.7 %copy-start.2 = (bf16[1,256,384]{2,1,0:T(8,128)(2,1)S(1)}, bf16[1,256,384]{2,1,0:T(8,128)(2,1)}, u32[]{:S(2)}) copy-start(bf16[1,256,384]{2,1,0:T(8,128)(2,1)} %param.5) | copy-start | bytes 589828
  32.7 10.8 %copy-start.3 = (bf16[1,256,384]{2,1,0:T(8,128)(2,1)S(1)}, bf16[1,256,384]{2,1,0:T(8,128)(2,1)}, u32[]{:S(2)}) copy-start(bf16[1,256,384]{2,1,0:T(8,128)(2,1)} %param.6) | copy-start | bytes 589828
  32.9 10.6 %copy-start.4 = (bf16[1,256,384]{2,1,0:T(8,128)(2,1)S(1)}, bf16[1,256,384]{2,1,0:T(8,128)(2,1)}, u32[]{:S(2)}) copy-start(bf16[1,256,384]{2,1,0:T(8,128)(2,1)} %param.7) | copy-start | bytes 589828
  34.0 33.6 %all-to-all-start.1 = ((bf16[16,16,2048]{2,1,0:T(8,128)(2,1)}), bf16[16,16,2048]{2,1,0:T(8,128)(2,1)S(1)}, u32[]{:S(2)}, u32[]{:S(2)}) async-start(bf16[16,16,2048]{2,1,0:T(8,128)(2,1)} %bitcast.22), calls=%async_computation.1 | async-start | bytes 2097152 | tf_op jit(solution)/shard_map/all_to_all | solution.py:98
  43.6 31.5 %copy-start = (bf16[1,256,384]{1,2,0:T(8,128)(2,1)}, bf16[1,256,384]{1,2,0:T(8,128)(2,1)S(1)}, u32[]{:S(2)}) copy-start(bf16[1,256,384]{1,2,0:T(8,128)(2,1)S(1)} %copy.74) | copy-start | bytes 589828
  43.7 31.3 %copy-start.5 = (bf16[1,256,384]{1,2,0:T(8,128)(2,1)}, bf16[1,256,384]{1,2,0:T(8,128)(2,1)S(1)}, u32[]{:S(2)}) copy-start(bf16[1,256,384]{1,2,0:T(8,128)(2,1)S(1)} %copy.77) | copy-start | bytes 589828
  67.7 23.8 %collective-permute-start.2 = (bf16[8,2,16,2048]{3,2,1,0:T(8,128)(2,1)S(1)}, bf16[8,2,16,2048]{3,2,1,0:T(8,128)(2,1)S(1)}, u32[]{:S(2)}, u32[]{:S(2)}) collective-permute-start(bf16[8,2,16,2048]{3,2,1,0:T(8,128)(2,1)S(1)} %bitcast.92), channel_id=1, source_target_pairs={{0,2},{2,0},{1,3},{3,1},{4,6},{6,4},{5,7},{7,5},{8,10},{10,8},{9,1... | collective-permute-start | bytes 3145736 | tf_op jit(solution)/shard_map/ppermute | solution.py:70
  75.1 8.7 %collective-permute-start = (bf16[256,384]{0,1:T(8,128)(2,1)}, bf16[256,384]{0,1:T(8,128)(2,1)}, u32[]{:S(2)}, u32[]{:S(2)}) collective-permute-start(bf16[256,384]{0,1:T(8,128)(2,1)} %bitcast.115), channel_id=1, source_target_pairs={{0,1},{1,0},{2,3},{3,2},{4,5},{5,4},{6,7},{7,6},{8,9},{9,8},{10,11... | collective-permute-start | bytes 589832 | tf_op jit(solution)/shard_map/ppermute | solution.py:80
  88.8 5.8 %collective-permute-start.1 = (bf16[8,2,16,2048]{3,2,0,1:T(8,128)(2,1)S(1)}, bf16[8,2,16,2048]{3,2,0,1:T(8,128)(2,1)S(1)}, u32[]{:S(2)}, u32[]{:S(2)}) collective-permute-start(bf16[8,2,16,2048]{3,2,0,1:T(8,128)(2,1)S(1)} %dynamic-slice_bitcast_fusion), channel_id=1, source_target_pairs={{0,2},{2,0},{1,3},{3,1},{4,6},{6,4},{5,7},{7,5},{8,10},{10,8},{9,1... | collective-permute-start | bytes 3145736 | tf_op jit(solution)/shard_map/ppermute | solution.py:70
  91.9 1.4 %copy-start.6 = (bf16[384,2048]{1,0:T(8,128)(2,1)S(1)}, bf16[384,2048]{1,0:T(8,128)(2,1)}, u32[]{:S(2)}) copy-start(bf16[384,2048]{1,0:T(8,128)(2,1)} %all-gather.2.cloned.1.call-done) | copy-start | bytes 4718596
  96.0 31.5 %all-to-all-start = ((bf16[16,16,2048]{2,1,0:T(8,128)(2,1)}), bf16[16,16,2048]{2,1,0:T(8,128)(2,1)S(1)}, u32[]{:S(2)}, u32[]{:S(2)}) async-start(bf16[16,16,2048]{2,1,0:T(8,128)(2,1)} %bitcast.18), calls=%async_computation | async-start | bytes 2097152 | tf_op jit(solution)/shard_map/all_to_all | solution.py:113
  102.0 13.4 %collective-permute-start.3 = (f32[256,384]{1,0:T(8,128)}, f32[256,384]{1,0:T(8,128)S(1)}, u32[]{:S(2)}, u32[]{:S(2)}) collective-permute-start(f32[256,384]{1,0:T(8,128)} %dynamic-slice_bitcast_fusion.1), channel_id=1, source_target_pairs={{0,1},{1,0},{2,3},{3,2},{4,5},{5,4},{6,7},{7,6},{8,9},{9,8},{10,11... | collective-permute-start | bytes 1179656 | tf_op jit(solution)/shard_map/ppermute | solution.py:80
  116.8 1.4 copy-start.1
Sparse Core Ops, SparseCore 0:
  31.5 48.4 all-gather.1

commit v9 on v8

--- a/solution.py
+++ b/solution.py
@@ -143,7 +143,8 @@
         "qgd,cd->gqc", grad_full, columns, preferred_element_type=jnp.float32
     )
     keep, send = split_pair(grad_partial)
-    grad_rounded = (keep + swap_pair(send)).astype(jnp.bfloat16)[None]
+    arrived = swap_pair(send.astype(jnp.bfloat16)).astype(jnp.float32)
+    grad_rounded = (keep + arrived).astype(jnp.bfloat16)[None]
     grad_q, grad_k, grad_v = backward_heads(
         soft, queries, key_rows, value_rows, grad_rounded, head_count
     )

time: 138 us -> 141 us (1.022)
  waiting for transfers between devices: 47 us -> 35.8 us
  starting transfers between devices: 28.4 us -> 35.7 us
  other arithmetic: 2.11 us -> 4.51 us
  matrix products: 8.19 us -> 10.2 us
  local copies, waits for them, and re-layouts: 12.5 us -> 14.4 us
    ppermute x2, waiting for transfers between devices: 16.9 us -> 5.15 us  [swap_pair(): return lax.ppermute(block, 'zl', [(0, 1), (1, 0)])]
    all_to_all x1, waiting for transfers between devices: 23.5 us -> 18.7 us  [gather_patch_blocks(): lax.all_to_all(copies.reshape(chips * pairs, *pieces.shape[1:]), ('x', 'z...]
    all_gather x1, waiting for transfers between devices: 0.02 us -> 4.47 us  [on_device(): columns = lax.all_gather(columns, 'y', axis=1, tiled=True)]
    ppermute x2, starting transfers between devices: 8.81 us -> 12.3 us  [swap_cores(): return lax.ppermute(block, 'c', [(0, 1), (1, 0)])]
    all_to_all x1, starting transfers between devices: 5.18 us -> 7.58 us  [sum_patch_blocks(): received = lax.all_to_all(pair, ('x', 'zl'), 0, 0, tiled=False)]
  transfers between devices with their start and end apart: 7 -> 7, of which waited for: 4 -> 4; matrix products, arithmetic and copies ran while one was open for 13% -> 17% of each run, Pallas kernels for 0% -> 0%
where the time goes in v9:
time: 141 us; the launch traced here: 138 us
  waiting for transfers between devices  35.8 us (25%)
  starting transfers between devices  35.7 us (25%)
  blocking collectives  23.3 us (17%)
  local copies, waits for them, and re-layouts  14.4 us (10%)
  between operations  14.3 us (10%)
  matrix products  10.2 us (7%)
  other arithmetic  4.51 us (3%)
    all_gather x1, blocking collectives, on_device(): columns = lax.all_gather(projection, 'zh', axis=1, tiled=True)  23.3 us
    all_to_all x1, waiting for transfers between devices, gather_patch_blocks(): lax.all_to_all(copies.reshape(chips * pairs, *pieces.shape[1:]), ('x', 'z...  18.7 us
    ppermute x2, starting transfers between devices, swap_cores(): return lax.ppermute(block, 'c', [(0, 1), (1, 0)])  12.3 us
    all_to_all x1, starting transfers between devices, gather_patch_blocks(): lax.all_to_all(copies.reshape(chips * pairs, *pieces.shape[1:]), ('x', 'z...  9.22 us
    all_to_all x1, starting transfers between devices, sum_patch_blocks(): received = lax.all_to_all(pair, ('x', 'zl'), 0, 0, tiled=False)  7.58 us
    all_to_all x1, waiting for transfers between devices, sum_patch_blocks(): received = lax.all_to_all(pair, ('x', 'zl'), 0, 0, tiled=False)  7.44 us
    ppermute x2, starting transfers between devices, swap_pair(): return lax.ppermute(block, 'zl', [(0, 1), (1, 0)])  6.53 us
    ppermute x2, waiting for transfers between devices, swap_pair(): return lax.ppermute(block, 'zl', [(0, 1), (1, 0)])  5.15 us
  transfers between devices with their start and end apart: 7, of which 4 were waited for; matrix products, arithmetic and copies ran while one was open for 17% of the time, Pallas kernels for 0%

profile of v9, /device:TPU:1, one launch (start us, length us, event | category | flops | bytes accessed | tf_op | source)
XLA Modules:
  0.0 138.2 jit_solution(13102450274298522228)
XLA Ops:
  7.2 0.0 all-gather.2.cloned.1.call-start
  7.2 23.3 %all_gather.6 = bf16[384,256]{0,1:T(8,128)(2,1)S(1)} all-gather(bf16[384,64]{0,1:T(8,128)(2,1)} %param.8), channel_id=1, replica_groups=mesh['zh'=4,'y'=8,'x'=8,'c'=2,'zl'=2] {'zh'}, dimensions={1}, use_global_device_ids=true | all-gather | bytes 245760 | tf_op jit(solution)/shard_map/all_gather | solution.py:126
  30.5 0.8 copy.82
  31.3 0.0 all-gather.2.cloned.1.call-update
  31.4 1.2 reshape_squeeze.3
  32.6 0.1 copy.108
  32.7 0.3 broadcast_in_dim.4
  33.0 1.1 broadcast_in_dim.5
  34.0 9.2 %all-to-all-start.1 = ((bf16[16,16,2048]{2,1,0:T(8,128)(2,1)}), bf16[16,16,2048]{2,1,0:T(8,128)(2,1)S(1)}, u32[]{:S(2)}, u32[]{:S(2)}) async-start(bf16[16,16,2048]{2,1,0:T(8,128)(2,1)} %bitcast.22), calls=%async_computation.1 | async-start | bytes 2097152 | tf_op jit(solution)/shard_map/all_to_all | solution.py:98
  43.3 0.1 copy.74
  43.4 0.1 copy.75
  43.6 0.1 copy.78
  43.8 1.3 fusion.18
  45.1 0.6 convolution_convert_fusion.1
  45.7 3.3 %collective-permute-start = (bf16[256,384]{0,1:T(8,128)(2,1)S(1)}, bf16[256,384]{0,1:T(8,128)(2,1)S(1)}, u32[]{:S(2)}, u32[]{:S(2)}) collective-permute-start(bf16[256,384]{0,1:T(8,128)(2,1)S(1)} %bitcast.115), channel_id=1, source_target_pairs={{0,1},{1,0},{2,3},{3,2},{4,5},{5,4},{6,7},{7,6},{8,9},{9,8},{10,11... | collective-permute-start | bytes 589832 | tf_op jit(solution)/shard_map/ppermute | solution.py:80
  49.0 18.7 %all-to-all-done.1 = bf16[16,16,2048]{2,1,0:T(8,128)(2,1)S(1)} async-done(((bf16[16,16,2048]{2,1,0:T(8,128)(2,1)}), bf16[16,16,2048]{2,1,0:T(8,128)(2,1)S(1)}, u32[]{:S(2)}, u32[]{:S(2)}) %all-to-all-start.1) | async-done | bytes 1048608 | tf_op jit(solution)/shard_map/all_to_all | solution.py:98
  67.7 6.1 %collective-permute-start.2 = (bf16[8,2,16,2048]{3,2,1,0:T(8,128)(2,1)S(1)}, bf16[8,2,16,2048]{3,2,1,0:T(8,128)(2,1)}, u32[]{:S(2)}, u32[]{:S(2)}) collective-permute-start(bf16[8,2,16,2048]{3,2,1,0:T(8,128)(2,1)S(1)} %bitcast.92), channel_id=1, source_target_pairs={{0,2},{2,0},{1,3},{3,1},{4,6},{6,4},{5,7},{7,5},{8,10},{10,8},{9,1... | collective-permute-start | bytes 3145736 | tf_op jit(solution)/shard_map/ppermute | solution.py:70
  73.9 0.8 copy.80
  74.7 0.8 copy.81
  75.5 4.5 %all-gather.2.cloned.1.call-done = bf16[384,2048]{1,0:T(8,128)(2,1)} async-done(((bf16[384,256]{1,0:T(8,128)(2,1)}), bf16[384,2048]{1,0:T(8,128)(2,1)}) %all-gather.2.cloned.1.call-update) | async-done | bytes 1572880 | tf_op jit(solution)/shard_map/all_gather | solution.py:127
  80.0 2.9 %convolution_convert_fusion = bf16[2,8,2,16,2048]{4,3,2,1,0:T(8,128)(2,1)S(1)} fusion(bf16[384,2048]{1,0:T(8,128)(2,1)} %all-gather.2.cloned.1.call-done, bf16[1,8,2,16,384]{4,3,2,1,0:T(8,128)(2,1)} %bitcast.114, bf16[1,8,2,16,384]{4,3,2,1,0:T(8,128)(2,1)} %bitcast.113), kind=kOutput, calls=%fused_computation.1 | convolution fusion | flops 806551552 | bytes 4063232 | tf_op jit(solution)/shard_map/gxcpf,fd->xcgpd/dot_general | solution.py:131
  82.9 1.1 dynamic-slice_bitcast_fusion
  83.9 6.2 %collective-permute-start.1 = (bf16[8,2,16,2048]{3,2,0,1:T(8,128)(2,1)}, bf16[8,2,16,2048]{3,2,0,1:T(8,128)(2,1)}, u32[]{:S(2)}, u32[]{:S(2)}) collective-permute-start(bf16[8,2,16,2048]{3,2,0,1:T(8,128)(2,1)} %dynamic-slice_bitcast_fusion), channel_id=1, source_target_pairs={{0,2},{2,0},{1,3},{3,1},{4,6},{6,4},{5,7},{7,5},{8,10},{10,8},{9,1... | collective-permute-start | bytes 3145736 | tf_op jit(solution)/shard_map/ppermute | solution.py:70
  90.1 1.4 select_bitcast_fusion.1
  91.5 0.2 maximum_bitcast_fusion
  91.7 1.5 %copy.87 = bf16[8,2,16,2,2048]{4,2,1,0,3:T(8,128)(2,1)} copy(bf16[8,2,16,2,2048]{4,2,3,0,1:T(8,128)(2,1)S(1)} %maximum_bitcast_fusion) | data formatting | bytes 4194304 | tf_op jit(solution)/shard_map/transpose | solution.py:103
  93.2 1.6 %fusion.1 = bf16[8,2,16,2048]{3,2,0,1:T(8,128)(2,1)S(1)} fusion(bf16[8,2,16,2048]{3,2,0,1:T(8,128)(2,1)} %collective-permute-done.1, bf16[2,8,2,16,2048]{4,3,2,1,0:T(8,128)(2,1)S(1)} %convolution_convert_fusion, s32[]{:T(128)S(6)} %select_n.41), kind=kLoop, calls=%fused_computation.4 | loop fusion | flops 2097152 | bytes 3145732 | tf_op jit(solution)/shard_map/convert_element_type | solution.py:111
  94.8 1.0 copy.84
  95.8 7.6 %all-to-all-start = ((bf16[16,16,2048]{2,1,0:T(8,128)(2,1)}), bf16[16,16,2048]{2,1,0:T(8,128)(2,1)S(1)}, u32[]{:S(2)}, u32[]{:S(2)}) async-start(bf16[16,16,2048]{2,1,0:T(8,128)(2,1)} %bitcast.18), calls=%async_computation | async-start | bytes 2097152 | tf_op jit(solution)/shard_map/all_to_all | solution.py:113
  103.4 2.7 %fusion.3 = f32[256,2,384]{2,0,1:T(8,128)S(1)} fusion(bf16[256,2,2048]{2,0,1:T(8,128)(2,1)S(1)} %bitcast.95, bf16[384,2048]{1,0:T(8,128)(2,1)} %all-gather.2.cloned.1.call-done), kind=kOutput, calls=%fused_computation.6 | convolution fusion | flops 805306368 | bytes 4456448 | tf_op jit(solution)/shard_map/qgd,cd->gqc/dot_general | solution.py:142
  106.1 0.9 copy-done.2
  107.1 3.3 %collective-permute-start.3 = (bf16[256,384]{1,0:T(8,128)(2,1)S(1)}, bf16[256,384]{1,0:T(8,128)(2,1)S(1)}, u32[]{:S(2)}, u32[]{:S(2)}) collective-permute-start(bf16[256,384]{1,0:T(8,128)(2,1)S(1)} %fusion.11), channel_id=1, source_target_pairs={{0,1},{1,0},{2,3},{3,2},{4,5},{5,4},{6,7},{7,6},{8,9},{9,8},{10,11... | collective-permute-start | bytes 589832 | tf_op jit(solution)/shard_map/ppermute | solution.py:80
  110.3 5.1 %collective-permute-done.3 = bf16[256,384]{1,0:T(8,128)(2,1)S(1)} collective-permute-done((bf16[256,384]{1,0:T(8,128)(2,1)S(1)}, bf16[256,384]{1,0:T(8,128)(2,1)S(1)}, u32[]{:S(2)}, u32[]{:S(2)}) %collective-permute-start.3) | collective-permute-done | bytes 196640 | tf_op jit(solution)/shard_map/ppermute | solution.py:80
  115.5 1.0 fusion.10
  116.5 0.1 copy.88
  116.7 1.6 %multiply_reduce_fusion = (f32[3,256]{1,0:T(4,128)S(1)}, f32[3,256,256]{1,2,0:T(8,128)S(1)}) fusion(f32[3,256,256]{1,2,0:T(8,128)} %get-tuple-element.25, f32[3,256]{1,0:T(4,128)S(1)} %get-tuple-element.24, bf16[256,3,128]{0,2,1:T(8,128)(2,1)S(1)} %bitcast.111, bf16[256,3,128]{0,2,1:T(8,128)(2,1)} %bitcast.110), kind=kOutput, calls=%fused_computation.18 | convolution fusion | flops 50920704 | bytes 1972224 | tf_op jit(solution)/shard_map/fqhd,fkhd->fhqk/dot_general | solution.py:48
  118.3 0.1 multiply_convert_fusion
  118.4 0.3 convolution_multiply_fusion.2
  118.7 0.9 copy.95
  119.6 0.2 convolution_multiply_fusion.1
  119.8 0.9 copy.94
  120.7 0.6 fusion.12
  121.4 0.9 copy.96
  122.3 7.4 %all-to-all-done = bf16[16,16,2048]{2,1,0:T(8,128)(2,1)S(1)} async-done(((bf16[16,16,2048]{2,1,0:T(8,128)(2,1)}), bf16[16,16,2048]{2,1,0:T(8,128)(2,1)S(1)}, u32[]{:S(2)}, u32[]{:S(2)}) %all-to-all-start) | async-done | bytes 1048608 | tf_op jit(solution)/shard_map/all_to_all | solution.py:113
  129.7 0.2 reduce_sum.31
  129.9 0.2 reshape.129
  130.1 0.3 copy.85
  130.4 0.9 reshape.130
  (18 shorter events, 0.1 us)
Async XLA Ops:
  7.2 72.8 %all-gather.2.cloned.1.call-start = ((), (), s32[]{:S(2)}) async-start(), calls=%async_computation.2 | async-start | bytes 1769472 | tf_op jit(solution)/shard_map/all_gather | solution.py:127
  32.5 10.7 %copy-start.3 = (bf16[1,256,384]{2,1,0:T(8,128)(2,1)S(1)}, bf16[1,256,384]{2,1,0:T(8,128)(2,1)}, u32[]{:S(2)}) copy-start(bf16[1,256,384]{2,1,0:T(8,128)(2,1)} %param.5) | copy-start | bytes 589828
  32.7 10.8 %copy-start.4 = (bf16[1,256,384]{2,1,0:T(8,128)(2,1)S(1)}, bf16[1,256,384]{2,1,0:T(8,128)(2,1)}, u32[]{:S(2)}) copy-start(bf16[1,256,384]{2,1,0:T(8,128)(2,1)} %param.6) | copy-start | bytes 589828
  32.9 10.6 %copy-start.5 = (bf16[1,256,384]{2,1,0:T(8,128)(2,1)S(1)}, bf16[1,256,384]{2,1,0:T(8,128)(2,1)}, u32[]{:S(2)}) copy-start(bf16[1,256,384]{2,1,0:T(8,128)(2,1)} %param.7) | copy-start | bytes 589828
  34.0 33.6 %all-to-all-start.1 = ((bf16[16,16,2048]{2,1,0:T(8,128)(2,1)}), bf16[16,16,2048]{2,1,0:T(8,128)(2,1)S(1)}, u32[]{:S(2)}, u32[]{:S(2)}) async-start(bf16[16,16,2048]{2,1,0:T(8,128)(2,1)} %bitcast.22), calls=%async_computation.1 | async-start | bytes 2097152 | tf_op jit(solution)/shard_map/all_to_all | solution.py:98
  43.8 2.0 %copy-start.6 = (bf16[1,256,384]{1,2,0:T(8,128)(2,1)}, bf16[1,256,384]{1,2,0:T(8,128)(2,1)S(1)}, u32[]{:S(2)}) copy-start(bf16[1,256,384]{1,2,0:T(8,128)(2,1)S(1)} %copy.78) | copy-start | bytes 589828
  45.7 28.1 %collective-permute-start = (bf16[256,384]{0,1:T(8,128)(2,1)S(1)}, bf16[256,384]{0,1:T(8,128)(2,1)S(1)}, u32[]{:S(2)}, u32[]{:S(2)}) collective-permute-start(bf16[256,384]{0,1:T(8,128)(2,1)S(1)} %bitcast.115), channel_id=1, source_target_pairs={{0,1},{1,0},{2,3},{3,2},{4,5},{5,4},{6,7},{7,6},{8,9},{9,8},{10,11... | collective-permute-start | bytes 589832 | tf_op jit(solution)/shard_map/ppermute | solution.py:80
  67.7 22.4 %collective-permute-start.2 = (bf16[8,2,16,2048]{3,2,1,0:T(8,128)(2,1)S(1)}, bf16[8,2,16,2048]{3,2,1,0:T(8,128)(2,1)}, u32[]{:S(2)}, u32[]{:S(2)}) collective-permute-start(bf16[8,2,16,2048]{3,2,1,0:T(8,128)(2,1)S(1)} %bitcast.92), channel_id=1, source_target_pairs={{0,2},{2,0},{1,3},{3,1},{4,6},{6,4},{5,7},{7,5},{8,10},{10,8},{9,1... | collective-permute-start | bytes 3145736 | tf_op jit(solution)/shard_map/ppermute | solution.py:70
  83.9 9.3 %collective-permute-start.1 = (bf16[8,2,16,2048]{3,2,0,1:T(8,128)(2,1)}, bf16[8,2,16,2048]{3,2,0,1:T(8,128)(2,1)}, u32[]{:S(2)}, u32[]{:S(2)}) collective-permute-start(bf16[8,2,16,2048]{3,2,0,1:T(8,128)(2,1)} %dynamic-slice_bitcast_fusion), channel_id=1, source_target_pairs={{0,2},{2,0},{1,3},{3,1},{4,6},{6,4},{5,7},{7,5},{8,10},{10,8},{9,1... | collective-permute-start | bytes 3145736 | tf_op jit(solution)/shard_map/ppermute | solution.py:70
  94.8 8.6 %copy-start = (bf16[8,2,16,2,2048]{4,2,1,0,3:T(8,128)(2,1)S(1)}, bf16[8,2,16,2,2048]{4,2,1,0,3:T(8,128)(2,1)}, u32[]{:S(2)}) copy-start(bf16[8,2,16,2,2048]{4,2,1,0,3:T(8,128)(2,1)} %copy.87) | copy-start | bytes 6291460
  95.8 33.9 %all-to-all-start = ((bf16[16,16,2048]{2,1,0:T(8,128)(2,1)}), bf16[16,16,2048]{2,1,0:T(8,128)(2,1)S(1)}, u32[]{:S(2)}, u32[]{:S(2)}) async-start(bf16[16,16,2048]{2,1,0:T(8,128)(2,1)} %bitcast.18), calls=%async_computation | async-start | bytes 2097152 | tf_op jit(solution)/shard_map/all_to_all | solution.py:113
  106.1 0.9 copy-start.2
  107.1 8.4 %collective-permute-start.3 = (bf16[256,384]{1,0:T(8,128)(2,1)S(1)}, bf16[256,384]{1,0:T(8,128)(2,1)S(1)}, u32[]{:S(2)}, u32[]{:S(2)}) collective-permute-start(bf16[256,384]{1,0:T(8,128)(2,1)S(1)} %fusion.11), channel_id=1, source_target_pairs={{0,1},{1,0},{2,3},{3,2},{4,5},{5,4},{6,7},{7,6},{8,9},{9,8},{10,11... | collective-permute-start | bytes 589832 | tf_op jit(solution)/shard_map/ppermute | solution.py:80
  110.3 7.9 %copy-start.1 = (f32[3,256,256]{1,2,0:T(8,128)S(1)}, f32[3,256,256]{1,2,0:T(8,128)}, u32[]{:S(2)}) copy-start(f32[3,256,256]{1,2,0:T(8,128)} %get-tuple-element.25) | copy-start | bytes 2359300
Sparse Core Ops, SparseCore 0:
  31.5 48.4 all-gather.1

commit v10 on v8

--- a/solution.py
+++ b/solution.py
@@ -103,11 +103,8 @@
     return both.transpose(0, 1, 3, 2, 4).reshape(chips * 2 * pieces.shape[1], pairs, pieces.shape[2])
 
 
-def sum_patch_blocks(blocks):
+def sum_patch_blocks(send, keep):
     chips, pairs = lax.axis_size("x"), lax.axis_size("zl")
-    core = lax.axis_index("c")
-    keep = lax.dynamic_index_in_dim(blocks, core, axis=1, keepdims=False)
-    send = lax.dynamic_index_in_dim(blocks, 1 - core, axis=1, keepdims=False)
     pair = (keep.astype(jnp.float32) + swap_cores(send).astype(jnp.float32)).astype(jnp.bfloat16)
     pair = pair.reshape(chips * pairs, *pair.shape[2:])
     received = lax.all_to_all(pair, ("x", "zl"), 0, 0, tiled=False)
@@ -128,10 +125,17 @@
     span = columns.shape[1]
     group = in_pair_order(attended[0], swap_pair(attended[0]))
     tokens = group.reshape(zls, chips, 2, block, width)
-    partial = jnp.einsum(
-        "gxcpf,fd->xcgpd", tokens, columns, preferred_element_type=jnp.float32
-    ).astype(jnp.bfloat16)
-    own = sum_patch_blocks(partial)
+    core = lax.axis_index("c")
+    halves = [
+        jnp.einsum(
+            "gxpf,fd->xgpd",
+            lax.dynamic_index_in_dim(tokens, pick, axis=2, keepdims=False),
+            columns,
+            preferred_element_type=jnp.float32,
+        ).astype(jnp.bfloat16)
+        for pick in (1 - core, core)
+    ]
+    own = sum_patch_blocks(*halves)
     projected = (
         own.reshape(zls, block, ys, zhs, span // (ys * zhs))
         .transpose(1, 3, 2, 0, 4)

time: 138 us -> 156 us (1.13)
  waiting for transfers between devices: 47 us -> 56.9 us
  starting transfers between devices: 28.4 us -> 37.6 us
    all_gather x1, waiting for transfers between devices: 0.02 us -> 33.1 us  [on_device(): columns = lax.all_gather(columns, 'y', axis=1, tiled=True)]
    all_to_all x1, waiting for transfers between devices: 23.5 us -> 0.01 us  [gather_patch_blocks(): lax.all_to_all(copies.reshape(chips * pairs, *pieces.shape[1:]), ('x', 'z...]
    ppermute x2, starting transfers between devices: 8.81 us -> 14.2 us  [swap_cores(): return lax.ppermute(block, 'c', [(0, 1), (1, 0)])]
    all_to_all x1, starting transfers between devices: 5.18 us -> 7.76 us  [sum_patch_blocks(): received = lax.all_to_all(pair, ('x', 'zl'), 0, 0, tiled=False)]
    unnamed x20 -> x24, local copies, waits for them, and re-layouts: 4.37 us -> 5.06 us
  transfers between devices with their start and end apart: 7 -> 7, of which waited for: 4 -> 4; matrix products, arithmetic and copies ran while one was open for 13% -> 10% of each run, Pallas kernels for 0% -> 0%
where the time goes in v10:
time: 156 us; the launch traced here: 154 us
  waiting for transfers between devices  56.9 us (36%)
  starting transfers between devices  37.6 us (24%)
  blocking collectives  21.8 us (14%)
  between operations  14.3 us (9%)
  local copies, waits for them, and re-layouts  12.6 us (8%)
  matrix products  9.19 us (6%)
  other arithmetic  1.61 us (1%)
    all_gather x1, waiting for transfers between devices, on_device(): columns = lax.all_gather(columns, 'y', axis=1, tiled=True)  33.1 us
    all_gather x1, blocking collectives, on_device(): columns = lax.all_gather(projection, 'zh', axis=1, tiled=True)  21.8 us
    ppermute x2, waiting for transfers between devices, swap_pair(): return lax.ppermute(block, 'zl', [(0, 1), (1, 0)])  15.9 us
    ppermute x2, starting transfers between devices, swap_cores(): return lax.ppermute(block, 'c', [(0, 1), (1, 0)])  14.2 us
    all_to_all x1, starting transfers between devices, gather_patch_blocks(): lax.all_to_all(copies.reshape(chips * pairs, *pieces.shape[1:]), ('x', 'z...  10.3 us
    all_to_all x1, waiting for transfers between devices, sum_patch_blocks(): received = lax.all_to_all(pair, ('x', 'zl'), 0, 0, tiled=False)  7.85 us
    all_to_all x1, starting transfers between devices, sum_patch_blocks(): received = lax.all_to_all(pair, ('x', 'zl'), 0, 0, tiled=False)  7.76 us
    ppermute x2, starting transfers between devices, swap_pair(): return lax.ppermute(block, 'zl', [(0, 1), (1, 0)])  5.41 us
  transfers between devices with their start and end apart: 7, of which 4 were waited for; matrix products, arithmetic and copies ran while one was open for 10% of the time, Pallas kernels for 0%

profile of v10, /device:TPU:1, one launch (start us, length us, event | category | flops | bytes accessed | tf_op | source)
XLA Modules:
  0.0 154.1 jit_solution(18032289449628496231)
XLA Ops:
  7.2 1.2 reshape_squeeze.3
  8.4 0.0 copy-start.8
  8.4 0.1 copy.105
  8.5 0.3 broadcast_in_dim.4
  8.8 0.0 copy-start.6
  8.8 1.1 broadcast_in_dim.5
  9.9 10.3 %all-to-all-start.1 = ((bf16[16,16,2048]{2,1,0:T(8,128)(2,1)}), bf16[16,16,2048]{2,1,0:T(8,128)(2,1)S(1)}, u32[]{:S(2)}, u32[]{:S(2)}) async-start(bf16[16,16,2048]{2,1,0:T(8,128)(2,1)} %bitcast.23), calls=%async_computation.1 | async-start | bytes 2097152 | tf_op jit(solution)/shard_map/all_to_all | solution.py:98
  20.1 0.0 all-gather.2.cloned.1.call-start
  20.2 21.8 %all_gather.6 = bf16[384,256]{0,1:T(8,128)(2,1)S(1)} all-gather(bf16[384,64]{0,1:T(8,128)(2,1)S(1)} %copy-done.8), channel_id=1, replica_groups=mesh['zh'=4,'y'=8,'x'=8,'c'=2,'zl'=2] {'zh'}, dimensions={1}, use_global_device_ids=true | all-gather | bytes 245760 | tf_op jit(solution)/shard_map/all_gather | solution.py:123
  42.0 0.8 copy.81
  42.9 0.0 all-gather.2.cloned.1.call-update
  42.9 0.1 copy.72
  43.1 0.1 copy.73
  43.2 7.7 %collective-permute-start.2 = (bf16[8,2,16,2048]{3,2,1,0:T(8,128)(2,1)S(1)}, bf16[8,2,16,2048]{3,2,1,0:T(8,128)(2,1)S(1)}, u32[]{:S(2)}, u32[]{:S(2)}) collective-permute-start(bf16[8,2,16,2048]{3,2,1,0:T(8,128)(2,1)S(1)} %bitcast.94), channel_id=1, source_target_pairs={{0,2},{2,0},{1,3},{3,1},{4,6},{6,4},{5,7},{7,5},{8,10},{10,8},{9,1... | collective-permute-start | bytes 3145736 | tf_op jit(solution)/shard_map/ppermute | solution.py:70
  51.0 0.5 fusion.28
  51.4 0.8 copy.76
  52.3 2.2 %convolution_convert_fusion.2 = bf16[3,256,128]{1,2,0:T(8,128)(2,1)} fusion(bf16[256,3,128]{0,2,1:T(8,128)(2,1)} %bitcast.115, f32[3,256]{1,0:T(4,128)S(1)} %get-tuple-element.24, bf16[256,3,128]{0,2,1:T(8,128)(2,1)S(1)} %bitcast.107, bf16[256,3,128]{0,2,1:T(8,128)(2,1)S(1)} %bitcast.111), kind=kOutput, calls=%fused_computation.17 | convolution fusion | flops 101549056 | bytes 789504 | tf_op jit(solution)/shard_map/fhqk,fkhd->fqhd/dot_general | solution.py:32
  54.5 1.1 copy.79
  55.6 2.1 %collective-permute-start = (bf16[256,384]{1,0:T(8,128)(2,1)S(1)}, bf16[256,384]{1,0:T(8,128)(2,1)}, u32[]{:S(2)}, u32[]{:S(2)}) collective-permute-start(bf16[256,384]{1,0:T(8,128)(2,1)S(1)} %copy.79), channel_id=1, source_target_pairs={{0,1},{1,0},{2,3},{3,2},{4,5},{5,4},{6,7},{7,6},{8,9},{9,8},{10,11... | collective-permute-start | bytes 589832 | tf_op jit(solution)/shard_map/ppermute | solution.py:80
  57.7 6.4 %collective-permute-done = bf16[256,384]{1,0:T(8,128)(2,1)} collective-permute-done((bf16[256,384]{1,0:T(8,128)(2,1)S(1)}, bf16[256,384]{1,0:T(8,128)(2,1)}, u32[]{:S(2)}, u32[]{:S(2)}) %collective-permute-start) | collective-permute-done | bytes 196640 | tf_op jit(solution)/shard_map/ppermute | solution.py:80
  64.1 1.0 broadcast_select_fusion
  65.1 33.1 %all-gather.2.cloned.1.call-done = bf16[384,2048]{1,0:T(8,128)(2,1)} async-done(((bf16[384,256]{1,0:T(8,128)(2,1)}), bf16[384,2048]{1,0:T(8,128)(2,1)}) %all-gather.2.cloned.1.call-update) | async-done | bytes 1572880 | tf_op jit(solution)/shard_map/all_gather | solution.py:124
  98.2 2.1 %fusion.3 = bf16[8,2,16,2048]{3,2,0,1:T(8,128)(2,1)S(1)} fusion(bf16[384,2048]{1,0:T(8,128)(2,1)} %all-gather.2.cloned.1.call-done, s32[]{:T(128)S(6)} %select_n.42, bf16[1,8,2,16,384]{4,3,2,1,0:T(8,128)(2,1)S(1)} %bitcast.100, bf16[1,8,2,16,384]{4,3,2,1,0:T(8,128)(2,1)S(1)} %bitcast.98), kind=kOutput, calls=%fused_computation.5 | convolution fusion | flops 403275776 | bytes 3014660 | tf_op jit(solution)/shard_map/gxpf,fd->xgpd/dot_general | solution.py:130
  100.3 6.4 %collective-permute-start.1 = (bf16[8,2,16,2048]{3,2,0,1:T(8,128)(2,1)S(1)}, bf16[8,2,16,2048]{3,2,0,1:T(8,128)(2,1)S(1)}, u32[]{:S(2)}, u32[]{:S(2)}) collective-permute-start(bf16[8,2,16,2048]{3,2,0,1:T(8,128)(2,1)S(1)} %fusion.3), channel_id=1, source_target_pairs={{0,2},{2,0},{1,3},{3,1},{4,6},{6,4},{5,7},{7,5},{8,10},{10,8},{9,1... | collective-permute-start | bytes 3145736 | tf_op jit(solution)/shard_map/ppermute | solution.py:70
  106.7 0.1 select_bitcast_fusion.1
  106.9 0.2 maximum_bitcast_fusion
  107.1 0.2 copy.85
  107.3 1.2 copy-done
  108.5 1.3 fusion.4
  109.8 0.7 add_convert_fusion
  110.5 1.1 copy.82
  111.6 7.8 %all-to-all-start = ((bf16[16,16,2048]{2,1,0:T(8,128)(2,1)}), bf16[16,16,2048]{2,1,0:T(8,128)(2,1)S(1)}, u32[]{:S(2)}, u32[]{:S(2)}) async-start(bf16[16,16,2048]{2,1,0:T(8,128)(2,1)} %bitcast.19), calls=%async_computation | async-start | bytes 2097152 | tf_op jit(solution)/shard_map/all_to_all | solution.py:110
  119.4 3.3 %collective-permute-start.3 = (f32[256,384]{1,0:T(8,128)S(1)}, f32[256,384]{1,0:T(8,128)S(1)}, u32[]{:S(2)}, u32[]{:S(2)}) collective-permute-start(f32[256,384]{1,0:T(8,128)S(1)} %dynamic-slice_bitcast_fusion), channel_id=1, source_target_pairs={{0,1},{1,0},{2,3},{3,2},{4,5},{5,4},{6,7},{7,6},{8,9},{9,8},{10,11... | collective-permute-start | bytes 1179656 | tf_op jit(solution)/shard_map/ppermute | solution.py:80
  122.7 9.6 %collective-permute-done.3 = f32[256,384]{1,0:T(8,128)S(1)} collective-permute-done((f32[256,384]{1,0:T(8,128)S(1)}, f32[256,384]{1,0:T(8,128)S(1)}, u32[]{:S(2)}, u32[]{:S(2)}) %collective-permute-start.3) | collective-permute-done | bytes 393248 | tf_op jit(solution)/shard_map/ppermute | solution.py:80
  132.3 0.1 copy.86
  132.4 1.3 multiply_reduce_fusion
  133.7 0.1 multiply_convert_fusion
  133.9 0.3 convolution_multiply_fusion.2
  134.2 0.9 copy.93
  135.1 0.2 convolution_multiply_fusion.1
  135.3 0.9 copy.92
  136.2 0.6 fusion.19
  136.9 0.9 copy.94
  137.8 7.9 %all-to-all-done = bf16[16,16,2048]{2,1,0:T(8,128)(2,1)S(1)} async-done(((bf16[16,16,2048]{2,1,0:T(8,128)(2,1)}), bf16[16,16,2048]{2,1,0:T(8,128)(2,1)S(1)}, u32[]{:S(2)}, u32[]{:S(2)}) %all-to-all-start) | async-done | bytes 1048608 | tf_op jit(solution)/shard_map/all_to_all | solution.py:110
  145.6 0.2 reduce_sum.31
  145.8 0.2 reshape.126
  146.0 0.3 copy.83
  146.3 0.9 reshape.127
  (20 shorter events, 0.1 us)
Async XLA Ops:
  8.4 11.8 %copy-start.8 = (bf16[384,64]{0,1:T(8,128)(2,1)S(1)}, bf16[384,64]{0,1:T(8,128)(2,1)}, u32[]{:S(2)}) copy-start(bf16[384,64]{0,1:T(8,128)(2,1)} %param.8) | copy-start | bytes 147460
  8.7 34.2 %copy-start.5 = (bf16[1,256,384]{2,1,0:T(8,128)(2,1)S(1)}, bf16[1,256,384]{2,1,0:T(8,128)(2,1)}, u32[]{:S(2)}) copy-start(bf16[1,256,384]{2,1,0:T(8,128)(2,1)} %param.5) | copy-start | bytes 589828
  8.8 34.3 %copy-start.6 = (bf16[1,256,384]{2,1,0:T(8,128)(2,1)S(1)}, bf16[1,256,384]{2,1,0:T(8,128)(2,1)}, u32[]{:S(2)}) copy-start(bf16[1,256,384]{2,1,0:T(8,128)(2,1)} %param.6) | copy-start | bytes 589828
  9.9 41.6 %copy-start.7 = (bf16[1,256,384]{2,1,0:T(8,128)(2,1)S(1)}, bf16[1,256,384]{2,1,0:T(8,128)(2,1)}, u32[]{:S(2)}) copy-start(bf16[1,256,384]{2,1,0:T(8,128)(2,1)} %param.7) | copy-start | bytes 589828
  9.9 33.4 %all-to-all-start.1 = ((bf16[16,16,2048]{2,1,0:T(8,128)(2,1)}), bf16[16,16,2048]{2,1,0:T(8,128)(2,1)S(1)}, u32[]{:S(2)}, u32[]{:S(2)}) async-start(bf16[16,16,2048]{2,1,0:T(8,128)(2,1)} %bitcast.23), calls=%async_computation.1 | async-start | bytes 2097152 | tf_op jit(solution)/shard_map/all_to_all | solution.py:98
  20.1 78.0 %all-gather.2.cloned.1.call-start = ((), (), s32[]{:S(2)}) async-start(), calls=%async_computation.2 | async-start | bytes 1769472 | tf_op jit(solution)/shard_map/all_gather | solution.py:124
  43.1 11.4 %copy-start.1 = (bf16[1,256,384]{1,2,0:T(8,128)(2,1)}, bf16[1,256,384]{1,2,0:T(8,128)(2,1)S(1)}, u32[]{:S(2)}) copy-start(bf16[1,256,384]{1,2,0:T(8,128)(2,1)S(1)} %copy.72) | copy-start | bytes 589828
  43.2 11.3 %copy-start.3 = (bf16[1,256,384]{1,2,0:T(8,128)(2,1)}, bf16[1,256,384]{1,2,0:T(8,128)(2,1)S(1)}, u32[]{:S(2)}) copy-start(bf16[1,256,384]{1,2,0:T(8,128)(2,1)S(1)} %copy.73) | copy-start | bytes 589828
  43.2 63.5 %collective-permute-start.2 = (bf16[8,2,16,2048]{3,2,1,0:T(8,128)(2,1)S(1)}, bf16[8,2,16,2048]{3,2,1,0:T(8,128)(2,1)S(1)}, u32[]{:S(2)}, u32[]{:S(2)}) collective-permute-start(bf16[8,2,16,2048]{3,2,1,0:T(8,128)(2,1)S(1)} %bitcast.94), channel_id=1, source_target_pairs={{0,2},{2,0},{1,3},{3,1},{4,6},{6,4},{5,7},{7,5},{8,10},{10,8},{9,1... | collective-permute-start | bytes 3145736 | tf_op jit(solution)/shard_map/ppermute | solution.py:70
  55.6 8.5 %collective-permute-start = (bf16[256,384]{1,0:T(8,128)(2,1)S(1)}, bf16[256,384]{1,0:T(8,128)(2,1)}, u32[]{:S(2)}, u32[]{:S(2)}) collective-permute-start(bf16[256,384]{1,0:T(8,128)(2,1)S(1)} %copy.79), channel_id=1, source_target_pairs={{0,1},{1,0},{2,3},{3,2},{4,5},{5,4},{6,7},{7,6},{8,9},{9,8},{10,11... | collective-permute-start | bytes 589832 | tf_op jit(solution)/shard_map/ppermute | solution.py:80
  100.3 9.5 %collective-permute-start.1 = (bf16[8,2,16,2048]{3,2,0,1:T(8,128)(2,1)S(1)}, bf16[8,2,16,2048]{3,2,0,1:T(8,128)(2,1)S(1)}, u32[]{:S(2)}, u32[]{:S(2)}) collective-permute-start(bf16[8,2,16,2048]{3,2,0,1:T(8,128)(2,1)S(1)} %fusion.3), channel_id=1, source_target_pairs={{0,2},{2,0},{1,3},{3,1},{4,6},{6,4},{5,7},{7,5},{8,10},{10,8},{9,1... | collective-permute-start | bytes 3145736 | tf_op jit(solution)/shard_map/ppermute | solution.py:70
  107.1 1.4 copy-start
  111.6 34.0 %all-to-all-start = ((bf16[16,16,2048]{2,1,0:T(8,128)(2,1)}), bf16[16,16,2048]{2,1,0:T(8,128)(2,1)S(1)}, u32[]{:S(2)}, u32[]{:S(2)}) async-start(bf16[16,16,2048]{2,1,0:T(8,128)(2,1)} %bitcast.19), calls=%async_computation | async-start | bytes 2097152 | tf_op jit(solution)/shard_map/all_to_all | solution.py:110
  119.4 12.8 %collective-permute-start.3 = (f32[256,384]{1,0:T(8,128)S(1)}, f32[256,384]{1,0:T(8,128)S(1)}, u32[]{:S(2)}, u32[]{:S(2)}) collective-permute-start(f32[256,384]{1,0:T(8,128)S(1)} %dynamic-slice_bitcast_fusion), channel_id=1, source_target_pairs={{0,1},{1,0},{2,3},{3,2},{4,5},{5,4},{6,7},{7,6},{8,9},{9,8},{10,11... | collective-permute-start | bytes 1179656 | tf_op jit(solution)/shard_map/ppermute | solution.py:80
  132.4 1.4 copy-start.2
  133.7 1.4 copy-start.4
Sparse Core Ops, SparseCore 0:
  43.0 55.0 all-gather.1

commit v11 on v8

--- a/solution.py
+++ b/solution.py
@@ -115,6 +115,24 @@
     return received.astype(jnp.float32).sum(axis=0).astype(jnp.bfloat16)
 
 
+def ring_gather_columns(block, axis):
+    count = lax.axis_size(axis)
+    ahead = [(i, (i + 1) % count) for i in range(count)]
+    behind = [(i, (i - 1) % count) for i in range(count)]
+    before, after = [], []
+    from_behind = from_ahead = block
+    for step in range(count // 2):
+        from_behind = lax.ppermute(from_behind, axis, ahead)
+        before.append(from_behind)
+        if step < (count - 1) // 2:
+            from_ahead = lax.ppermute(from_ahead, axis, behind)
+            after.append(from_ahead)
+    ordered = jnp.stack(before[::-1] + [block] + after, axis=0)
+    shift = lax.axis_index(axis) - count // 2
+    placed = jnp.roll(ordered, shift, axis=0)
+    return placed.transpose(1, 0, 2).reshape(block.shape[0], -1)
+
+
 def on_device(queries, key_rows, value_rows, projection, upstream):
     chips, ys = lax.axis_size("x"), lax.axis_size("y")
     zhs, zls = lax.axis_size("zh"), lax.axis_size("zl")
@@ -124,7 +142,7 @@
     patches, width = attended.shape[1], attended.shape[2]
     block = patches // (chips * 2)
     columns = lax.all_gather(projection, "zh", axis=1, tiled=True)
-    columns = lax.all_gather(columns, "y", axis=1, tiled=True)
+    columns = ring_gather_columns(columns, "y")
     span = columns.shape[1]
     group = in_pair_order(attended[0], swap_pair(attended[0]))
     tokens = group.reshape(zls, chips, 2, block, width)

time: 138 us -> 137 us (level)
  the two profiles are of different devices: /device:TPU:1 before, /device:TPU:52 now
where the time goes in v11:
time: 137 us; the launch traced here: 136 us
  starting transfers between devices  53.6 us (39%)
  waiting for transfers between devices  28.9 us (21%)
  blocking collectives  25.1 us (18%)
  local copies, waits for them, and re-layouts  16.3 us (12%)
  matrix products  5.69 us (4%)
  other arithmetic  5.43 us (4%)
    all_gather x1, blocking collectives, on_device(): columns = lax.all_gather(projection, 'zh', axis=1, tiled=True)  25.1 us
    ppermute x4, starting transfers between devices, ring_gather_columns(): from_behind = lax.ppermute(from_behind, axis, ahead)  20.8 us
    ppermute x2, waiting for transfers between devices, swap_pair(): return lax.ppermute(block, 'zl', [(0, 1), (1, 0)])  19.3 us
    unnamed x37, local copies, waits for them, and re-layouts  8.17 us
    all_to_all x1, starting transfers between devices, sum_patch_blocks(): received = lax.all_to_all(pair, ('x', 'zl'), 0, 0, tiled=False)  8.13 us
    ppermute x2, starting transfers between devices, swap_pair(): return lax.ppermute(block, 'zl', [(0, 1), (1, 0)])  7.33 us
    all_to_all x1, starting transfers between devices, gather_patch_blocks(): lax.all_to_all(copies.reshape(chips * pairs, *pieces.shape[1:]), ('x', 'z...  7.28 us
    ppermute x3, waiting for transfers between devices, ring_gather_columns(): from_ahead = lax.ppermute(from_ahead, axis, behind)  6.56 us
  transfers between devices with their start and end apart: 13, of which 4 were waited for; matrix products, arithmetic and copies ran while one was open for 18% of the time, Pallas kernels for 0%

profile of v11, /device:TPU:52, one launch (start us, length us, event | category | flops | bytes accessed | tf_op | source)
XLA Modules:
  0.0 136.1 jit_solution(4107331548188545285)
XLA Ops:
  0.6 25.1 %all_gather.3 = bf16[384,256]{0,1:T(8,128)(2,1)S(1)} all-gather(bf16[384,64]{0,1:T(8,128)(2,1)} %param.8), channel_id=1, replica_groups=mesh['zh'=4,'y'=8,'x'=8,'c'=2,'zl'=2] {'zh'}, dimensions={1}, use_global_device_ids=true | all-gather | bytes 245760 | tf_op jit(solution)/shard_map/all_gather | solution.py:144
  25.7 4.9 %collective-permute-start = (bf16[384,256]{0,1:T(8,128)(2,1)S(1)}, bf16[384,256]{0,1:T(8,128)(2,1)S(1)}, u32[]{:S(2)}, u32[]{:S(2)}) collective-permute-start(bf16[384,256]{0,1:T(8,128)(2,1)S(1)} %all_gather.3), channel_id=1, source_target_pairs={{0,32},{32,64},{64,96},{96,128},{128,160},{160,192},{192,224},{224... | collective-permute-start | bytes 589832 | tf_op jit(solution)/shard_map/ppermute | solution.py:125
  30.6 1.9 %collective-permute-start.4 = (bf16[384,256]{0,1:T(8,128)(2,1)S(1)}, bf16[384,256]{0,1:T(8,128)(2,1)S(1)}, u32[]{:S(2)}, u32[]{:S(2)}) collective-permute-start(bf16[384,256]{0,1:T(8,128)(2,1)S(1)} %all_gather.3), channel_id=1, source_target_pairs={{0,224},{32,0},{64,32},{96,64},{128,96},{160,128},{192,160},{224,1... | collective-permute-start | bytes 589832 | tf_op jit(solution)/shard_map/ppermute | solution.py:128
  32.6 1.1 copy.54
  33.7 1.1 copy.50
  34.8 1.1 copy.51
  35.9 1.3 fusion.14
  37.2 5.1 %collective-permute-start.1 = (bf16[384,256]{0,1:T(8,128)(2,1)S(1)}, bf16[384,256]{0,1:T(8,128)(2,1)S(1)}, u32[]{:S(2)}, u32[]{:S(2)}) collective-permute-start(bf16[384,256]{0,1:T(8,128)(2,1)S(1)} %collective-permute-done), channel_id=1, source_target_pairs={{0,32},{32,64},{64,96},{96,128},{128,160},{160,192},{192,224},{224... | collective-permute-start | bytes 589832 | tf_op jit(solution)/shard_map/ppermute | solution.py:125
  42.3 0.6 convolution_convert_fusion.1
  42.9 2.6 %collective-permute-done.1 = bf16[384,256]{0,1:T(8,128)(2,1)S(1)} collective-permute-done((bf16[384,256]{0,1:T(8,128)(2,1)S(1)}, bf16[384,256]{0,1:T(8,128)(2,1)S(1)}, u32[]{:S(2)}, u32[]{:S(2)}) %collective-permute-start.1) | collective-permute-done | bytes 196640 | tf_op jit(solution)/shard_map/ppermute | solution.py:125
  45.5 5.6 %collective-permute-start.2 = (bf16[384,256]{0,1:T(8,128)(2,1)S(1)}, bf16[384,256]{0,1:T(8,128)(2,1)S(1)}, u32[]{:S(2)}, u32[]{:S(2)}) collective-permute-start(bf16[384,256]{0,1:T(8,128)(2,1)S(1)} %collective-permute-done.1), channel_id=1, source_target_pairs={{0,32},{32,64},{64,96},{96,128},{128,160},{160,192},{192,224},{224... | collective-permute-start | bytes 589832 | tf_op jit(solution)/shard_map/ppermute | solution.py:125
  51.1 4.0 %collective-permute-start.7 = (bf16[256,384]{0,1:T(8,128)(2,1)S(1)}, bf16[256,384]{0,1:T(8,128)(2,1)}, u32[]{:S(2)}, u32[]{:S(2)}) collective-permute-start(bf16[256,384]{0,1:T(8,128)(2,1)S(1)} %bitcast.150), channel_id=1, source_target_pairs={{0,1},{1,0},{2,3},{3,2},{4,5},{5,4},{6,7},{7,6},{8,9},{9,8},{10,11... | collective-permute-start | bytes 589832 | tf_op jit(solution)/shard_map/ppermute | solution.py:80
  55.1 0.2 reshape_squeeze.3
  55.4 0.3 broadcast_in_dim.4
  55.7 1.1 broadcast_in_dim.5
  56.8 7.3 %all-to-all-start.1 = ((bf16[16,16,2048]{2,1,0:T(8,128)(2,1)}), bf16[16,16,2048]{2,1,0:T(8,128)(2,1)S(1)}, u32[]{:S(2)}, u32[]{:S(2)}) async-start(bf16[16,16,2048]{2,1,0:T(8,128)(2,1)} %bitcast.34), calls=%async_computation.1 | async-start | bytes 2097152 | tf_op jit(solution)/shard_map/all_to_all | solution.py:98
  64.1 1.9 %collective-permute-start.5 = (bf16[384,256]{0,1:T(8,128)(2,1)S(1)}, bf16[384,256]{0,1:T(8,128)(2,1)S(1)}, u32[]{:S(2)}, u32[]{:S(2)}) collective-permute-start(bf16[384,256]{0,1:T(8,128)(2,1)S(1)} %collective-permute-done.4), channel_id=1, source_target_pairs={{0,224},{32,0},{64,32},{96,64},{128,96},{160,128},{192,160},{224,1... | collective-permute-start | bytes 589832 | tf_op jit(solution)/shard_map/ppermute | solution.py:128
  66.0 5.1 %collective-permute-start.3 = (bf16[384,256]{0,1:T(8,128)(2,1)S(1)}, bf16[384,256]{0,1:T(8,128)(2,1)S(1)}, u32[]{:S(2)}, u32[]{:S(2)}) collective-permute-start(bf16[384,256]{0,1:T(8,128)(2,1)S(1)} %collective-permute-done.2), channel_id=1, source_target_pairs={{0,32},{32,64},{64,96},{96,128},{128,160},{160,192},{192,224},{224... | collective-permute-start | bytes 589832 | tf_op jit(solution)/shard_map/ppermute | solution.py:125
  71.2 1.0 broadcast_select_fusion.1
  72.1 0.8 copy.57
  73.0 0.8 copy.56
  73.8 1.9 %collective-permute-start.6 = (bf16[384,256]{0,1:T(8,128)(2,1)S(1)}, bf16[384,256]{0,1:T(8,128)(2,1)S(1)}, u32[]{:S(2)}, u32[]{:S(2)}) collective-permute-start(bf16[384,256]{0,1:T(8,128)(2,1)S(1)} %collective-permute-done.5), channel_id=1, source_target_pairs={{0,224},{32,0},{64,32},{96,64},{128,96},{160,128},{192,160},{224,1... | collective-permute-start | bytes 589832 | tf_op jit(solution)/shard_map/ppermute | solution.py:128
  76.0 6.6 %collective-permute-done.6 = bf16[384,256]{0,1:T(8,128)(2,1)S(1)} collective-permute-done((bf16[384,256]{0,1:T(8,128)(2,1)S(1)}, bf16[384,256]{0,1:T(8,128)(2,1)S(1)}, u32[]{:S(2)}, u32[]{:S(2)}) %collective-permute-start.6) | collective-permute-done | bytes 196640 | tf_op jit(solution)/shard_map/ppermute | solution.py:128
  83.1 0.4 copy-done.5
  83.6 1.3 convolution_convert_fusion
  84.9 1.1 dynamic-slice_bitcast_fusion
  86.0 1.9 %collective-permute-start.8 = (bf16[8,2,16,2048]{3,2,0,1:T(8,128)(2,1)}, bf16[8,2,16,2048]{3,2,0,1:T(8,128)(2,1)}, u32[]{:S(2)}, u32[]{:S(2)}) collective-permute-start(bf16[8,2,16,2048]{3,2,0,1:T(8,128)(2,1)} %dynamic-slice_bitcast_fusion), channel_id=1, source_target_pairs={{0,2},{2,0},{1,3},{3,1},{4,6},{6,4},{5,7},{7,5},{8,10},{10,8},{9,1... | collective-permute-start | bytes 3145736 | tf_op jit(solution)/shard_map/ppermute | solution.py:70
  87.9 2.4 %collective-permute-start.9 = (bf16[8,2,16,2048]{3,2,1,0:T(8,128)(2,1)S(1)}, bf16[8,2,16,2048]{3,2,1,0:T(8,128)(2,1)}, u32[]{:S(2)}, u32[]{:S(2)}) collective-permute-start(bf16[8,2,16,2048]{3,2,1,0:T(8,128)(2,1)S(1)} %bitcast.125), channel_id=1, source_target_pairs={{0,2},{2,0},{1,3},{3,1},{4,6},{6,4},{5,7},{7,5},{8,10},{10,8},{9,1... | collective-permute-start | bytes 3145736 | tf_op jit(solution)/shard_map/ppermute | solution.py:70
  90.3 0.5 collective-permute-done.8
  90.8 1.6 %fusion.1 = bf16[8,2,16,2048]{3,2,0,1:T(8,128)(2,1)S(1)} fusion(bf16[8,2,16,2048]{3,2,0,1:T(8,128)(2,1)} %collective-permute-done.8, bf16[2048,2,8,2,16]{0,4,3,2,1:T(8,128)(2,1)S(1)} %convolution_convert_fusion, s32[]{:T(128)S(6)} %select_n.56), kind=kLoop, calls=%fused_computation.4 | loop fusion | flops 2097152 | bytes 3145732 | tf_op jit(solution)/shard_map/convert_element_type | solution.py:111
  92.5 1.0 copy.59
  93.5 8.1 %all-to-all-start = ((bf16[16,16,2048]{2,1,0:T(8,128)(2,1)}), bf16[16,16,2048]{2,1,0:T(8,128)(2,1)S(1)}, u32[]{:S(2)}, u32[]{:S(2)}) async-start(bf16[16,16,2048]{2,1,0:T(8,128)(2,1)} %bitcast.28), calls=%async_computation | async-start | bytes 2097152 | tf_op jit(solution)/shard_map/all_to_all | solution.py:113
  101.6 1.4 %select_bitcast_fusion.1 = (bf16[8,1,2,16,2048]{4,3,2,0,1:T(8,128)(2,1)S(1)}, bf16[8,1,2,16,2048]{4,3,2,0,1:T(8,128)(2,1)S(1)}) fusion(bf16[8,2,16,2048]{3,2,1,0:T(8,128)(2,1)S(1)} %bitcast.126, bf16[8,2,16,2048]{3,2,1,0:T(8,128)(2,1)} %collective-permute-done.9, pred[]{:T(512)S(6)} %eq.10), kind=kLoop, calls=%fused_computation.12 | loop fusion | flops 1048576 | bytes 4194305 | tf_op jit(solution)/shard_map/stack | solution.py:102
  103.5 1.2 copy-done.1
  104.6 1.0 fusion.15
  105.6 0.8 dynamic-slice_bitcast_fusion.1
  106.4 3.4 %collective-permute-start.10 = (f32[256,384]{0,1:T(8,128)}, f32[256,384]{0,1:T(8,128)}, u32[]{:S(2)}, u32[]{:S(2)}) collective-permute-start(f32[256,384]{0,1:T(8,128)} %dynamic-slice_bitcast_fusion.1), channel_id=1, source_target_pairs={{0,1},{1,0},{2,3},{3,2},{4,5},{5,4},{6,7},{7,6},{8,9},{9,8},{10,11... | collective-permute-start | bytes 1179656 | tf_op jit(solution)/shard_map/ppermute | solution.py:80
  109.8 19.3 %collective-permute-done.10 = f32[256,384]{0,1:T(8,128)} collective-permute-done((f32[256,384]{0,1:T(8,128)}, f32[256,384]{0,1:T(8,128)}, u32[]{:S(2)}, u32[]{:S(2)}) %collective-permute-start.10) | collective-permute-done | bytes 393248 | tf_op jit(solution)/shard_map/ppermute | solution.py:80
  129.1 1.0 fusion.7
  130.1 0.3 multiply_reduce_fusion
  130.8 0.9 copy.68
  131.7 0.3 convolution_multiply_fusion.2
  132.0 0.9 copy.69
  132.9 0.6 fusion.8
  133.6 0.9 copy.70
  134.6 0.2 reshape.128
  134.9 0.3 copy.60
  135.1 0.9 reshape.129
  (46 shorter events, 1.9 us)
Async XLA Ops:
  25.7 29.4 %copy-start.7 = (bf16[16,1,4096]{2,0,1:T(8,128)(2,1)S(1)}, bf16[16,1,4096]{2,0,1:T(8,128)(2,1)}, u32[]{:S(2)}) copy-start(bf16[16,1,4096]{2,0,1:T(8,128)(2,1)} %param.9) | copy-start | bytes 393220
  25.7 11.5 %collective-permute-start = (bf16[384,256]{0,1:T(8,128)(2,1)S(1)}, bf16[384,256]{0,1:T(8,128)(2,1)S(1)}, u32[]{:S(2)}, u32[]{:S(2)}) collective-permute-start(bf16[384,256]{0,1:T(8,128)(2,1)S(1)} %all_gather.3), channel_id=1, source_target_pairs={{0,32},{32,64},{64,96},{96,128},{128,160},{160,192},{192,224},{224... | collective-permute-start | bytes 589832 | tf_op jit(solution)/shard_map/ppermute | solution.py:125
  30.6 33.4 %collective-permute-start.4 = (bf16[384,256]{0,1:T(8,128)(2,1)S(1)}, bf16[384,256]{0,1:T(8,128)(2,1)S(1)}, u32[]{:S(2)}, u32[]{:S(2)}) collective-permute-start(bf16[384,256]{0,1:T(8,128)(2,1)S(1)} %all_gather.3), channel_id=1, source_target_pairs={{0,224},{32,0},{64,32},{96,64},{128,96},{160,128},{192,160},{224,1... | collective-permute-start | bytes 589832 | tf_op jit(solution)/shard_map/ppermute | solution.py:128
  33.6 21.4 %copy-start.3 = (bf16[1,256,384]{1,2,0:T(8,128)(2,1)}, bf16[1,256,384]{1,2,0:T(8,128)(2,1)S(1)}, u32[]{:S(2)}) copy-start(bf16[1,256,384]{1,2,0:T(8,128)(2,1)S(1)} %copy.54) | copy-start | bytes 589828
  37.2 8.3 %collective-permute-start.1 = (bf16[384,256]{0,1:T(8,128)(2,1)S(1)}, bf16[384,256]{0,1:T(8,128)(2,1)S(1)}, u32[]{:S(2)}, u32[]{:S(2)}) collective-permute-start(bf16[384,256]{0,1:T(8,128)(2,1)S(1)} %collective-permute-done), channel_id=1, source_target_pairs={{0,32},{32,64},{64,96},{96,128},{128,160},{160,192},{192,224},{224... | collective-permute-start | bytes 589832 | tf_op jit(solution)/shard_map/ppermute | solution.py:125
  45.5 20.5 %collective-permute-start.2 = (bf16[384,256]{0,1:T(8,128)(2,1)S(1)}, bf16[384,256]{0,1:T(8,128)(2,1)S(1)}, u32[]{:S(2)}, u32[]{:S(2)}) collective-permute-start(bf16[384,256]{0,1:T(8,128)(2,1)S(1)} %collective-permute-done.1), channel_id=1, source_target_pairs={{0,32},{32,64},{64,96},{96,128},{128,160},{160,192},{192,224},{224... | collective-permute-start | bytes 589832 | tf_op jit(solution)/shard_map/ppermute | solution.py:125
  51.1 20.1 %collective-permute-start.7 = (bf16[256,384]{0,1:T(8,128)(2,1)S(1)}, bf16[256,384]{0,1:T(8,128)(2,1)}, u32[]{:S(2)}, u32[]{:S(2)}) collective-permute-start(bf16[256,384]{0,1:T(8,128)(2,1)S(1)} %bitcast.150), channel_id=1, source_target_pairs={{0,1},{1,0},{2,3},{3,2},{4,5},{5,4},{6,7},{7,6},{8,9},{9,8},{10,11... | collective-permute-start | bytes 589832 | tf_op jit(solution)/shard_map/ppermute | solution.py:80
  56.8 31.1 %all-to-all-start.1 = ((bf16[16,16,2048]{2,1,0:T(8,128)(2,1)}), bf16[16,16,2048]{2,1,0:T(8,128)(2,1)S(1)}, u32[]{:S(2)}, u32[]{:S(2)}) async-start(bf16[16,16,2048]{2,1,0:T(8,128)(2,1)} %bitcast.34), calls=%async_computation.1 | async-start | bytes 2097152 | tf_op jit(solution)/shard_map/all_to_all | solution.py:98
  64.1 9.7 %collective-permute-start.5 = (bf16[384,256]{0,1:T(8,128)(2,1)S(1)}, bf16[384,256]{0,1:T(8,128)(2,1)S(1)}, u32[]{:S(2)}, u32[]{:S(2)}) collective-permute-start(bf16[384,256]{0,1:T(8,128)(2,1)S(1)} %collective-permute-done.4), channel_id=1, source_target_pairs={{0,224},{32,0},{64,32},{96,64},{128,96},{160,128},{192,160},{224,1... | collective-permute-start | bytes 589832 | tf_op jit(solution)/shard_map/ppermute | solution.py:128
  66.0 9.7 %collective-permute-start.3 = (bf16[384,256]{0,1:T(8,128)(2,1)S(1)}, bf16[384,256]{0,1:T(8,128)(2,1)S(1)}, u32[]{:S(2)}, u32[]{:S(2)}) collective-permute-start(bf16[384,256]{0,1:T(8,128)(2,1)S(1)} %collective-permute-done.2), channel_id=1, source_target_pairs={{0,32},{32,64},{64,96},{96,128},{128,160},{160,192},{192,224},{224... | collective-permute-start | bytes 589832 | tf_op jit(solution)/shard_map/ppermute | solution.py:125
  73.8 8.8 %collective-permute-start.6 = (bf16[384,256]{0,1:T(8,128)(2,1)S(1)}, bf16[384,256]{0,1:T(8,128)(2,1)S(1)}, u32[]{:S(2)}, u32[]{:S(2)}) collective-permute-start(bf16[384,256]{0,1:T(8,128)(2,1)S(1)} %collective-permute-done.5), channel_id=1, source_target_pairs={{0,224},{32,0},{64,32},{96,64},{128,96},{160,128},{192,160},{224,1... | collective-permute-start | bytes 589832 | tf_op jit(solution)/shard_map/ppermute | solution.py:128
  82.6 0.9 copy-start.5
  82.6 1.0 copy-start.6
  83.1 1.8 %copy-start = (bf16[8,384,256]{1,2,0:T(8,128)(2,1)}, bf16[8,384,256]{1,2,0:T(8,128)(2,1)S(1)}, u32[]{:S(2)}) copy-start(bf16[8,384,256]{1,2,0:T(8,128)(2,1)S(1)} %constant_dynamic-slice_fusion) | copy-start | bytes 4718596
  86.0 4.9 %collective-permute-start.8 = (bf16[8,2,16,2048]{3,2,0,1:T(8,128)(2,1)}, bf16[8,2,16,2048]{3,2,0,1:T(8,128)(2,1)}, u32[]{:S(2)}, u32[]{:S(2)}) collective-permute-start(bf16[8,2,16,2048]{3,2,0,1:T(8,128)(2,1)} %dynamic-slice_bitcast_fusion), channel_id=1, source_target_pairs={{0,2},{2,0},{1,3},{3,1},{4,6},{6,4},{5,7},{7,5},{8,10},{10,8},{9,1... | collective-permute-start | bytes 3145736 | tf_op jit(solution)/shard_map/ppermute | solution.py:70
  87.9 13.7 %collective-permute-start.9 = (bf16[8,2,16,2048]{3,2,1,0:T(8,128)(2,1)S(1)}, bf16[8,2,16,2048]{3,2,1,0:T(8,128)(2,1)}, u32[]{:S(2)}, u32[]{:S(2)}) collective-permute-start(bf16[8,2,16,2048]{3,2,1,0:T(8,128)(2,1)S(1)} %bitcast.125), channel_id=1, source_target_pairs={{0,2},{2,0},{1,3},{3,1},{4,6},{6,4},{5,7},{7,5},{8,10},{10,8},{9,1... | collective-permute-start | bytes 3145736 | tf_op jit(solution)/shard_map/ppermute | solution.py:70
  93.5 41.0 %all-to-all-start = ((bf16[16,16,2048]{2,1,0:T(8,128)(2,1)}), bf16[16,16,2048]{2,1,0:T(8,128)(2,1)S(1)}, u32[]{:S(2)}, u32[]{:S(2)}) async-start(bf16[16,16,2048]{2,1,0:T(8,128)(2,1)} %bitcast.28), calls=%async_computation | async-start | bytes 2097152 | tf_op jit(solution)/shard_map/all_to_all | solution.py:113
  103.2 1.4 %copy-start.1 = (bf16[8,384,256]{1,2,0:T(8,128)(2,1)S(1)}, bf16[8,384,256]{1,2,0:T(8,128)(2,1)}, u32[]{:S(2)}) copy-start(bf16[8,384,256]{1,2,0:T(8,128)(2,1)} %copy-done) | copy-start | bytes 4718596
  104.6 25.5 %copy-start.2 = (f32[3,256,256]{1,2,0:T(8,128)S(1)}, f32[3,256,256]{1,2,0:T(8,128)}, u32[]{:S(2)}) copy-start(f32[3,256,256]{1,2,0:T(8,128)} %get-tuple-element.21) | copy-start | bytes 2359300
  104.6 25.5 %copy-start.4 = (bf16[1,256,384]{1,2,0:T(8,128)(2,1)S(1)}, bf16[1,256,384]{1,2,0:T(8,128)(2,1)}, u32[]{:S(2)}) copy-start(bf16[1,256,384]{1,2,0:T(8,128)(2,1)} %copy-done.3) | copy-start | bytes 589828
  106.4 22.6 %collective-permute-start.10 = (f32[256,384]{0,1:T(8,128)}, f32[256,384]{0,1:T(8,128)}, u32[]{:S(2)}, u32[]{:S(2)}) collective-permute-start(f32[256,384]{0,1:T(8,128)} %dynamic-slice_bitcast_fusion.1), channel_id=1, source_target_pairs={{0,1},{1,0},{2,3},{3,2},{4,5},{5,4},{6,7},{7,6},{8,9},{9,8},{10,11... | collective-permute-start | bytes 1179656 | tf_op jit(solution)/shard_map/ppermute | solution.py:80

commit v12 on v11

--- a/solution.py
+++ b/solution.py
@@ -141,7 +141,7 @@
     attended = attend_values(soft, value_rows, head_count)
     patches, width = attended.shape[1], attended.shape[2]
     block = patches // (chips * 2)
-    columns = lax.all_gather(projection, "zh", axis=1, tiled=True)
+    columns = ring_gather_columns(projection, "zh")
     columns = ring_gather_columns(columns, "y")
     span = columns.shape[1]
     group = in_pair_order(attended[0], swap_pair(attended[0]))

time: 137 us -> 137 us (level)
  the two profiles are of different devices: /device:TPU:52 before, /device:TPU:1 now
where the time goes in v12:
time: 137 us; the launch traced here: 135 us
  starting transfers between devices  72 us (53%)
  waiting for transfers between devices  31.5 us (23%)
  local copies, waits for them, and re-layouts  18.6 us (14%)
  matrix products  5.68 us (4%)
  other arithmetic  5.53 us (4%)
    ppermute x4, starting transfers between devices, ring_gather_columns(): from_ahead = lax.ppermute(from_ahead, axis, behind)  19.5 us
    ppermute x6, starting transfers between devices, ring_gather_columns(): from_behind = lax.ppermute(from_behind, axis, ahead)  19.4 us
    ppermute x2, waiting for transfers between devices, swap_pair(): return lax.ppermute(block, 'zl', [(0, 1), (1, 0)])  18 us
    ppermute x2, starting transfers between devices, swap_cores(): return lax.ppermute(block, 'c', [(0, 1), (1, 0)])  14.2 us
    ppermute x6, waiting for transfers between devices, ring_gather_columns(): from_behind = lax.ppermute(from_behind, axis, ahead)  12.8 us
    unnamed x46, local copies, waits for them, and re-layouts  9.86 us
    ppermute x2, starting transfers between devices, swap_pair(): return lax.ppermute(block, 'zl', [(0, 1), (1, 0)])  8.67 us
    all_to_all x1, starting transfers between devices, gather_patch_blocks(): lax.all_to_all(copies.reshape(chips * pairs, *pieces.shape[1:]), ('x', 'z...  6.58 us
  transfers between devices with their start and end apart: 16, of which 4 were waited for; matrix products, arithmetic and copies ran while one was open for 19% of the time, Pallas kernels for 0%

profile of v12, /device:TPU:1, one launch (start us, length us, event | category | flops | bytes accessed | tf_op | source)
XLA Modules:
  0.0 134.7 jit_solution(11085986703137671449)
XLA Ops:
  0.6 8.5 %collective-permute-start = (bf16[384,64]{0,1:T(8,128)(2,1)}, bf16[384,64]{0,1:T(8,128)(2,1)S(1)}, u32[]{:S(2)}, u32[]{:S(2)}) collective-permute-start(bf16[384,64]{0,1:T(8,128)(2,1)} %param.8), channel_id=1, source_target_pairs={{0,256},{256,512},{512,768},{768,0},{1,257},{257,513},{513,769},{7... | collective-permute-start | bytes 147464 | tf_op jit(solution)/shard_map/ppermute | solution.py:125
  9.1 10.2 %collective-permute-done = bf16[384,64]{0,1:T(8,128)(2,1)S(1)} collective-permute-done((bf16[384,64]{0,1:T(8,128)(2,1)}, bf16[384,64]{0,1:T(8,128)(2,1)S(1)}, u32[]{:S(2)}, u32[]{:S(2)}) %collective-permute-start) | collective-permute-done | bytes 49184 | tf_op jit(solution)/shard_map/ppermute | solution.py:125
  19.3 1.9 %collective-permute-start.1 = (bf16[384,64]{0,1:T(8,128)(2,1)S(1)}, bf16[384,64]{0,1:T(8,128)(2,1)S(1)}, u32[]{:S(2)}, u32[]{:S(2)}) collective-permute-start(bf16[384,64]{0,1:T(8,128)(2,1)S(1)} %collective-permute-done), channel_id=1, source_target_pairs={{0,256},{256,512},{512,768},{768,0},{1,257},{257,513},{513,769},{7... | collective-permute-start | bytes 147464 | tf_op jit(solution)/shard_map/ppermute | solution.py:125
  21.2 5.5 %collective-permute-start.2 = (bf16[384,64]{0,1:T(8,128)(2,1)}, bf16[384,64]{0,1:T(8,128)(2,1)S(1)}, u32[]{:S(2)}, u32[]{:S(2)}) collective-permute-start(bf16[384,64]{0,1:T(8,128)(2,1)} %param.8), channel_id=1, source_target_pairs={{0,768},{256,0},{512,256},{768,512},{1,769},{257,1},{513,257},{769... | collective-permute-start | bytes 147464 | tf_op jit(solution)/shard_map/ppermute | solution.py:128
  26.7 1.1 copy.71
  27.7 1.1 copy.72
  28.8 1.1 copy.75
  30.0 0.9 constant_dynamic-update-slice_fusion.5
  30.9 0.8 constant_dynamic-update-slice_fusion.1
  31.8 3.3 %collective-permute-start.3 = (bf16[384,256]{0,1:T(8,128)(2,1)S(1)}, bf16[384,256]{0,1:T(8,128)(2,1)S(1)}, u32[]{:S(2)}, u32[]{:S(2)}) collective-permute-start(bf16[384,256]{0,1:T(8,128)(2,1)S(1)} %bitcast.143), channel_id=1, source_target_pairs={{0,32},{32,64},{64,96},{96,128},{128,160},{160,192},{192,224},{224... | collective-permute-start | bytes 589832 | tf_op jit(solution)/shard_map/ppermute | solution.py:125
  35.1 1.3 fusion.14
  36.4 4.5 %collective-permute-start.7 = (bf16[384,256]{0,1:T(8,128)(2,1)S(1)}, bf16[384,256]{0,1:T(8,128)(2,1)S(1)}, u32[]{:S(2)}, u32[]{:S(2)}) collective-permute-start(bf16[384,256]{0,1:T(8,128)(2,1)S(1)} %bitcast.144), channel_id=1, source_target_pairs={{0,224},{32,0},{64,32},{96,64},{128,96},{160,128},{192,160},{224,1... | collective-permute-start | bytes 589832 | tf_op jit(solution)/shard_map/ppermute | solution.py:128
  40.9 1.9 %collective-permute-start.4 = (bf16[384,256]{0,1:T(8,128)(2,1)S(1)}, bf16[384,256]{0,1:T(8,128)(2,1)S(1)}, u32[]{:S(2)}, u32[]{:S(2)}) collective-permute-start(bf16[384,256]{0,1:T(8,128)(2,1)S(1)} %collective-permute-done.3), channel_id=1, source_target_pairs={{0,32},{32,64},{64,96},{96,128},{128,160},{160,192},{192,224},{224... | collective-permute-start | bytes 589832 | tf_op jit(solution)/shard_map/ppermute | solution.py:125
  42.8 0.6 convolution_convert_fusion.1
  43.5 5.0 %collective-permute-start.8 = (bf16[384,256]{0,1:T(8,128)(2,1)S(1)}, bf16[384,256]{0,1:T(8,128)(2,1)S(1)}, u32[]{:S(2)}, u32[]{:S(2)}) collective-permute-start(bf16[384,256]{0,1:T(8,128)(2,1)S(1)} %collective-permute-done.7), channel_id=1, source_target_pairs={{0,224},{32,0},{64,32},{96,64},{128,96},{160,128},{192,160},{224,1... | collective-permute-start | bytes 589832 | tf_op jit(solution)/shard_map/ppermute | solution.py:128
  48.5 1.9 %collective-permute-start.5 = (bf16[384,256]{0,1:T(8,128)(2,1)S(1)}, bf16[384,256]{0,1:T(8,128)(2,1)S(1)}, u32[]{:S(2)}, u32[]{:S(2)}) collective-permute-start(bf16[384,256]{0,1:T(8,128)(2,1)S(1)} %collective-permute-done.4), channel_id=1, source_target_pairs={{0,32},{32,64},{64,96},{96,128},{128,160},{160,192},{192,224},{224... | collective-permute-start | bytes 589832 | tf_op jit(solution)/shard_map/ppermute | solution.py:125
  50.5 5.5 %collective-permute-start.10 = (bf16[256,384]{0,1:T(8,128)(2,1)S(1)}, bf16[256,384]{0,1:T(8,128)(2,1)}, u32[]{:S(2)}, u32[]{:S(2)}) collective-permute-start(bf16[256,384]{0,1:T(8,128)(2,1)S(1)} %bitcast.170), channel_id=1, source_target_pairs={{0,1},{1,0},{2,3},{3,2},{4,5},{5,4},{6,7},{7,6},{8,9},{9,8},{10,11... | collective-permute-start | bytes 589832 | tf_op jit(solution)/shard_map/ppermute | solution.py:80
  56.6 1.1 broadcast_in_dim.5
  57.7 6.6 %all-to-all-start.1 = ((bf16[16,16,2048]{2,1,0:T(8,128)(2,1)}), bf16[16,16,2048]{2,1,0:T(8,128)(2,1)S(1)}, u32[]{:S(2)}, u32[]{:S(2)}) async-start(bf16[16,16,2048]{2,1,0:T(8,128)(2,1)} %bitcast.41), calls=%async_computation.1 | async-start | bytes 2097152 | tf_op jit(solution)/shard_map/all_to_all | solution.py:98
  64.4 4.6 %collective-permute-start.9 = (bf16[384,256]{0,1:T(8,128)(2,1)S(1)}, bf16[384,256]{0,1:T(8,128)(2,1)S(1)}, u32[]{:S(2)}, u32[]{:S(2)}) collective-permute-start(bf16[384,256]{0,1:T(8,128)(2,1)S(1)} %collective-permute-done.8), channel_id=1, source_target_pairs={{0,224},{32,0},{64,32},{96,64},{128,96},{160,128},{192,160},{224,1... | collective-permute-start | bytes 589832 | tf_op jit(solution)/shard_map/ppermute | solution.py:128
  69.0 1.9 %collective-permute-start.6 = (bf16[384,256]{0,1:T(8,128)(2,1)S(1)}, bf16[384,256]{0,1:T(8,128)(2,1)S(1)}, u32[]{:S(2)}, u32[]{:S(2)}) collective-permute-start(bf16[384,256]{0,1:T(8,128)(2,1)S(1)} %collective-permute-done.5), channel_id=1, source_target_pairs={{0,32},{32,64},{64,96},{96,128},{128,160},{160,192},{192,224},{224... | collective-permute-start | bytes 589832 | tf_op jit(solution)/shard_map/ppermute | solution.py:125
  70.9 1.1 broadcast_select_fusion.1
  72.0 0.8 copy.77
  72.8 0.8 copy.78
  74.3 2.6 %collective-permute-done.6 = bf16[384,256]{0,1:T(8,128)(2,1)S(1)} collective-permute-done((bf16[384,256]{0,1:T(8,128)(2,1)S(1)}, bf16[384,256]{0,1:T(8,128)(2,1)S(1)}, u32[]{:S(2)}, u32[]{:S(2)}) %collective-permute-start.6) | collective-permute-done | bytes 196640 | tf_op jit(solution)/shard_map/ppermute | solution.py:125
  77.7 0.4 copy-done.5
  78.2 1.3 convolution_convert_fusion
  79.5 1.1 dynamic-slice_bitcast_fusion
  80.6 7.0 %collective-permute-start.11 = (bf16[8,2,16,2048]{3,2,0,1:T(8,128)(2,1)}, bf16[8,2,16,2048]{3,2,0,1:T(8,128)(2,1)}, u32[]{:S(2)}, u32[]{:S(2)}) collective-permute-start(bf16[8,2,16,2048]{3,2,0,1:T(8,128)(2,1)} %dynamic-slice_bitcast_fusion), channel_id=1, source_target_pairs={{0,2},{2,0},{1,3},{3,1},{4,6},{6,4},{5,7},{7,5},{8,10},{10,8},{9,1... | collective-permute-start | bytes 3145736 | tf_op jit(solution)/shard_map/ppermute | solution.py:70
  87.6 0.6 all-to-all-done.1
  88.2 7.2 %collective-permute-start.12 = (bf16[8,2,16,2048]{3,2,1,0:T(8,128)(2,1)S(1)}, bf16[8,2,16,2048]{3,2,1,0:T(8,128)(2,1)}, u32[]{:S(2)}, u32[]{:S(2)}) collective-permute-start(bf16[8,2,16,2048]{3,2,1,0:T(8,128)(2,1)S(1)} %bitcast.139), channel_id=1, source_target_pairs={{0,2},{2,0},{1,3},{3,1},{4,6},{6,4},{5,7},{7,5},{8,10},{10,8},{9,1... | collective-permute-start | bytes 3145736 | tf_op jit(solution)/shard_map/ppermute | solution.py:70
  95.4 1.6 %fusion.1 = bf16[8,2,16,2048]{3,2,0,1:T(8,128)(2,1)S(1)} fusion(bf16[8,2,16,2048]{3,2,0,1:T(8,128)(2,1)} %collective-permute-done.11, bf16[2048,2,8,2,16]{0,4,3,2,1:T(8,128)(2,1)S(1)} %convolution_convert_fusion, s32[]{:T(128)S(6)} %select_n.68), kind=kLoop, calls=%fused_computation.4 | loop fusion | flops 2097152 | bytes 3145732 | tf_op jit(solution)/shard_map/convert_element_type | solution.py:111
  97.0 1.1 copy.80
  98.1 3.7 %all-to-all-start = ((bf16[16,16,2048]{2,1,0:T(8,128)(2,1)}), bf16[16,16,2048]{2,1,0:T(8,128)(2,1)S(1)}, u32[]{:S(2)}, u32[]{:S(2)}) async-start(bf16[16,16,2048]{2,1,0:T(8,128)(2,1)} %bitcast.35), calls=%async_computation | async-start | bytes 2097152 | tf_op jit(solution)/shard_map/all_to_all | solution.py:113
  101.7 1.4 %select_bitcast_fusion.1 = (bf16[8,1,2,16,2048]{4,3,2,0,1:T(8,128)(2,1)S(1)}, bf16[8,1,2,16,2048]{4,3,2,0,1:T(8,128)(2,1)S(1)}) fusion(bf16[8,2,16,2048]{3,2,1,0:T(8,128)(2,1)S(1)} %bitcast.140, bf16[8,2,16,2048]{3,2,1,0:T(8,128)(2,1)} %collective-permute-done.12, pred[]{:T(512)S(6)} %eq.12), kind=kLoop, calls=%fused_computation.12 | loop fusion | flops 1048576 | bytes 4194305 | tf_op jit(solution)/shard_map/stack | solution.py:102
  103.6 1.2 copy-done.1
  104.7 1.0 fusion.15
  105.8 0.8 dynamic-slice_bitcast_fusion.1
  106.5 3.1 %collective-permute-start.13 = (f32[256,384]{0,1:T(8,128)}, f32[256,384]{0,1:T(8,128)}, u32[]{:S(2)}, u32[]{:S(2)}) collective-permute-start(f32[256,384]{0,1:T(8,128)} %dynamic-slice_bitcast_fusion.1), channel_id=1, source_target_pairs={{0,1},{1,0},{2,3},{3,2},{4,5},{5,4},{6,7},{7,6},{8,9},{9,8},{10,11... | collective-permute-start | bytes 1179656 | tf_op jit(solution)/shard_map/ppermute | solution.py:80
  109.7 18.0 %collective-permute-done.13 = f32[256,384]{0,1:T(8,128)} collective-permute-done((f32[256,384]{0,1:T(8,128)}, f32[256,384]{0,1:T(8,128)}, u32[]{:S(2)}, u32[]{:S(2)}) %collective-permute-start.13) | collective-permute-done | bytes 393248 | tf_op jit(solution)/shard_map/ppermute | solution.py:80
  127.7 1.0 fusion.7
  128.8 0.6 fusion.8
  129.4 0.9 copy.91
  130.3 0.3 multiply_reduce_fusion
  130.8 0.3 convolution_multiply_fusion.2
  131.0 0.9 copy.90
  132.2 0.9 copy.89
  133.8 0.9 reshape.133
  (66 shorter events, 3.6 us)
Async XLA Ops:
  0.6 18.6 %collective-permute-start = (bf16[384,64]{0,1:T(8,128)(2,1)}, bf16[384,64]{0,1:T(8,128)(2,1)S(1)}, u32[]{:S(2)}, u32[]{:S(2)}) collective-permute-start(bf16[384,64]{0,1:T(8,128)(2,1)} %param.8), channel_id=1, source_target_pairs={{0,256},{256,512},{512,768},{768,0},{1,257},{257,513},{513,769},{7... | collective-permute-start | bytes 147464 | tf_op jit(solution)/shard_map/ppermute | solution.py:125
  19.3 10.7 %collective-permute-start.1 = (bf16[384,64]{0,1:T(8,128)(2,1)S(1)}, bf16[384,64]{0,1:T(8,128)(2,1)S(1)}, u32[]{:S(2)}, u32[]{:S(2)}) collective-permute-start(bf16[384,64]{0,1:T(8,128)(2,1)S(1)} %collective-permute-done), channel_id=1, source_target_pairs={{0,256},{256,512},{512,768},{768,0},{1,257},{257,513},{513,769},{7... | collective-permute-start | bytes 147464 | tf_op jit(solution)/shard_map/ppermute | solution.py:125
  21.2 9.7 %collective-permute-start.2 = (bf16[384,64]{0,1:T(8,128)(2,1)}, bf16[384,64]{0,1:T(8,128)(2,1)S(1)}, u32[]{:S(2)}, u32[]{:S(2)}) collective-permute-start(bf16[384,64]{0,1:T(8,128)(2,1)} %param.8), channel_id=1, source_target_pairs={{0,768},{256,0},{512,256},{768,512},{1,769},{257,1},{513,257},{769... | collective-permute-start | bytes 147464 | tf_op jit(solution)/shard_map/ppermute | solution.py:128
  29.9 13.6 %copy-start.3 = (bf16[1,256,384]{1,2,0:T(8,128)(2,1)}, bf16[1,256,384]{1,2,0:T(8,128)(2,1)S(1)}, u32[]{:S(2)}) copy-start(bf16[1,256,384]{1,2,0:T(8,128)(2,1)S(1)} %copy.75) | copy-start | bytes 589828
  29.9 26.1 %copy-start.8 = (bf16[16,1,4096]{2,0,1:T(8,128)(2,1)S(1)}, bf16[16,1,4096]{2,0,1:T(8,128)(2,1)}, u32[]{:S(2)}) copy-start(bf16[16,1,4096]{2,0,1:T(8,128)(2,1)} %param.9) | copy-start | bytes 393220
  31.8 9.1 %collective-permute-start.3 = (bf16[384,256]{0,1:T(8,128)(2,1)S(1)}, bf16[384,256]{0,1:T(8,128)(2,1)S(1)}, u32[]{:S(2)}, u32[]{:S(2)}) collective-permute-start(bf16[384,256]{0,1:T(8,128)(2,1)S(1)} %bitcast.143), channel_id=1, source_target_pairs={{0,32},{32,64},{64,96},{96,128},{128,160},{160,192},{192,224},{224... | collective-permute-start | bytes 589832 | tf_op jit(solution)/shard_map/ppermute | solution.py:125
  36.4 7.1 %collective-permute-start.7 = (bf16[384,256]{0,1:T(8,128)(2,1)S(1)}, bf16[384,256]{0,1:T(8,128)(2,1)S(1)}, u32[]{:S(2)}, u32[]{:S(2)}) collective-permute-start(bf16[384,256]{0,1:T(8,128)(2,1)S(1)} %bitcast.144), channel_id=1, source_target_pairs={{0,224},{32,0},{64,32},{96,64},{128,96},{160,128},{192,160},{224,1... | collective-permute-start | bytes 589832 | tf_op jit(solution)/shard_map/ppermute | solution.py:128
  40.9 7.6 %collective-permute-start.4 = (bf16[384,256]{0,1:T(8,128)(2,1)S(1)}, bf16[384,256]{0,1:T(8,128)(2,1)S(1)}, u32[]{:S(2)}, u32[]{:S(2)}) collective-permute-start(bf16[384,256]{0,1:T(8,128)(2,1)S(1)} %collective-permute-done.3), channel_id=1, source_target_pairs={{0,32},{32,64},{64,96},{96,128},{128,160},{160,192},{192,224},{224... | collective-permute-start | bytes 589832 | tf_op jit(solution)/shard_map/ppermute | solution.py:125
  43.5 27.4 %copy-start.7 = (bf16[3,256,128]{1,2,0:T(8,128)(2,1)}, bf16[3,256,128]{1,2,0:T(8,128)(2,1)S(1)}, u32[]{:S(2)}) copy-start(bf16[3,256,128]{1,2,0:T(8,128)(2,1)S(1)} %convolution_convert_fusion.1) | copy-start | bytes 589828
  43.5 20.9 %collective-permute-start.8 = (bf16[384,256]{0,1:T(8,128)(2,1)S(1)}, bf16[384,256]{0,1:T(8,128)(2,1)S(1)}, u32[]{:S(2)}, u32[]{:S(2)}) collective-permute-start(bf16[384,256]{0,1:T(8,128)(2,1)S(1)} %collective-permute-done.7), channel_id=1, source_target_pairs={{0,224},{32,0},{64,32},{96,64},{128,96},{160,128},{192,160},{224,1... | collective-permute-start | bytes 589832 | tf_op jit(solution)/shard_map/ppermute | solution.py:128
  48.5 20.4 %collective-permute-start.5 = (bf16[384,256]{0,1:T(8,128)(2,1)S(1)}, bf16[384,256]{0,1:T(8,128)(2,1)S(1)}, u32[]{:S(2)}, u32[]{:S(2)}) collective-permute-start(bf16[384,256]{0,1:T(8,128)(2,1)S(1)} %collective-permute-done.4), channel_id=1, source_target_pairs={{0,32},{32,64},{64,96},{96,128},{128,160},{160,192},{192,224},{224... | collective-permute-start | bytes 589832 | tf_op jit(solution)/shard_map/ppermute | solution.py:125
  50.5 20.5 %collective-permute-start.10 = (bf16[256,384]{0,1:T(8,128)(2,1)S(1)}, bf16[256,384]{0,1:T(8,128)(2,1)}, u32[]{:S(2)}, u32[]{:S(2)}) collective-permute-start(bf16[256,384]{0,1:T(8,128)(2,1)S(1)} %bitcast.170), channel_id=1, source_target_pairs={{0,1},{1,0},{2,3},{3,2},{4,5},{5,4},{6,7},{7,6},{8,9},{9,8},{10,11... | collective-permute-start | bytes 589832 | tf_op jit(solution)/shard_map/ppermute | solution.py:80
  57.7 30.5 %all-to-all-start.1 = ((bf16[16,16,2048]{2,1,0:T(8,128)(2,1)}), bf16[16,16,2048]{2,1,0:T(8,128)(2,1)S(1)}, u32[]{:S(2)}, u32[]{:S(2)}) async-start(bf16[16,16,2048]{2,1,0:T(8,128)(2,1)} %bitcast.41), calls=%async_computation.1 | async-start | bytes 2097152 | tf_op jit(solution)/shard_map/all_to_all | solution.py:98
  64.4 9.5 %collective-permute-start.9 = (bf16[384,256]{0,1:T(8,128)(2,1)S(1)}, bf16[384,256]{0,1:T(8,128)(2,1)S(1)}, u32[]{:S(2)}, u32[]{:S(2)}) collective-permute-start(bf16[384,256]{0,1:T(8,128)(2,1)S(1)} %collective-permute-done.8), channel_id=1, source_target_pairs={{0,224},{32,0},{64,32},{96,64},{128,96},{160,128},{192,160},{224,1... | collective-permute-start | bytes 589832 | tf_op jit(solution)/shard_map/ppermute | solution.py:128
  69.0 7.9 %collective-permute-start.6 = (bf16[384,256]{0,1:T(8,128)(2,1)S(1)}, bf16[384,256]{0,1:T(8,128)(2,1)S(1)}, u32[]{:S(2)}, u32[]{:S(2)}) collective-permute-start(bf16[384,256]{0,1:T(8,128)(2,1)S(1)} %collective-permute-done.5), channel_id=1, source_target_pairs={{0,32},{32,64},{64,96},{96,128},{128,160},{160,192},{192,224},{224... | collective-permute-start | bytes 589832 | tf_op jit(solution)/shard_map/ppermute | solution.py:125
  77.2 0.9 copy-start.5
  77.2 1.0 copy-start.6
  77.7 1.8 %copy-start = (bf16[8,384,256]{1,2,0:T(8,128)(2,1)}, bf16[8,384,256]{1,2,0:T(8,128)(2,1)S(1)}, u32[]{:S(2)}) copy-start(bf16[8,384,256]{1,2,0:T(8,128)(2,1)S(1)} %constant_dynamic-slice_fusion) | copy-start | bytes 4718596
  80.6 14.8 %collective-permute-start.11 = (bf16[8,2,16,2048]{3,2,0,1:T(8,128)(2,1)}, bf16[8,2,16,2048]{3,2,0,1:T(8,128)(2,1)}, u32[]{:S(2)}, u32[]{:S(2)}) collective-permute-start(bf16[8,2,16,2048]{3,2,0,1:T(8,128)(2,1)} %dynamic-slice_bitcast_fusion), channel_id=1, source_target_pairs={{0,2},{2,0},{1,3},{3,1},{4,6},{6,4},{5,7},{7,5},{8,10},{10,8},{9,1... | collective-permute-start | bytes 3145736 | tf_op jit(solution)/shard_map/ppermute | solution.py:70
  88.2 13.5 %collective-permute-start.12 = (bf16[8,2,16,2048]{3,2,1,0:T(8,128)(2,1)S(1)}, bf16[8,2,16,2048]{3,2,1,0:T(8,128)(2,1)}, u32[]{:S(2)}, u32[]{:S(2)}) collective-permute-start(bf16[8,2,16,2048]{3,2,1,0:T(8,128)(2,1)S(1)} %bitcast.139), channel_id=1, source_target_pairs={{0,2},{2,0},{1,3},{3,1},{4,6},{6,4},{5,7},{7,5},{8,10},{10,8},{9,1... | collective-permute-start | bytes 3145736 | tf_op jit(solution)/shard_map/ppermute | solution.py:70
  98.1 35.1 %all-to-all-start = ((bf16[16,16,2048]{2,1,0:T(8,128)(2,1)}), bf16[16,16,2048]{2,1,0:T(8,128)(2,1)S(1)}, u32[]{:S(2)}, u32[]{:S(2)}) async-start(bf16[16,16,2048]{2,1,0:T(8,128)(2,1)} %bitcast.35), calls=%async_computation | async-start | bytes 2097152 | tf_op jit(solution)/shard_map/all_to_all | solution.py:113
  103.3 1.4 %copy-start.1 = (bf16[8,384,256]{1,2,0:T(8,128)(2,1)S(1)}, bf16[8,384,256]{1,2,0:T(8,128)(2,1)}, u32[]{:S(2)}) copy-start(bf16[8,384,256]{1,2,0:T(8,128)(2,1)} %copy-done) | copy-start | bytes 4718596
  105.7 24.6 %copy-start.2 = (f32[3,256,256]{1,2,0:T(8,128)S(1)}, f32[3,256,256]{1,2,0:T(8,128)}, u32[]{:S(2)}) copy-start(f32[3,256,256]{1,2,0:T(8,128)} %get-tuple-element.21) | copy-start | bytes 2359300
  105.7 24.6 %copy-start.4 = (bf16[1,256,384]{1,2,0:T(8,128)(2,1)S(1)}, bf16[1,256,384]{1,2,0:T(8,128)(2,1)}, u32[]{:S(2)}) copy-start(bf16[1,256,384]{1,2,0:T(8,128)(2,1)} %copy-done.3) | copy-start | bytes 589828
  106.5 21.2 %collective-permute-start.13 = (f32[256,384]{0,1:T(8,128)}, f32[256,384]{0,1:T(8,128)}, u32[]{:S(2)}, u32[]{:S(2)}) collective-permute-start(f32[256,384]{0,1:T(8,128)} %dynamic-slice_bitcast_fusion.1), channel_id=1, source_target_pairs={{0,1},{1,0},{2,3},{3,2},{4,5},{5,4},{6,7},{7,6},{8,9},{9,8},{10,11... | collective-permute-start | bytes 1179656 | tf_op jit(solution)/shard_map/ppermute | solution.py:80
